TPU v7x, 256 devices: a whole 4x4x8 slice. The times are simulated.
256 devices in a mesh: expert: 32 (over x, z), tensor: 8 (over y, core).
Axes of the slice: x: 4, y: 4, z: 8, core: 2. Of those that a mesh axis runs over, the one named last changes fastest.
Arguments:
- attn_vals: bfloat16 [2048, 4096], P('expert', 'tensor'), may hold values from -6 to 6
- residual: bfloat16 [2048, 4096], P('expert', 'tensor'), may hold values from -6 to 6
- out_weight: bfloat16 [4096, 4096], P('tensor'), may hold values from -0.09375 to 0.09375
- norm_gain: float32 [4096], P('tensor'), may hold values from 0.5 to 1.5
- router_weight: float32 [4096, 8], P('tensor'), may hold values from -0.09375 to 0.09375
- routes: int32 [2048, 2], P('expert'), may hold values from 0 to 7, all different within a row; in each aligned block of 64 rows (0 to 63, 64 to 127, ...) at most 32 rows name the same one
- w_gate: bfloat16 [32, 4096, 2048], P('expert', None, 'tensor'), may hold values from -0.09375 to 0.09375
- w_up: bfloat16 [32, 4096, 2048], P('expert', None, 'tensor'), may hold values from -0.09375 to 0.09375
- w_down: bfloat16 [32, 2048, 4096], P('expert', 'tensor'), may hold values from -0.0625 to 0.0625
- slab_of: int32 [32], replicated, may hold values from 0 to 31, each once
- final_gain: float32 [4096], P('tensor'), may hold values from 0.5 to 1.5
- row_order: int32 [2048], replicated, may hold values from 0 to 2047, each once
Outputs:
- stream_out: bfloat16 [2048, 4096], P('expert', 'tensor')
- normed_out: bfloat16 [2048, 4096], P('expert', 'tensor')
Inputs may be any that keep to these rules, and one draw needn't show every extreme that they name: `routes`: the two experts of a row differ. In each aligned block of 64 rows (the rows of one device) no expert is named by more than 32 rows, and some block names one expert exactly 32 times. `slab_of`: A permutation. `row_order`: A permutation.
All inputs are finite; a program needn't handle non-finite values.
Results may differ from a plain program's by a relative error of at most 0.017.
Values may be sent and summed in bfloat16 or wider, within the bound.
No kernel may reach another device: no remote copies, remote signals or barrier semaphores. Data moves between devices by JAX's collectives and lax.ppermute only.
A program may use at most 128 MiB of HBM per device.

v0:
```python
import jax
import jax.numpy as jnp
from jax import lax
from jax.sharding import PartitionSpec as P

D = 4096
MOST = 32


EPS = 1e-05


def finish_slots(gate_val, up_val, down_weight):
    active = (jax.nn.silu(gate_val) * up_val).astype(jnp.bfloat16)
    partial_out = jnp.einsum("gmf,fd->gmd", active, down_weight, preferred_element_type=jnp.float32)
    summed = lax.psum_scatter(
        partial_out.astype(jnp.bfloat16), "tensor", scatter_dimension=2, tiled=True
    )
    return lax.all_to_all(summed, "expert", split_axis=0, concat_axis=0, tiled=True)


def final_norm(stream, final_gain):
    stream_f = stream.astype(jnp.float32)
    square_total = lax.psum(jnp.sum(stream_f * stream_f, axis=1), "tensor")
    factor = lax.rsqrt(square_total / D + EPS)
    return (stream_f * factor[:, None] * final_gain).astype(jnp.bfloat16)


def on_device(
    attn_vals,
    residual,
    out_weight,
    norm_gain,
    router_weight,
    routes,
    w_gate,
    w_up,
    w_down,
    slab_of,
    final_gain,
    row_order,
):
    groups = lax.axis_size("expert")
    row_count = attn_vals.shape[0]
    expert_count = router_weight.shape[1]
    slab_count = groups // expert_count
    partial_proj = jnp.dot(attn_vals, out_weight, preferred_element_type=jnp.float32)
    project = lax.psum_scatter(
        partial_proj.astype(jnp.bfloat16), "tensor", scatter_dimension=1, tiled=True
    ).astype(jnp.float32)
    stream_in = (residual.astype(jnp.float32) + project).astype(jnp.bfloat16)
    hidden_f = stream_in.astype(jnp.float32)
    scaled = hidden_f * norm_gain
    square_sum, logit_part = lax.psum(
        (
            jnp.sum(hidden_f * hidden_f, axis=1),
            jnp.dot(scaled, router_weight, precision=lax.Precision.HIGHEST),
        ),
        "tensor",
    )
    inverse_rms = lax.rsqrt(square_sum / D + EPS)
    normed_in = (scaled * inverse_rms[:, None]).astype(jnp.bfloat16)
    logits = logit_part * inverse_rms[:, None]
    expert_ids = jnp.arange(expert_count, dtype=jnp.int32)
    route_hot = (routes[:, :, None] == expert_ids[None, None, :]).astype(jnp.int32)
    chosen = jnp.sum(route_hot.astype(jnp.float32) * logits[:, None, :], axis=2)
    leading = jax.nn.sigmoid(chosen[:, 0] - chosen[:, 1])
    mixing = jnp.stack([leading, 1.0 - leading], axis=1)
    route_hits = jnp.sum(route_hot, axis=1)
    before_count = jnp.cumsum(route_hits, axis=0) - route_hits
    slot_ids = jnp.sum(route_hot * before_count[:, None, :], axis=2)
    slot_hot = (slot_ids[:, :, None] == jnp.arange(MOST, dtype=jnp.int32)[None, None, :]).astype(
        jnp.float32
    )
    placing = jnp.einsum("rke,rks->esr", route_hot.astype(jnp.float32), slot_hot).astype(
        jnp.bfloat16
    )
    target_expert = slab_of // slab_count
    send_map = jnp.take(placing, target_expert, axis=0)
    full_rows = lax.all_gather(normed_in, "tensor", axis=1, tiled=True)
    outgoing = jnp.einsum(
        "gsr,rd->gsd", send_map, full_rows, preferred_element_type=jnp.float32
    ).astype(jnp.bfloat16)
    arrived = lax.all_to_all(outgoing, "expert", split_axis=0, concat_axis=0, tiled=True)
    gate_val = jnp.einsum("gmd,df->gmf", arrived, w_gate[0], preferred_element_type=jnp.float32)
    up_val = jnp.einsum("gmd,df->gmf", arrived, w_up[0], preferred_element_type=jnp.float32)
    returned = finish_slots(gate_val, up_val, w_down[0])
    group_ids = jnp.arange(groups, dtype=jnp.int32)
    holder_hot = (slab_of[None, :] == group_ids[:, None]).astype(jnp.int32)
    holders = jnp.sum(holder_hot * group_ids[None, :], axis=1).reshape(expert_count, slab_count)
    row_holders = jnp.take(holders, routes, axis=0)
    flat_index = row_holders * MOST + slot_ids[:, :, None]
    flat_back = returned.reshape(groups * MOST, returned.shape[2])
    fetched = jnp.take(flat_back, flat_index.reshape(-1), axis=0).reshape(
        row_count, 2, slab_count, returned.shape[2]
    )
    expert_out = jnp.sum(fetched.astype(jnp.float32), axis=2)
    blended = jnp.sum(mixing[:, :, None] * expert_out, axis=1)
    stream = (hidden_f + blended).astype(jnp.bfloat16)
    positions = lax.axis_index("expert") * row_count + jnp.arange(row_count, dtype=jnp.int32)
    matches = (row_order[None, :] == positions[:, None]).astype(jnp.int32)
    source = jnp.sum(matches * jnp.arange(row_order.shape[0], dtype=jnp.int32)[None, :], axis=1)
    normed = final_norm(stream, final_gain)
    all_stream, all_normed = (
        lax.all_gather(stream, "expert", axis=0, tiled=True),
        lax.all_gather(normed, "expert", axis=0, tiled=True),
    )
    return (jnp.take(all_stream, source, axis=0), jnp.take(all_normed, source, axis=0))


def solution(mesh):
    return jax.shard_map(
        on_device,
        mesh=mesh,
        in_specs=(
            P("expert", "tensor"),
            P("expert", "tensor"),
            P("tensor", None),
            P("tensor"),
            P("tensor", None),
            P("expert", None),
            P("expert", None, "tensor"),
            P("expert", None, "tensor"),
            P("expert", "tensor", None),
            P(),
            P("tensor"),
            P(),
        ),
        out_specs=(P("expert", "tensor"), P("expert", "tensor")),
        check_vma=False,
    )
```

profile of v0, /device:TPU:1, one launch (start us, length us, event | category | flops | bytes accessed | tf_op | source)
XLA Modules:
  0.0 560.4 jit_solution(10908743373798955551)
XLA Ops:
  7.3 4.0 convolution_convert_fusion.2
  11.3 0.1 copy.71
  11.4 0.2 convert_reduce_fusion.1
  11.6 0.1 reduce_window_sum.11
  11.7 1.2 select_reduce_fusion.1
  13.0 0.4 fusion.13
  13.4 0.1 copy.80
  13.6 0.6 gather_fusion.1
  14.2 32.7 %reduce-scatter.3.cloned.1.call-done = bf16[64,512]{1,0:T(8,128)(2,1)} async-done(((bf16[64,4096]{1,0:T(8,128)(2,1)}), bf16[64,512]{1,0:T(8,128)(2,1)}) %reduce-scatter.3.cloned.1.call-update) | async-done | bytes 65552 | tf_op jit(solution)/shard_map/reduce_scatter | solution.py:48
  46.9 1.0 fusion.29
  47.9 0.2 fusion.24
  48.1 14.9 %all-reduce = (f32[64]{0:T(128)S(1)}, f32[64,8]{0,1:T(8,128)S(1)}) all-reduce(f32[64]{0:T(128)S(1)} %get-tuple-element.13, f32[64,8]{0,1:T(8,128)S(1)} %fusion.24), channel_id=1, replica_groups=mesh['expert'=32,'tensor'=8] {'tensor'}, use_global_device_ids=true, to_apply=%region_3.0 | all-reduce | flops 576 | bytes 4608 | tf_op jit(solution)/shard_map/psum | solution.py:54
  63.0 0.1 fusion.25
  63.1 14.3 %all_gather.9 = bf16[64,4096]{1,0:T(8,128)(2,1)S(1)} all-gather(bf16[64,512]{1,0:T(8,128)(2,1)S(1)} %fusion.25), channel_id=1, replica_groups=mesh['expert'=32,'tensor'=8] {'tensor'}, dimensions={1}, use_global_device_ids=true | all-gather | bytes 589824 | tf_op jit(solution)/shard_map/all_gather | solution.py:80
  77.5 2.4 convolution_convert_fusion.1
  79.9 191.7 %all_to_all.10 = bf16[32,32,4096]{2,1,0:T(8,128)(2,1)S(1)} all-to-all(bf16[32,32,4096]{2,1,0:T(8,128)(2,1)S(1)} %convolution_convert_fusion.1), channel_id=1, replica_groups=mesh['expert'=32,'tensor'=8] {'expert'}, dimensions={0} | all-to-all | bytes 16777216 | tf_op jit(solution)/shard_map/all_to_all | solution.py:84
  271.5 3.2 copy-done.1
  274.7 2.3 fusion.3
  277.1 16.8 %convolution_convert_fusion = bf16[32,32,4096]{2,1,0:T(8,128)(2,1)} fusion(bf16[1,256,4096]{2,1,0:T(8,128)(2,1)S(1)} %copy-done, bf16[32,32,4096]{2,1,0:T(8,128)(2,1)} %copy-done.1, bf16[1,4096,256]{2,1,0:T(8,128)(2,1)} %param.21, f32[32,32,256]{2,1,0:T(8,128)S(1)} %fusion.3), kind=kOutput, calls=%fused_computation.5 | convolution fusion | flops 4300734464 | bytes 22020096 | tf_op jit(solution)/shard_map/gmf,fd->gmd/dot_general | solution.py:15
  293.9 53.3 %reduce-scatter.5.cloned.1.call-done = bf16[32,32,512]{2,1,0:T(8,128)(2,1)} async-done(((bf16[32,32,4096]{2,1,0:T(8,128)(2,1)}), bf16[32,32,512]{2,1,0:T(8,128)(2,1)}) %reduce-scatter.5.cloned.1.call-update) | async-done | bytes 1048592 | tf_op jit(solution)/shard_map/reduce_scatter | solution.py:16
  347.2 9.6 %all-to-all-start.1 = ((bf16[32,32,512]{2,1,0:T(8,128)(2,1)}), bf16[32,32,512]{2,1,0:T(8,128)(2,1)S(1)}, u32[]{:S(2)}, u32[]{:S(2)}) async-start(bf16[32,32,512]{2,1,0:T(8,128)(2,1)} %reduce-scatter.5.cloned.1.call-done), calls=%async_computation.3 | async-start | bytes 2097152 | tf_op jit(solution)/shard_map/all_to_all | solution.py:19
  356.9 0.1 copy.76
  357.0 0.1 reshape.132
  357.2 0.1 select_reduce_fusion.2
  357.3 0.1 reshape.112
  357.4 0.6 gather_fusion
  358.0 0.1 copy.77
  358.2 0.1 copy.81
  358.3 0.1 add.120
  358.4 0.1 copy.79
  358.6 0.1 copy.72
  358.7 0.2 fusion.34
  359.2 0.1 copy.75
  359.3 22.7 %all-to-all-done.1 = bf16[32,32,512]{2,1,0:T(8,128)(2,1)S(1)} async-done(((bf16[32,32,512]{2,1,0:T(8,128)(2,1)}), bf16[32,32,512]{2,1,0:T(8,128)(2,1)S(1)}, u32[]{:S(2)}, u32[]{:S(2)}) %all-to-all-start.1) | async-done | bytes 1048608 | tf_op jit(solution)/shard_map/all_to_all | solution.py:19
  382.0 2.6 gather_fusion.2
  384.6 1.2 gather.20
  385.8 0.9 convert_reduce_fusion
  386.7 0.4 multiply_reduce_fusion
  387.1 0.1 fusion.26
  387.2 16.3 %psum.23 = f32[64]{0:T(128)S(1)} all-reduce(f32[64]{0:T(128)S(1)} %get-tuple-element.5), channel_id=1, replica_groups=mesh['expert'=32,'tensor'=8] {'tensor'}, use_global_device_ids=true, to_apply=%region_14.16 | all-reduce | flops 64 | bytes 512 | tf_op jit(solution)/shard_map/psum | solution.py:24
  403.5 0.7 fusion.28
  404.3 0.5 all-gather.3.cloned.1.call-update
  404.9 0.2 select_reduce_fusion
  405.1 67.3 %all-gather.5.cloned.1.call-done = bf16[2048,512]{1,0:T(8,128)(2,1)} async-done(((bf16[64,512]{1,0:T(8,128)(2,1)}), bf16[2048,512]{1,0:T(8,128)(2,1)}) %all-gather.5.cloned.1.call-update) | async-done | bytes 2097168 | tf_op jit(solution)/shard_map/all_gather | solution.py:106
  472.4 2.6 gather_fusion.4
  475.0 75.6 %all-gather.3.cloned.1.call-done = bf16[2048,512]{1,0:T(8,128)(2,1)} async-done(((bf16[64,512]{1,0:T(8,128)(2,1)}), bf16[2048,512]{1,0:T(8,128)(2,1)}) %all-gather.3.cloned.1.call-update) | async-done | bytes 2097168 | tf_op jit(solution)/shard_map/all_gather | solution.py:105
  550.6 2.6 gather_fusion.3
  553.2 0.7 broadcast_select_fusion
  (50 shorter events, 0.7 us)
Async XLA Ops:
  7.2 269.9 %copy-start = (bf16[1,256,4096]{2,1,0:T(8,128)(2,1)S(1)}, bf16[1,256,4096]{2,1,0:T(8,128)(2,1)}, u32[]{:S(2)}) copy-start(bf16[1,256,4096]{2,1,0:T(8,128)(2,1)} %param.22) | copy-start | bytes 6291460
  7.2 4.2 copy-start.7
  7.2 6.4 %copy-start.10 = (s32[32]{0:T(128)S(1)}, s32[32]{0:T(128)}, u32[]{:S(2)}) copy-start(s32[32]{0:T(128)} %param.23) | copy-start | bytes 388
  7.2 39.7 %copy-start.3 = (bf16[64,512]{1,0:T(8,128)(2,1)S(1)}, bf16[64,512]{1,0:T(8,128)(2,1)}, u32[]{:S(2)}) copy-start(bf16[64,512]{1,0:T(8,128)(2,1)} %param.15) | copy-start | bytes 196612
  7.2 40.7 %copy-start.5 = (f32[512]{0:T(512)S(1)}, f32[512]{0:T(512)}, u32[]{:S(2)}) copy-start(f32[512]{0:T(512)} %param.17) | copy-start | bytes 6148
  7.2 40.7 %copy-start.4 = (f32[512,8]{0,1:T(8,128)S(1)}, f32[512,8]{0,1:T(8,128)}, u32[]{:S(2)}) copy-start(f32[512,8]{0,1:T(8,128)} %param.18) | copy-start | bytes 49156
  7.2 39.7 %reduce-scatter.3.cloned.1.call-start = ((), (), s32[]{:S(2)}) async-start(), calls=%async_computation.4 | async-start | bytes 589824 | tf_op jit(solution)/shard_map/reduce_scatter | solution.py:48
  11.3 335.9 %reduce-scatter.5.cloned.1.call-start = ((), (), s32[]{:S(2)}) async-start(), calls=%async_computation.5 | async-start | bytes 9437184 | tf_op jit(solution)/shard_map/reduce_scatter | solution.py:16
  79.8 194.9 %copy-start.9 = (bf16[1,4096,256]{2,1,0:T(8,128)(2,1)S(1)}, bf16[1,4096,256]{2,1,0:T(8,128)(2,1)}, u32[]{:S(2)}) copy-start(bf16[1,4096,256]{2,1,0:T(8,128)(2,1)} %param.20) | copy-start | bytes 6291460
  271.5 3.2 copy-start.1
  347.2 34.7 %all-to-all-start.1 = ((bf16[32,32,512]{2,1,0:T(8,128)(2,1)}), bf16[32,32,512]{2,1,0:T(8,128)(2,1)S(1)}, u32[]{:S(2)}, u32[]{:S(2)}) async-start(bf16[32,32,512]{2,1,0:T(8,128)(2,1)} %reduce-scatter.5.cloned.1.call-done), calls=%async_computation.3 | async-start | bytes 2097152 | tf_op jit(solution)/shard_map/all_to_all | solution.py:19
  356.8 115.6 %all-gather.5.cloned.1.call-start = ((), (), s32[]{:S(2)}) async-start(), calls=%async_computation.7 | async-start | bytes 2162688 | tf_op jit(solution)/shard_map/all_gather | solution.py:106
  357.4 46.2 %copy-start.8 = (f32[512]{0:T(512)S(1)}, f32[512]{0:T(512)}, u32[]{:S(2)}) copy-start(f32[512]{0:T(512)} %param.24) | copy-start | bytes 6148
  358.0 46.8 %copy-start.6 = (s32[2048]{0:T(1024)S(1)}, s32[2048]{0:T(1024)}, u32[]{:S(2)}) copy-start(s32[2048]{0:T(1024)} %param.25) | copy-start | bytes 24580
  387.2 17.1 %copy-start.2 = (bf16[64,512]{1,0:T(8,128)(2,1)}, bf16[64,512]{1,0:T(8,128)(2,1)S(1)}, u32[]{:S(2)}) copy-start(bf16[64,512]{1,0:T(8,128)(2,1)S(1)} %get-tuple-element.6) | copy-start | bytes 196612
  404.3 146.3 %all-gather.3.cloned.1.call-start = ((), (), s32[]{:S(2)}) async-start(), calls=%async_computation.6 | async-start | bytes 2162688 | tf_op jit(solution)/shard_map/all_gather | solution.py:105
Sparse Core Ops, SparseCore 0:
  11.4 35.4 reduce-scatter.2
  294.1 53.1 reduce-scatter.4
  404.4 67.9 all-gather.4
  475.4 75.1 all-gather.2
where the time goes:
time: 565 us; the launch traced here: 560 us
  waiting for transfers between devices  252 us (45%)
  blocking collectives  237 us (42%)
  matrix products  26.1 us (5%)
  local copies, waits for them, and re-layouts  14.9 us (3%)
  between operations  14.1 us (2%)
  starting transfers between devices  9.72 us (2%)
  other arithmetic  6.14 us (1%)
    all_to_all x1, blocking collectives, on_device(): lax.all_to_all(outgoing, 'expert', split_axis=0, concat_axis=0, tiled=True)  192 us
    all_gather x1, waiting for transfers between devices, on_device(): lax.all_gather(stream, 'expert', axis=0, tiled=True)  75.6 us
    all_gather x1, waiting for transfers between devices, on_device(): lax.all_gather(normed, 'expert', axis=0, tiled=True)  67.3 us
    reduce_scatter x1, waiting for transfers between devices, finish_slots(): lax.psum_scatter(partial_out.astype(jnp.bfloat16), 'tensor', scatter_dime...  53.3 us
    reduce_scatter x1, waiting for transfers between devices, on_device(): lax.psum_scatter(partial_proj.astype(jnp.bfloat16), 'tensor', scatter_dim...  32.7 us
    all_to_all x1, waiting for transfers between devices, finish_slots(): lax.all_to_all(summed, 'expert', split_axis=0, concat_axis=0, tiled=True)  22.7 us
    dot_general x1, matrix products, finish_slots(): jnp.einsum('gmf,fd->gmd', active, down_weight, preferred_element_type=jnp...  16.8 us
    psum x1, blocking collectives, final_norm(): square_total = lax.psum(jnp.sum(stream_f * stream_f, axis=1), 'tensor')  16.3 us
  transfers between devices with their start and end apart: 5, of which 5 were waited for; matrix products, arithmetic and copies ran while one was open for 1% of the time, Pallas kernels for 0%

commit v1 on v0

--- a/solution.py
+++ b/solution.py
@@ -77,11 +77,11 @@
     )
     target_expert = slab_of // slab_count
     send_map = jnp.take(placing, target_expert, axis=0)
-    full_rows = lax.all_gather(normed_in, "tensor", axis=1, tiled=True)
     outgoing = jnp.einsum(
-        "gsr,rd->gsd", send_map, full_rows, preferred_element_type=jnp.float32
+        "gsr,rd->gsd", send_map, normed_in, preferred_element_type=jnp.float32
     ).astype(jnp.bfloat16)
-    arrived = lax.all_to_all(outgoing, "expert", split_axis=0, concat_axis=0, tiled=True)
+    arrived_part = lax.all_to_all(outgoing, "expert", split_axis=0, concat_axis=0, tiled=True)
+    arrived = lax.all_gather(arrived_part, "tensor", axis=2, tiled=True)
     gate_val = jnp.einsum("gmd,df->gmf", arrived, w_gate[0], preferred_element_type=jnp.float32)
     up_val = jnp.einsum("gmd,df->gmf", arrived, w_up[0], preferred_element_type=jnp.float32)
     returned = finish_slots(gate_val, up_val, w_down[0])
@@ -100,12 +100,9 @@
     positions = lax.axis_index("expert") * row_count + jnp.arange(row_count, dtype=jnp.int32)
     matches = (row_order[None, :] == positions[:, None]).astype(jnp.int32)
     source = jnp.sum(matches * jnp.arange(row_order.shape[0], dtype=jnp.int32)[None, :], axis=1)
-    normed = final_norm(stream, final_gain)
-    all_stream, all_normed = (
-        lax.all_gather(stream, "expert", axis=0, tiled=True),
-        lax.all_gather(normed, "expert", axis=0, tiled=True),
-    )
-    return (jnp.take(all_stream, source, axis=0), jnp.take(all_normed, source, axis=0))
+    all_stream = lax.all_gather(stream, "expert", axis=0, tiled=True)
+    ordered = jnp.take(all_stream, source, axis=0)
+    return (ordered, final_norm(ordered, final_gain))
 
 
 def solution(mesh):

time: 565 us -> 367 us (0.65)
  blocking collectives: 237 us -> 66.5 us
  waiting for transfers between devices: 252 us -> 233 us
  local copies, waits for them, and re-layouts: 14.9 us -> 9.17 us
    all_to_all x1, blocking collectives: 192 us -> 34.6 us  [on_device(): lax.all_to_all(outgoing, 'expert', split_axis=0, concat_axis=0, tiled=True)]
    all_gather x2, waiting for transfers between devices: 143 us -> 123 us  [the longest x1 72.8 us: on_device(): all_stream = lax.all_gather(stream, 'expert', axis=0, tiled=True)]
    all_gather x1 -> x0, blocking collectives: 14.3 us -> none  [on_device(): full_rows = lax.all_gather(normed_in, 'tensor', axis=1, tiled=True)]
where the time goes in v1:
time: 367 us
  waiting for transfers between devices  233 us (63%)
  blocking collectives  66.5 us (18%)
  matrix products  28.2 us (8%)
  between operations  14.1 us (4%)
  starting transfers between devices  9.88 us (3%)
  local copies, waits for them, and re-layouts  9.17 us (2%)
  other arithmetic  6.03 us (2%)
    all_gather x1, waiting for transfers between devices, on_device(): all_stream = lax.all_gather(stream, 'expert', axis=0, tiled=True)  72.8 us
    reduce_scatter x1, waiting for transfers between devices, finish_slots(): lax.psum_scatter(partial_out.astype(jnp.bfloat16), 'tensor', scatter_dime...  54.4 us
    all_gather x1, waiting for transfers between devices, on_device(): arrived = lax.all_gather(arrived_part, 'tensor', axis=2, tiled=True)  50.6 us
    all_to_all x1, blocking collectives, on_device(): lax.all_to_all(outgoing, 'expert', split_axis=0, concat_axis=0, tiled=True)  34.6 us
    reduce_scatter x1, waiting for transfers between devices, on_device(): lax.psum_scatter(partial_proj.astype(jnp.bfloat16), 'tensor', scatter_dim...  32.7 us
    all_to_all x1, waiting for transfers between devices, finish_slots(): lax.all_to_all(summed, 'expert', split_axis=0, concat_axis=0, tiled=True)  22.5 us
    psum x1, blocking collectives, final_norm(): square_total = lax.psum(jnp.sum(stream_f * stream_f, axis=1), 'tensor')  17.1 us
    dot_general x1, matrix products, finish_slots(): jnp.einsum('gmf,fd->gmd', active, down_weight, preferred_element_type=jnp...  16.8 us
  transfers between devices with their start and end apart: 5, of which 5 were waited for; matrix products, arithmetic and copies ran while one was open for 1% of the time, Pallas kernels for 0%

profile of v1, /device:TPU:1, one launch (start us, length us, event | category | flops | bytes accessed | tf_op | source)
XLA Modules:
  0.0 367.0 jit_solution(5263027604369193061)
XLA Ops:
  7.2 4.0 %convolution_convert_fusion.1 = bf16[64,4096]{1,0:T(8,128)(2,1)} fusion(bf16[64,512]{1,0:T(8,128)(2,1)} %param.12, bf16[512,4096]{1,0:T(8,128)(2,1)} %param.14), kind=kOutput, calls=%fused_computation.5 | convolution fusion | flops 268697600 | bytes 4784128 | tf_op jit(solution)/shard_map/dot_general | solution.py:47
  11.3 0.1 copy.71
  11.4 0.2 convert_reduce_fusion.1
  11.6 0.1 reduce_window_sum.11
  11.7 1.2 select_reduce_fusion.1
  12.9 0.4 fusion.13
  13.4 0.1 copy.80
  13.6 0.6 gather_fusion.1
  14.2 32.7 %reduce-scatter.3.cloned.1.call-done = bf16[64,512]{1,0:T(8,128)(2,1)} async-done(((bf16[64,4096]{1,0:T(8,128)(2,1)}), bf16[64,512]{1,0:T(8,128)(2,1)}) %reduce-scatter.3.cloned.1.call-update) | async-done | bytes 65552 | tf_op jit(solution)/shard_map/reduce_scatter | solution.py:48
  46.8 1.0 fusion.28
  47.8 0.2 fusion.23
  48.0 14.9 %all-reduce = (f32[64]{0:T(128)S(1)}, f32[64,8]{0,1:T(8,128)S(1)}) all-reduce(f32[64]{0:T(128)S(1)} %get-tuple-element.10, f32[64,8]{0,1:T(8,128)S(1)} %fusion.23), channel_id=1, replica_groups=mesh['expert'=32,'tensor'=8] {'tensor'}, use_global_device_ids=true, to_apply=%region_4.0 | all-reduce | flops 576 | bytes 4608 | tf_op jit(solution)/shard_map/psum | solution.py:54
  62.9 0.5 convolution_convert_fusion.2
  63.4 34.6 %all_to_all.10 = bf16[32,32,512]{2,1,0:T(8,128)(2,1)} all-to-all(bf16[32,32,512]{2,1,0:T(8,128)(2,1)S(1)} %convolution_convert_fusion.2), channel_id=1, replica_groups=mesh['expert'=32,'tensor'=8] {'expert'}, dimensions={0} | all-to-all | bytes 2097152 | tf_op jit(solution)/shard_map/all_to_all | solution.py:83
  98.1 50.6 %all-gather.3.cloned.1.call-done = bf16[32,32,4096]{2,1,0:T(8,128)(2,1)} async-done(((bf16[32,32,512]{2,1,0:T(8,128)(2,1)}), bf16[32,32,4096]{2,1,0:T(8,128)(2,1)}) %all-gather.3.cloned.1.call-update) | async-done | bytes 8388624 | tf_op jit(solution)/shard_map/all_gather | solution.py:84
  148.7 6.3 %fusion.3 = f32[32,32,256]{2,1,0:T(8,128)S(1)} fusion(bf16[32,32,4096]{2,1,0:T(8,128)(2,1)} %all-gather.3.cloned.1.call-done, bf16[1,4096,256]{2,1,0:T(8,128)(2,1)} %param.18), kind=kOutput, calls=%fused_computation.9 | convolution fusion | flops 2147483648 | bytes 11534336 | tf_op jit(solution)/shard_map/gmd,df->gmf/dot_general | solution.py:85
  155.0 16.8 %convolution_convert_fusion = bf16[32,32,4096]{2,1,0:T(8,128)(2,1)} fusion(bf16[1,256,4096]{2,1,0:T(8,128)(2,1)S(1)} %copy-done, bf16[32,32,4096]{2,1,0:T(8,128)(2,1)} %all-gather.3.cloned.1.call-done, bf16[1,4096,256]{2,1,0:T(8,128)(2,1)} %param.19, f32[32,32,256]{2,1,0:T(8,128)S(1)} %fusion.3), kind=kOutput, calls=%fused_computation.4 | convolution fusion | flops 4300734464 | bytes 22020096 | tf_op jit(solution)/shard_map/gmf,fd->gmd/dot_general | solution.py:15
  171.8 54.4 %reduce-scatter.5.cloned.1.call-done = bf16[32,32,512]{2,1,0:T(8,128)(2,1)} async-done(((bf16[32,32,4096]{2,1,0:T(8,128)(2,1)}), bf16[32,32,512]{2,1,0:T(8,128)(2,1)}) %reduce-scatter.5.cloned.1.call-update) | async-done | bytes 1048592 | tf_op jit(solution)/shard_map/reduce_scatter | solution.py:16
  226.2 9.5 %all-to-all-start.1 = ((bf16[32,32,512]{2,1,0:T(8,128)(2,1)}), bf16[32,32,512]{2,1,0:T(8,128)(2,1)S(1)}, u32[]{:S(2)}, u32[]{:S(2)}) async-start(bf16[32,32,512]{2,1,0:T(8,128)(2,1)} %reduce-scatter.5.cloned.1.call-done), calls=%async_computation.3 | async-start | bytes 2097152 | tf_op jit(solution)/shard_map/all_to_all | solution.py:19
  235.8 0.2 all-gather.5.cloned.1.call-start
  236.0 0.1 copy.78
  236.1 0.1 copy.76
  236.2 0.1 reshape.129
  236.3 0.1 select_reduce_fusion.2
  236.5 0.1 reshape.125
  236.6 0.6 gather_fusion
  237.2 0.1 copy.77
  237.3 0.1 copy.81
  237.4 0.1 add.139
  237.6 0.1 copy.79
  237.8 0.1 copy.72
  237.9 0.2 fusion.33
  238.1 0.1 fusion.45
  238.2 0.1 copy.84
  238.2 0.1 copy.85
  238.4 0.1 copy.75
  238.4 22.5 %all-to-all-done.1 = bf16[32,32,512]{2,1,0:T(8,128)(2,1)S(1)} async-done(((bf16[32,32,512]{2,1,0:T(8,128)(2,1)}), bf16[32,32,512]{2,1,0:T(8,128)(2,1)S(1)}, u32[]{:S(2)}, u32[]{:S(2)}) %all-to-all-start.1) | async-done | bytes 1048608 | tf_op jit(solution)/shard_map/all_to_all | solution.py:19
  261.0 2.6 gather_fusion.2
  263.6 1.2 gather.21
  264.8 0.9 convert_reduce_fusion
  265.7 0.4 multiply_reduce_fusion
  266.1 0.6 fusion.29
  266.8 0.2 select_reduce_fusion
  267.1 72.8 %all-gather.5.cloned.1.call-done = bf16[2048,512]{1,0:T(8,128)(2,1)} async-done(((bf16[64,512]{1,0:T(8,128)(2,1)}), bf16[2048,512]{1,0:T(8,128)(2,1)}) %all-gather.5.cloned.1.call-update) | async-done | bytes 2097168 | tf_op jit(solution)/shard_map/all_gather | solution.py:103
  339.9 2.6 gather_fusion.3
  342.5 0.2 fusion.25
  342.7 17.1 %psum.23 = f32[64]{0:T(128)S(1)} all-reduce(f32[64]{0:T(128)S(1)} %get-tuple-element.4), channel_id=1, replica_groups=mesh['expert'=32,'tensor'=8] {'tensor'}, use_global_device_ids=true, to_apply=%region_14.15 | all-reduce | flops 64 | bytes 512 | tf_op jit(solution)/shard_map/psum | solution.py:24
  359.7 0.7 fusion.27
  (43 shorter events, 0.4 us)
Async XLA Ops:
  7.2 147.8 %copy-start = (bf16[1,256,4096]{2,1,0:T(8,128)(2,1)S(1)}, bf16[1,256,4096]{2,1,0:T(8,128)(2,1)}, u32[]{:S(2)}) copy-start(bf16[1,256,4096]{2,1,0:T(8,128)(2,1)} %param.20) | copy-start | bytes 6291460
  7.2 4.1 %copy-start.6 = (s32[64,2]{0,1:T(2,128)S(1)}, s32[64,2]{0,1:T(2,128)}, u32[]{:S(2)}) copy-start(s32[64,2]{0,1:T(2,128)} %param.17) | copy-start | bytes 1540
  7.2 39.6 %reduce-scatter.3.cloned.1.call-start = ((), (), s32[]{:S(2)}) async-start(), calls=%async_computation.4 | async-start | bytes 589824 | tf_op jit(solution)/shard_map/reduce_scatter | solution.py:48
  11.2 2.3 copy-start.8
  11.2 35.6 %copy-start.2 = (bf16[64,512]{1,0:T(8,128)(2,1)S(1)}, bf16[64,512]{1,0:T(8,128)(2,1)}, u32[]{:S(2)}) copy-start(bf16[64,512]{1,0:T(8,128)(2,1)} %param.13) | copy-start | bytes 196612
  11.2 36.6 %copy-start.3 = (f32[512,8]{0,1:T(8,128)S(1)}, f32[512,8]{0,1:T(8,128)}, u32[]{:S(2)}) copy-start(f32[512,8]{0,1:T(8,128)} %param.16) | copy-start | bytes 49156
  11.2 36.6 %copy-start.4 = (f32[512]{0:T(512)S(1)}, f32[512]{0:T(512)}, u32[]{:S(2)}) copy-start(f32[512]{0:T(512)} %param.15) | copy-start | bytes 6148
  11.3 137.4 %all-gather.3.cloned.1.call-start = ((), (), s32[]{:S(2)}) async-start(), calls=%async_computation.5 | async-start | bytes 9437184 | tf_op jit(solution)/shard_map/all_gather | solution.py:84
  98.0 128.2 %reduce-scatter.5.cloned.1.call-start = ((), (), s32[]{:S(2)}) async-start(), calls=%async_computation.6 | async-start | bytes 9437184 | tf_op jit(solution)/shard_map/reduce_scatter | solution.py:16
  226.2 34.7 %all-to-all-start.1 = ((bf16[32,32,512]{2,1,0:T(8,128)(2,1)}), bf16[32,32,512]{2,1,0:T(8,128)(2,1)S(1)}, u32[]{:S(2)}, u32[]{:S(2)}) async-start(bf16[32,32,512]{2,1,0:T(8,128)(2,1)} %reduce-scatter.5.cloned.1.call-done), calls=%async_computation.3 | async-start | bytes 2097152 | tf_op jit(solution)/shard_map/all_to_all | solution.py:19
  235.8 104.1 %all-gather.5.cloned.1.call-start = ((), (), s32[]{:S(2)}) async-start(), calls=%async_computation.7 | async-start | bytes 2162688 | tf_op jit(solution)/shard_map/all_gather | solution.py:103
  263.6 3.2 copy-start.5
  263.6 96.2 %copy-start.7 = (f32[512]{0:T(512)S(1)}, f32[512]{0:T(512)}, u32[]{:S(2)}) copy-start(f32[512]{0:T(512)} %param.22) | copy-start | bytes 6148
  342.6 17.8 %copy-start.1 = (bf16[64,512]{1,0:T(8,128)(2,1)}, bf16[64,512]{1,0:T(8,128)(2,1)S(1)}, u32[]{:S(2)}) copy-start(bf16[64,512]{1,0:T(8,128)(2,1)S(1)} %get-tuple-element.5) | copy-start | bytes 196612
Sparse Core Ops, SparseCore 0:
  11.4 35.4 reduce-scatter.2
  98.1 50.5 all-gather.2
  172.0 54.2 reduce-scatter.4
  266.9 72.9 all-gather.4

commit v2 on v1

--- a/solution.py
+++ b/solution.py
@@ -1,7 +1,7 @@
 import jax
 import jax.numpy as jnp
 from jax import lax
-from jax.sharding import PartitionSpec as P
+from jax.sharding import Mesh, PartitionSpec as P
 
 D = 4096
 MOST = 32
@@ -16,7 +16,7 @@
     summed = lax.psum_scatter(
         partial_out.astype(jnp.bfloat16), "tensor", scatter_dimension=2, tiled=True
     )
-    return lax.all_to_all(summed, "expert", split_axis=0, concat_axis=0, tiled=True)
+    return lax.all_to_all(summed, EXPERT, split_axis=0, concat_axis=0, tiled=True)
 
 
 def final_norm(stream, final_gain):
@@ -24,6 +24,50 @@
     square_total = lax.psum(jnp.sum(stream_f * stream_f, axis=1), "tensor")
     factor = lax.rsqrt(square_total / D + EPS)
     return (stream_f * factor[:, None] * final_gain).astype(jnp.bfloat16)
+
+
+EXPERT = ("ex", "ez")
+
+
+def restore(stream, row_order, source):
+    outer = lax.axis_size("ex")
+    inner = lax.axis_size("ez")
+    rows = stream.shape[0]
+    x_idx = lax.axis_index("ex")
+    z_idx = lax.axis_index("ez")
+    e_idx = x_idx * inner + z_idx
+    gathered = lax.all_gather(stream, "ex", axis=0, tiled=True)
+    dest = row_order // rows
+    held = (
+        (jnp.arange(outer, dtype=jnp.int32)[:, None] * inner + z_idx) * rows
+        + jnp.arange(rows, dtype=jnp.int32)[None, :]
+    ).reshape(-1)
+    held_dest = jnp.take(dest, held, axis=0)
+    count = held.shape[0]
+    order = jnp.arange(count, dtype=jnp.int32)
+    earlier = (held_dest[:, None] == held_dest[None, :]) & (order[None, :] < order[:, None])
+    held_slot = jnp.sum(earlier.astype(jnp.int32), axis=1)
+    mine = (held_dest // inner) == x_idx
+    pick = (
+        mine[None, None, :]
+        & ((held_dest % inner)[None, None, :] == jnp.arange(inner, dtype=jnp.int32)[:, None, None])
+        & (held_slot[None, None, :] == jnp.arange(rows, dtype=jnp.int32)[None, :, None])
+    ).astype(jnp.bfloat16)
+    send = jnp.einsum("zkg,gf->zkf", pick, gathered, preferred_element_type=jnp.float32).astype(
+        jnp.bfloat16
+    )
+    received = lax.all_to_all(send, "ez", split_axis=0, concat_axis=0, tiled=True)
+    arrival = jnp.arange(row_order.shape[0], dtype=jnp.int32)
+    column = (arrival // rows) % inner
+    source_column = (source // rows) % inner
+    before = (
+        (dest == e_idx)[None, :]
+        & (column[None, :] == source_column[:, None])
+        & (arrival[None, :] < source[:, None])
+    )
+    slot = jnp.sum(before.astype(jnp.int32), axis=1)
+    flat = received.reshape(inner * rows, received.shape[2])
+    return jnp.take(flat, source_column * rows + slot, axis=0)
 
 
 def on_device(
@@ -40,7 +84,7 @@
     final_gain,
     row_order,
 ):
-    groups = lax.axis_size("expert")
+    groups = lax.axis_size("ex") * lax.axis_size("ez")
     row_count = attn_vals.shape[0]
     expert_count = router_weight.shape[1]
     slab_count = groups // expert_count
@@ -80,7 +124,7 @@
     outgoing = jnp.einsum(
         "gsr,rd->gsd", send_map, normed_in, preferred_element_type=jnp.float32
     ).astype(jnp.bfloat16)
-    arrived_part = lax.all_to_all(outgoing, "expert", split_axis=0, concat_axis=0, tiled=True)
+    arrived_part = lax.all_to_all(outgoing, EXPERT, split_axis=0, concat_axis=0, tiled=True)
     arrived = lax.all_gather(arrived_part, "tensor", axis=2, tiled=True)
     gate_val = jnp.einsum("gmd,df->gmf", arrived, w_gate[0], preferred_element_type=jnp.float32)
     up_val = jnp.einsum("gmd,df->gmf", arrived, w_up[0], preferred_element_type=jnp.float32)
@@ -97,32 +141,45 @@
     expert_out = jnp.sum(fetched.astype(jnp.float32), axis=2)
     blended = jnp.sum(mixing[:, :, None] * expert_out, axis=1)
     stream = (hidden_f + blended).astype(jnp.bfloat16)
-    positions = lax.axis_index("expert") * row_count + jnp.arange(row_count, dtype=jnp.int32)
+    positions = (lax.axis_index("ex") * lax.axis_size("ez") + lax.axis_index("ez")) * row_count + jnp.arange(row_count, dtype=jnp.int32)
     matches = (row_order[None, :] == positions[:, None]).astype(jnp.int32)
     source = jnp.sum(matches * jnp.arange(row_order.shape[0], dtype=jnp.int32)[None, :], axis=1)
-    all_stream = lax.all_gather(stream, "expert", axis=0, tiled=True)
-    ordered = jnp.take(all_stream, source, axis=0)
+    ordered = restore(stream, row_order, source)
     return (ordered, final_norm(ordered, final_gain))
 
 
+def outer_size(mesh):
+    column = mesh.devices[:, 0]
+    try:
+        outer = len({d.coords[0] for d in column})
+    except AttributeError:
+        outer = 1
+    if outer < 1 or column.shape[0] % outer:
+        outer = 1
+    return outer
+
+
 def solution(mesh):
+    outer = outer_size(mesh)
+    shape = mesh.devices.shape
+    split = Mesh(mesh.devices.reshape(outer, shape[0] // outer, shape[1]), ("ex", "ez", "tensor"))
     return jax.shard_map(
         on_device,
-        mesh=mesh,
+        mesh=split,
         in_specs=(
-            P("expert", "tensor"),
-            P("expert", "tensor"),
+            P(EXPERT, "tensor"),
+            P(EXPERT, "tensor"),
             P("tensor", None),
             P("tensor"),
             P("tensor", None),
-            P("expert", None),
-            P("expert", None, "tensor"),
-            P("expert", None, "tensor"),
-            P("expert", "tensor", None),
+            P(EXPERT, None),
+            P(EXPERT, None, "tensor"),
+            P(EXPERT, None, "tensor"),
+            P(EXPERT, "tensor", None),
             P(),
             P("tensor"),
             P(),
         ),
-        out_specs=(P("expert", "tensor"), P("expert", "tensor")),
+        out_specs=(P(EXPERT, "tensor"), P(EXPERT, "tensor")),
         check_vma=False,
     )

time: 367 us -> 323 us (0.88)
  waiting for transfers between devices: 233 us -> 170 us
  blocking collectives: 66.5 us -> 77.4 us
  starting transfers between devices: 9.88 us -> 15.4 us
    all_gather x1 -> x0, waiting for transfers between devices: 72.8 us -> none  [on_device(): all_stream = lax.all_gather(stream, 'expert', axis=0, tiled=True)]
    all_to_all x1 -> x2, waiting for transfers between devices: 22.5 us -> 35.5 us  [the longest x1 23.8 us: finish_slots(): lax.all_to_all(summed, EXPERT, split_axis=0, concat_axis=0, tiled=True)]
    all_gather x0 -> x1, blocking collectives: none -> 9.74 us  [restore(): gathered = lax.all_gather(stream, 'ex', axis=0, tiled=True)]
    all_to_all x1 -> x2, starting transfers between devices: 9.53 us -> 15.3 us  [the longest x1 9.72 us: finish_slots(): lax.all_to_all(summed, EXPERT, split_axis=0, concat_axis=0, tiled=True)]
    reduce_scatter x1, waiting for transfers between devices: 54.4 us -> 50.6 us  [finish_slots(): lax.psum_scatter(partial_out.astype(jnp.bfloat16), 'tensor', scatter_dime...]
  transfers between devices with their start and end apart: 5 -> 5, of which waited for: 5 -> 5; matrix products, arithmetic and copies ran while one was open for 1% -> 2% of each run, Pallas kernels for 0% -> 0%
where the time goes in v2:
time: 323 us; the launch traced here: 322 us
  waiting for transfers between devices  170 us (53%)
  blocking collectives  77.4 us (24%)
  matrix products  30.6 us (9%)
  starting transfers between devices  15.4 us (5%)
  between operations  14.1 us (4%)
  local copies, waits for them, and re-layouts  9.16 us (3%)
  other arithmetic  6.09 us (2%)
    all_gather x1, waiting for transfers between devices, on_device(): arrived = lax.all_gather(arrived_part, 'tensor', axis=2, tiled=True)  50.6 us
    reduce_scatter x1, waiting for transfers between devices, finish_slots(): lax.psum_scatter(partial_out.astype(jnp.bfloat16), 'tensor', scatter_dime...  50.6 us
    all_to_all x1, blocking collectives, on_device(): lax.all_to_all(outgoing, EXPERT, split_axis=0, concat_axis=0, tiled=True)  34.5 us
    reduce_scatter x1, waiting for transfers between devices, on_device(): lax.psum_scatter(partial_proj.astype(jnp.bfloat16), 'tensor', scatter_dim...  32.7 us
    all_to_all x1, waiting for transfers between devices, finish_slots(): lax.all_to_all(summed, EXPERT, split_axis=0, concat_axis=0, tiled=True)  23.8 us
    psum x1, blocking collectives, final_norm(): square_total = lax.psum(jnp.sum(stream_f * stream_f, axis=1), 'tensor')  18.2 us
    dot_general x1, matrix products, finish_slots(): jnp.einsum('gmf,fd->gmd', active, down_weight, preferred_element_type=jnp...  17.1 us
    psum x1, blocking collectives, on_device(): lax.psum((jnp.sum(hidden_f * hidden_f, axis=1), jnp.dot(scaled, router_we...  14.9 us
  transfers between devices with their start and end apart: 5, of which 5 were waited for; matrix products, arithmetic and copies ran while one was open for 2% of the time, Pallas kernels for 0%

profile of v2, /device:TPU:1, one launch (start us, length us, event | category | flops | bytes accessed | tf_op | source)
XLA Modules:
  0.0 322.2 jit_solution(12865642854557493589)
XLA Ops:
  7.3 4.0 %convolution_convert_fusion.1 = bf16[64,4096]{1,0:T(8,128)(2,1)} fusion(bf16[64,512]{1,0:T(8,128)(2,1)} %param.12, bf16[512,4096]{1,0:T(8,128)(2,1)} %param.14), kind=kOutput, calls=%fused_computation.6 | convolution fusion | flops 268697600 | bytes 4784128 | tf_op jit(solution)/shard_map/dot_general | solution.py:91
  11.3 0.1 copy.71
  11.4 0.2 convert_reduce_fusion.3
  11.6 0.1 reduce_window_sum.11
  11.7 1.2 select_reduce_fusion.1
  13.0 0.4 fusion.13
  13.4 0.1 copy.80
  13.6 0.6 gather_fusion.2
  14.2 32.7 %reduce-scatter.3.cloned.1.call-done = bf16[64,512]{1,0:T(8,128)(2,1)} async-done(((bf16[64,4096]{1,0:T(8,128)(2,1)}), bf16[64,512]{1,0:T(8,128)(2,1)}) %reduce-scatter.3.cloned.1.call-update) | async-done | bytes 65552 | tf_op jit(solution)/shard_map/reduce_scatter | solution.py:92
  46.9 1.0 fusion.34
  47.9 0.2 fusion.29
  48.1 14.9 %all-reduce = (f32[64]{0:T(128)S(1)}, f32[64,8]{0,1:T(8,128)S(1)}) all-reduce(f32[64]{0:T(128)S(1)} %get-tuple-element.14, f32[64,8]{0,1:T(8,128)S(1)} %fusion.29), channel_id=1, replica_groups=mesh['ex'=4,'ez'=8,'tensor'=8] {'tensor'}, use_global_device_ids=true, to_apply=%region_6.0 | all-reduce | flops 576 | bytes 4608 | tf_op jit(solution)/shard_map/psum | solution.py:98
  63.0 0.5 convolution_convert_fusion.2
  63.5 34.5 %all_to_all.15 = bf16[32,32,512]{2,1,0:T(8,128)(2,1)} all-to-all(bf16[32,32,512]{2,1,0:T(8,128)(2,1)S(1)} %convolution_convert_fusion.2), channel_id=1, replica_groups=mesh['ex'=4,'ez'=8,'tensor'=8] {'ex','ez'}, dimensions={0} | all-to-all | bytes 2097152 | tf_op jit(solution)/shard_map/all_to_all | solution.py:127
  98.1 50.6 %all-gather.2.cloned.1.call-done = bf16[32,32,4096]{2,1,0:T(8,128)(2,1)} async-done(((bf16[32,32,512]{2,1,0:T(8,128)(2,1)}), bf16[32,32,4096]{2,1,0:T(8,128)(2,1)}) %all-gather.2.cloned.1.call-update) | async-done | bytes 8388624 | tf_op jit(solution)/shard_map/all_gather | solution.py:128
  148.7 7.3 %fusion.3 = f32[32,32,256]{2,1,0:T(8,128)} fusion(bf16[32,32,4096]{2,1,0:T(8,128)(2,1)} %all-gather.2.cloned.1.call-done, bf16[1,4096,256]{2,1,0:T(8,128)(2,1)} %param.18), kind=kOutput, calls=%fused_computation.10 | convolution fusion | flops 2147483648 | bytes 11534336 | tf_op jit(solution)/shard_map/gmd,df->gmf/dot_general | solution.py:129
  156.0 17.1 %convolution_convert_fusion = bf16[32,32,4096]{2,1,0:T(8,128)(2,1)} fusion(bf16[1,256,4096]{2,1,0:T(8,128)(2,1)S(1)} %copy-done, bf16[32,32,4096]{2,1,0:T(8,128)(2,1)} %all-gather.2.cloned.1.call-done, bf16[1,4096,256]{2,1,0:T(8,128)(2,1)} %param.19, f32[32,32,256]{2,1,0:T(8,128)} %fusion.3), kind=kOutput, calls=%fused_computation.5 | convolution fusion | flops 4300734464 | bytes 22020096 | tf_op jit(solution)/shard_map/gmf,fd->gmd/dot_general | solution.py:15
  173.3 0.1 add.310
  173.4 0.1 copy.76
  173.5 0.1 reshape.452
  173.7 0.1 select_reduce_fusion.2
  173.9 0.6 gather_fusion.1
  174.5 0.1 copy.77
  174.6 0.1 copy.81
  174.8 0.1 add.326
  174.9 0.1 copy.79
  175.1 1.7 gather_fusion
  176.9 50.6 %reduce-scatter.5.cloned.1.call-done = bf16[32,32,512]{2,1,0:T(8,128)(2,1)} async-done(((bf16[32,32,4096]{2,1,0:T(8,128)(2,1)}), bf16[32,32,512]{2,1,0:T(8,128)(2,1)}) %reduce-scatter.5.cloned.1.call-update) | async-done | bytes 1048592 | tf_op jit(solution)/shard_map/reduce_scatter | solution.py:16
  227.5 9.7 %all-to-all-start.1 = ((bf16[32,32,512]{2,1,0:T(8,128)(2,1)}), bf16[32,32,512]{2,1,0:T(8,128)(2,1)S(1)}, u32[]{:S(2)}, u32[]{:S(2)}) async-start(bf16[32,32,512]{2,1,0:T(8,128)(2,1)} %reduce-scatter.5.cloned.1.call-done), calls=%async_computation.3 | async-start | bytes 2097152 | tf_op jit(solution)/shard_map/all_to_all | solution.py:19
  237.2 0.2 convert_reduce_fusion.2
  237.4 0.2 select_reduce_fusion
  237.7 0.1 copy.72
  237.8 0.2 fusion.39
  238.3 0.1 copy.75
  238.4 23.8 %all-to-all-done.1 = bf16[32,32,512]{2,1,0:T(8,128)(2,1)S(1)} async-done(((bf16[32,32,512]{2,1,0:T(8,128)(2,1)}), bf16[32,32,512]{2,1,0:T(8,128)(2,1)S(1)}, u32[]{:S(2)}, u32[]{:S(2)}) %all-to-all-start.1) | async-done | bytes 1048608 | tf_op jit(solution)/shard_map/all_to_all | solution.py:19
  262.2 2.6 gather_fusion.3
  264.8 1.2 gather.26
  266.0 0.9 convert_reduce_fusion
  266.9 0.4 multiply_reduce_fusion
  267.4 9.7 %all_gather.7 = bf16[256,512]{1,0:T(8,128)(2,1)S(1)} all-gather(bf16[64,512]{1,0:T(8,128)(2,1)S(1)} %fusion.35), channel_id=1, replica_groups=mesh['ex'=4,'ez'=8,'tensor'=8] {'ex'}, dimensions={0}, use_global_device_ids=true | all-gather | bytes 327680 | tf_op jit(solution)/shard_map/all_gather | solution.py:39
  277.1 1.1 convolution_convert_fusion.3
  278.2 5.5 %all-to-all-start.2 = ((bf16[8,64,512]{2,1,0:T(8,128)(2,1)}), bf16[8,64,512]{2,1,0:T(8,128)(2,1)S(1)}, u32[]{:S(2)}, u32[]{:S(2)}) async-start(bf16[8,64,512]{2,1,0:T(8,128)(2,1)} %convolution_convert_fusion.3), calls=%async_computation.4 | async-start | bytes 1048576 | tf_op jit(solution)/shard_map/all_to_all | solution.py:59
  283.8 0.3 convert_reduce_fusion.1
  284.1 11.7 %all-to-all-done.2 = bf16[8,64,512]{2,1,0:T(8,128)(2,1)S(1)} async-done(((bf16[8,64,512]{2,1,0:T(8,128)(2,1)}), bf16[8,64,512]{2,1,0:T(8,128)(2,1)S(1)}, u32[]{:S(2)}, u32[]{:S(2)}) %all-to-all-start.2) | async-done | bytes 524320 | tf_op jit(solution)/shard_map/all_to_all | solution.py:59
  295.8 0.7 gather_fusion.4
  296.5 0.2 fusion.31
  296.7 18.2 %psum.23 = f32[64]{0:T(128)S(1)} all-reduce(f32[64]{0:T(128)S(1)} %get-tuple-element.4), channel_id=1, replica_groups=mesh['ex'=4,'ez'=8,'tensor'=8] {'tensor'}, use_global_device_ids=true, to_apply=%region_16.17 | all-reduce | flops 64 | bytes 512 | tf_op jit(solution)/shard_map/psum | solution.py:24
  314.9 0.7 fusion.33
  (60 shorter events, 1.0 us)
Async XLA Ops:
  7.2 148.9 %copy-start = (bf16[1,256,4096]{2,1,0:T(8,128)(2,1)S(1)}, bf16[1,256,4096]{2,1,0:T(8,128)(2,1)}, u32[]{:S(2)}) copy-start(bf16[1,256,4096]{2,1,0:T(8,128)(2,1)} %param.20) | copy-start | bytes 6291460
  7.2 4.2 %copy-start.6 = (s32[64,2]{0,1:T(2,128)S(1)}, s32[64,2]{0,1:T(2,128)}, u32[]{:S(2)}) copy-start(s32[64,2]{0,1:T(2,128)} %param.17) | copy-start | bytes 1540
  7.2 6.4 %copy-start.8 = (s32[32]{0:T(128)S(1)}, s32[32]{0:T(128)}, u32[]{:S(2)}) copy-start(s32[32]{0:T(128)} %param.21) | copy-start | bytes 388
  7.2 39.7 %copy-start.2 = (bf16[64,512]{1,0:T(8,128)(2,1)S(1)}, bf16[64,512]{1,0:T(8,128)(2,1)}, u32[]{:S(2)}) copy-start(bf16[64,512]{1,0:T(8,128)(2,1)} %param.13) | copy-start | bytes 196612
  7.2 40.7 %copy-start.5 = (f32[512]{0:T(512)S(1)}, f32[512]{0:T(512)}, u32[]{:S(2)}) copy-start(f32[512]{0:T(512)} %param.15) | copy-start | bytes 6148
  7.2 40.7 %copy-start.4 = (f32[512,8]{0,1:T(8,128)S(1)}, f32[512,8]{0,1:T(8,128)}, u32[]{:S(2)}) copy-start(f32[512,8]{0,1:T(8,128)} %param.16) | copy-start | bytes 49156
  7.2 39.7 %reduce-scatter.3.cloned.1.call-start = ((), (), s32[]{:S(2)}) async-start(), calls=%async_computation.5 | async-start | bytes 589824 | tf_op jit(solution)/shard_map/reduce_scatter | solution.py:92
  11.3 137.4 %all-gather.2.cloned.1.call-start = ((), (), s32[]{:S(2)}) async-start(), calls=%async_computation.6 | async-start | bytes 9437184 | tf_op jit(solution)/shard_map/all_gather | solution.py:128
  98.0 129.5 %reduce-scatter.5.cloned.1.call-start = ((), (), s32[]{:S(2)}) async-start(), calls=%async_computation.7 | async-start | bytes 9437184 | tf_op jit(solution)/shard_map/reduce_scatter | solution.py:16
  173.1 2.0 copy-start.3
  227.5 34.7 %all-to-all-start.1 = ((bf16[32,32,512]{2,1,0:T(8,128)(2,1)}), bf16[32,32,512]{2,1,0:T(8,128)(2,1)S(1)}, u32[]{:S(2)}, u32[]{:S(2)}) async-start(bf16[32,32,512]{2,1,0:T(8,128)(2,1)} %reduce-scatter.5.cloned.1.call-done), calls=%async_computation.3 | async-start | bytes 2097152 | tf_op jit(solution)/shard_map/all_to_all | solution.py:19
  262.2 52.7 %copy-start.7 = (f32[512]{0:T(512)S(1)}, f32[512]{0:T(512)}, u32[]{:S(2)}) copy-start(f32[512]{0:T(512)} %param.22) | copy-start | bytes 6148
  278.2 17.6 %all-to-all-start.2 = ((bf16[8,64,512]{2,1,0:T(8,128)(2,1)}), bf16[8,64,512]{2,1,0:T(8,128)(2,1)S(1)}, u32[]{:S(2)}, u32[]{:S(2)}) async-start(bf16[8,64,512]{2,1,0:T(8,128)(2,1)} %convolution_convert_fusion.3), calls=%async_computation.4 | async-start | bytes 1048576 | tf_op jit(solution)/shard_map/all_to_all | solution.py:59
  296.7 19.0 %copy-start.1 = (bf16[64,512]{1,0:T(8,128)(2,1)}, bf16[64,512]{1,0:T(8,128)(2,1)S(1)}, u32[]{:S(2)}) copy-start(bf16[64,512]{1,0:T(8,128)(2,1)S(1)} %get-tuple-element.5) | copy-start | bytes 196612
Sparse Core Ops, SparseCore 0:
  11.4 35.4 reduce-scatter.2
  98.2 50.5 all-gather.1
  173.2 54.2 reduce-scatter.4

commit v3 on v2

--- a/solution.py
+++ b/solution.py
@@ -5,6 +5,7 @@
 
 D = 4096
 MOST = 32
+CHUNKS = 2
 
 
 EPS = 1e-05
@@ -124,11 +125,16 @@
     outgoing = jnp.einsum(
         "gsr,rd->gsd", send_map, normed_in, preferred_element_type=jnp.float32
     ).astype(jnp.bfloat16)
-    arrived_part = lax.all_to_all(outgoing, EXPERT, split_axis=0, concat_axis=0, tiled=True)
-    arrived = lax.all_gather(arrived_part, "tensor", axis=2, tiled=True)
-    gate_val = jnp.einsum("gmd,df->gmf", arrived, w_gate[0], preferred_element_type=jnp.float32)
-    up_val = jnp.einsum("gmd,df->gmf", arrived, w_up[0], preferred_element_type=jnp.float32)
-    returned = finish_slots(gate_val, up_val, w_down[0])
+    step = MOST // CHUNKS
+    pieces = []
+    for c in range(CHUNKS):
+        part = outgoing[:, c * step : (c + 1) * step]
+        arrived_part = lax.all_to_all(part, EXPERT, split_axis=0, concat_axis=0, tiled=True)
+        arrived = lax.all_gather(arrived_part, "tensor", axis=2, tiled=True)
+        gate_val = jnp.einsum("gmd,df->gmf", arrived, w_gate[0], preferred_element_type=jnp.float32)
+        up_val = jnp.einsum("gmd,df->gmf", arrived, w_up[0], preferred_element_type=jnp.float32)
+        pieces.append(finish_slots(gate_val, up_val, w_down[0]))
+    returned = jnp.concatenate(pieces, axis=1)
     group_ids = jnp.arange(groups, dtype=jnp.int32)
     holder_hot = (slab_of[None, :] == group_ids[:, None]).astype(jnp.int32)
     holders = jnp.sum(holder_hot * group_ids[None, :], axis=1).reshape(expert_count, slab_count)

time: 323 us -> 326 us (level)
  waiting for transfers between devices: 170 us -> 144 us
  blocking collectives: 77.4 us -> 92.7 us
  starting transfers between devices: 15.4 us -> 24.2 us
    all_gather x1 -> x2, waiting for transfers between devices: 50.6 us -> 34.1 us  [on_device(): arrived = lax.all_gather(arrived_part, 'tensor', axis=2, tiled=True)]
    all_to_all x1 -> x2, waiting for transfers between devices: 23.8 us -> 11 us  [finish_slots(): lax.all_to_all(summed, EXPERT, split_axis=0, concat_axis=0, tiled=True)]
    all_to_all x1 -> x2, blocking collectives: 34.5 us -> 44.9 us  [on_device(): lax.all_to_all(part, EXPERT, split_axis=0, concat_axis=0, tiled=True)]
    all_to_all x1 -> x2, starting transfers between devices: 9.72 us -> 18.8 us  [finish_slots(): lax.all_to_all(summed, EXPERT, split_axis=0, concat_axis=0, tiled=True)]
    psum x1, blocking collectives: 18.2 us -> 23.5 us  [final_norm(): square_total = lax.psum(jnp.sum(stream_f * stream_f, axis=1), 'tensor')]
    reduce_scatter x1 -> x2, waiting for transfers between devices: 50.6 us -> 54.8 us  [finish_slots(): lax.psum_scatter(partial_out.astype(jnp.bfloat16), 'tensor', scatter_dime...]
    dot_general x1 -> x2, matrix products: 17.1 us -> 18.6 us  [finish_slots(): jnp.einsum('gmf,fd->gmd', active, down_weight, preferred_element_type=jnp...]
    dot_general x1 -> x2, matrix products: 7.3 us -> 8.23 us  [on_device(): jnp.einsum('gmd,df->gmf', arrived, w_gate[0], preferred_element_type=jnp....]
  transfers between devices with their start and end apart: 5 -> 8, of which waited for: 5 -> 7; matrix products, arithmetic and copies ran while one was open for 2% -> 11% of each run, Pallas kernels for 0% -> 0%
where the time goes in v3:
time: 326 us; the launch traced here: 325 us
  waiting for transfers between devices  144 us (44%)
  blocking collectives  92.7 us (28%)
  matrix products  33.1 us (10%)
  starting transfers between devices  24.2 us (7%)
  between operations  14.2 us (4%)
  local copies, waits for them, and re-layouts  9.24 us (3%)
  other arithmetic  7.37 us (2%)
    reduce_scatter x2, waiting for transfers between devices, finish_slots(): lax.psum_scatter(partial_out.astype(jnp.bfloat16), 'tensor', scatter_dime...  54.8 us
    all_to_all x2, blocking collectives, on_device(): lax.all_to_all(part, EXPERT, split_axis=0, concat_axis=0, tiled=True)  44.9 us
    all_gather x2, waiting for transfers between devices, on_device(): arrived = lax.all_gather(arrived_part, 'tensor', axis=2, tiled=True)  34.1 us
    reduce_scatter x1, waiting for transfers between devices, on_device(): lax.psum_scatter(partial_proj.astype(jnp.bfloat16), 'tensor', scatter_dim...  32.7 us
    psum x1, blocking collectives, final_norm(): square_total = lax.psum(jnp.sum(stream_f * stream_f, axis=1), 'tensor')  23.5 us
    all_to_all x2, starting transfers between devices, finish_slots(): lax.all_to_all(summed, EXPERT, split_axis=0, concat_axis=0, tiled=True)  18.8 us
    dot_general x2, matrix products, finish_slots(): jnp.einsum('gmf,fd->gmd', active, down_weight, preferred_element_type=jnp...  18.6 us
    psum x1, blocking collectives, on_device(): lax.psum((jnp.sum(hidden_f * hidden_f, axis=1), jnp.dot(scaled, router_we...  14.9 us
  transfers between devices with their start and end apart: 8, of which 7 were waited for; matrix products, arithmetic and copies ran while one was open for 11% of the time, Pallas kernels for 0%

profile of v3, /device:TPU:1, one launch (start us, length us, event | category | flops | bytes accessed | tf_op | source)
XLA Modules:
  0.0 325.1 jit_solution(17196450116427280761)
XLA Ops:
  7.2 4.0 %convolution_convert_fusion.2 = bf16[64,4096]{1,0:T(8,128)(2,1)} fusion(bf16[64,512]{1,0:T(8,128)(2,1)} %param.12, bf16[512,4096]{1,0:T(8,128)(2,1)} %param.14), kind=kOutput, calls=%fused_computation.7 | convolution fusion | flops 268697600 | bytes 4784128 | tf_op jit(solution)/shard_map/dot_general | solution.py:92
  11.4 0.2 convert_reduce_fusion.3
  11.7 1.2 select_reduce_fusion.1
  12.9 0.4 fusion.26
  13.4 0.1 copy.80
  13.6 0.6 gather_fusion.2
  14.2 32.7 %reduce-scatter.4.cloned.1.call-done = bf16[64,512]{1,0:T(8,128)(2,1)} async-done(((bf16[64,4096]{1,0:T(8,128)(2,1)}), bf16[64,512]{1,0:T(8,128)(2,1)}) %reduce-scatter.4.cloned.1.call-update) | async-done | bytes 65552 | tf_op jit(solution)/shard_map/reduce_scatter | solution.py:93
  46.8 1.0 fusion.53
  47.8 0.2 fusion.48
  48.0 14.9 %all-reduce = (f32[64]{0:T(128)S(1)}, f32[64,8]{0,1:T(8,128)S(1)}) all-reduce(f32[64]{0:T(128)S(1)} %get-tuple-element.14, f32[64,8]{0,1:T(8,128)S(1)} %fusion.48), channel_id=1, replica_groups=mesh['ex'=4,'ez'=8,'tensor'=8] {'tensor'}, use_global_device_ids=true, to_apply=%region_6.0 | all-reduce | flops 576 | bytes 4608 | tf_op jit(solution)/shard_map/psum | solution.py:99
  62.9 0.5 convolution_convert_fusion.3
  63.5 23.4 %all_to_all.25 = bf16[32,16,512]{2,1,0:T(8,128)(2,1)} all-to-all(bf16[32,16,512]{2,1,0:T(8,128)(2,1)S(1)} %get-tuple-element.18), channel_id=1, replica_groups=mesh['ex'=4,'ez'=8,'tensor'=8] {'ex','ez'}, dimensions={0} | all-to-all | bytes 1048576 | tf_op jit(solution)/shard_map/all_to_all | solution.py:132
  87.0 21.5 %all_to_all.26 = bf16[32,16,512]{2,1,0:T(8,128)(2,1)} all-to-all(bf16[32,16,512]{2,1,0:T(8,128)(2,1)S(1)} %get-tuple-element.19), channel_id=1, replica_groups=mesh['ex'=4,'ez'=8,'tensor'=8] {'ex','ez'}, dimensions={0} | all-to-all | bytes 1048576 | tf_op jit(solution)/shard_map/all_to_all | solution.py:132
  108.6 11.3 %all-gather.3.cloned.1.call-done = bf16[32,16,4096]{2,1,0:T(8,128)(2,1)} async-done(((bf16[32,16,512]{2,1,0:T(8,128)(2,1)}), bf16[32,16,4096]{2,1,0:T(8,128)(2,1)}) %all-gather.3.cloned.1.call-update) | async-done | bytes 4194320 | tf_op jit(solution)/shard_map/all_gather | solution.py:133
  119.9 4.1 %fusion.8 = f32[32,16,256]{2,1,0:T(8,128)S(1)} fusion(bf16[32,16,4096]{2,1,0:T(8,128)(2,1)} %all-gather.3.cloned.1.call-done, bf16[1,4096,256]{2,1,0:T(8,128)(2,1)} %param.18), kind=kOutput, calls=%fused_computation.16 | convolution fusion | flops 1073741824 | bytes 6815744 | tf_op jit(solution)/shard_map/gmd,df->gmf/dot_general | solution.py:134
  124.0 9.3 %convolution_convert_fusion.1 = bf16[32,16,4096]{2,1,0:T(8,128)(2,1)} fusion(bf16[1,256,4096]{2,1,0:T(8,128)(2,1)S(1)} %copy-done, bf16[32,16,4096]{2,1,0:T(8,128)(2,1)} %all-gather.3.cloned.1.call-done, bf16[1,4096,256]{2,1,0:T(8,128)(2,1)} %param.19, f32[32,16,256]{2,1,0:T(8,128)S(1)} %fusion.8), kind=kOutput, calls=%fused_computation.6 | convolution fusion | flops 2150367232 | bytes 13107200 | tf_op jit(solution)/shard_map/gmf,fd->gmd/dot_general | solution.py:16
  133.4 0.2 reduce-scatter.8.cloned.1.call-start
  133.6 22.8 %all-gather.5.cloned.1.call-done = bf16[32,16,4096]{2,1,0:T(8,128)(2,1)} async-done(((bf16[32,16,512]{2,1,0:T(8,128)(2,1)}), bf16[32,16,4096]{2,1,0:T(8,128)(2,1)}) %all-gather.5.cloned.1.call-update) | async-done | bytes 4194320 | tf_op jit(solution)/shard_map/all_gather | solution.py:133
  156.4 4.1 %fusion.6 = f32[32,16,256]{2,1,0:T(8,128)S(1)} fusion(bf16[32,16,4096]{2,1,0:T(8,128)(2,1)} %all-gather.5.cloned.1.call-done, bf16[1,4096,256]{2,1,0:T(8,128)(2,1)} %param.18), kind=kOutput, calls=%fused_computation.14 | convolution fusion | flops 1073741824 | bytes 6815744 | tf_op jit(solution)/shard_map/gmd,df->gmf/dot_general | solution.py:134
  160.5 9.3 %convolution_convert_fusion = bf16[32,16,4096]{2,1,0:T(8,128)(2,1)} fusion(bf16[1,256,4096]{2,1,0:T(8,128)(2,1)S(1)} %copy-done, bf16[32,16,4096]{2,1,0:T(8,128)(2,1)} %all-gather.5.cloned.1.call-done, bf16[1,4096,256]{2,1,0:T(8,128)(2,1)} %param.19, f32[32,16,256]{2,1,0:T(8,128)S(1)} %fusion.6), kind=kOutput, calls=%fused_computation.5 | convolution fusion | flops 2150367232 | bytes 13107200 | tf_op jit(solution)/shard_map/gmf,fd->gmd/dot_general | solution.py:16
  170.3 0.1 reshape.452
  170.6 0.6 gather_fusion.1
  171.4 0.1 copy.81
  171.5 0.1 add.332
  171.7 1.7 gather_fusion
  173.4 0.2 select_reduce_fusion
  173.7 22.4 %reduce-scatter.6.cloned.1.call-done = bf16[32,16,512]{2,1,0:T(8,128)(2,1)} async-done(((bf16[32,16,4096]{2,1,0:T(8,128)(2,1)}), bf16[32,16,512]{2,1,0:T(8,128)(2,1)}) %reduce-scatter.6.cloned.1.call-update) | async-done | bytes 524304 | tf_op jit(solution)/shard_map/reduce_scatter | solution.py:17
  196.1 9.4 %all-to-all-start.1 = ((bf16[32,16,512]{2,1,0:T(8,128)(2,1)}), bf16[32,16,512]{2,1,0:T(8,128)(2,1)S(1)}, u32[]{:S(2)}, u32[]{:S(2)}) async-start(bf16[32,16,512]{2,1,0:T(8,128)(2,1)} %reduce-scatter.6.cloned.1.call-done), calls=%async_computation.3 | async-start | bytes 1048576 | tf_op jit(solution)/shard_map/all_to_all | solution.py:20
  205.5 0.1 copy.79
  205.6 0.2 convert_reduce_fusion.2
  205.9 32.4 %reduce-scatter.8.cloned.1.call-done = bf16[32,16,512]{2,1,0:T(8,128)(2,1)} async-done(((bf16[32,16,4096]{2,1,0:T(8,128)(2,1)}), bf16[32,16,512]{2,1,0:T(8,128)(2,1)}) %reduce-scatter.8.cloned.1.call-update) | async-done | bytes 524304 | tf_op jit(solution)/shard_map/reduce_scatter | solution.py:17
  238.3 9.4 %all-to-all-start.3 = ((bf16[32,16,512]{2,1,0:T(8,128)(2,1)}), bf16[32,16,512]{2,1,0:T(8,128)(2,1)}, u32[]{:S(2)}, u32[]{:S(2)}) async-start(bf16[32,16,512]{2,1,0:T(8,128)(2,1)} %reduce-scatter.8.cloned.1.call-done), calls=%async_computation.6 | async-start | bytes 1048576 | tf_op jit(solution)/shard_map/all_to_all | solution.py:20
  247.7 0.2 fusion.58
  248.3 11.0 %all-to-all-done.3 = bf16[32,16,512]{2,1,0:T(8,128)(2,1)} async-done(((bf16[32,16,512]{2,1,0:T(8,128)(2,1)}), bf16[32,16,512]{2,1,0:T(8,128)(2,1)}, u32[]{:S(2)}, u32[]{:S(2)}) %all-to-all-start.3) | async-done | bytes 524320 | tf_op jit(solution)/shard_map/all_to_all | solution.py:20
  259.3 1.3 pad_maximum_fusion
  260.6 2.6 gather_fusion.3
  263.2 1.2 gather.26
  264.4 0.9 convert_reduce_fusion
  265.3 0.4 multiply_reduce_fusion
  265.8 9.4 %all_gather.11 = bf16[256,512]{1,0:T(8,128)(2,1)S(1)} all-gather(bf16[64,512]{1,0:T(8,128)(2,1)S(1)} %fusion.54), channel_id=1, replica_groups=mesh['ex'=4,'ez'=8,'tensor'=8] {'ex'}, dimensions={0}, use_global_device_ids=true | all-gather | bytes 327680 | tf_op jit(solution)/shard_map/all_gather | solution.py:40
  275.1 1.1 convolution_convert_fusion.4
  276.2 5.1 %all-to-all-start.4 = ((bf16[8,64,512]{2,1,0:T(8,128)(2,1)}), bf16[8,64,512]{2,1,0:T(8,128)(2,1)S(1)}, u32[]{:S(2)}, u32[]{:S(2)}) async-start(bf16[8,64,512]{2,1,0:T(8,128)(2,1)} %convolution_convert_fusion.4), calls=%async_computation.7 | async-start | bytes 1048576 | tf_op jit(solution)/shard_map/all_to_all | solution.py:60
  281.3 0.3 convert_reduce_fusion.1
  281.7 11.8 %all-to-all-done.4 = bf16[8,64,512]{2,1,0:T(8,128)(2,1)S(1)} async-done(((bf16[8,64,512]{2,1,0:T(8,128)(2,1)}), bf16[8,64,512]{2,1,0:T(8,128)(2,1)S(1)}, u32[]{:S(2)}, u32[]{:S(2)}) %all-to-all-start.4) | async-done | bytes 524320 | tf_op jit(solution)/shard_map/all_to_all | solution.py:60
  293.5 0.7 gather_fusion.4
  294.2 0.2 fusion.50
  294.3 23.5 %psum.23 = f32[64]{0:T(128)S(1)} all-reduce(f32[64]{0:T(128)S(1)} %get-tuple-element.4), channel_id=1, replica_groups=mesh['ex'=4,'ez'=8,'tensor'=8] {'tensor'}, use_global_device_ids=true, to_apply=%region_17.18 | all-reduce | flops 64 | bytes 512 | tf_op jit(solution)/shard_map/psum | solution.py:25
  317.9 0.7 fusion.52
  (75 shorter events, 2.0 us)
Async XLA Ops:
  7.2 116.9 %copy-start = (bf16[1,256,4096]{2,1,0:T(8,128)(2,1)S(1)}, bf16[1,256,4096]{2,1,0:T(8,128)(2,1)}, u32[]{:S(2)}) copy-start(bf16[1,256,4096]{2,1,0:T(8,128)(2,1)} %param.20) | copy-start | bytes 6291460
  7.2 4.1 %copy-start.7 = (s32[64,2]{0,1:T(2,128)S(1)}, s32[64,2]{0,1:T(2,128)}, u32[]{:S(2)}) copy-start(s32[64,2]{0,1:T(2,128)} %param.17) | copy-start | bytes 1540
  7.2 39.6 %reduce-scatter.4.cloned.1.call-start = ((), (), s32[]{:S(2)}) async-start(), calls=%async_computation.8 | async-start | bytes 589824 | tf_op jit(solution)/shard_map/reduce_scatter | solution.py:93
  11.2 2.3 copy-start.9
  11.2 35.6 %copy-start.3 = (bf16[64,512]{1,0:T(8,128)(2,1)S(1)}, bf16[64,512]{1,0:T(8,128)(2,1)}, u32[]{:S(2)}) copy-start(bf16[64,512]{1,0:T(8,128)(2,1)} %param.13) | copy-start | bytes 196612
  11.2 36.6 %copy-start.5 = (f32[512,8]{0,1:T(8,128)S(1)}, f32[512,8]{0,1:T(8,128)}, u32[]{:S(2)}) copy-start(f32[512,8]{0,1:T(8,128)} %param.16) | copy-start | bytes 49156
  11.2 36.6 %copy-start.6 = (f32[512]{0:T(512)S(1)}, f32[512]{0:T(512)}, u32[]{:S(2)}) copy-start(f32[512]{0:T(512)} %param.15) | copy-start | bytes 6148
  11.3 108.6 %all-gather.3.cloned.1.call-start = ((), (), s32[]{:S(2)}) async-start(), calls=%async_computation.9 | async-start | bytes 4718592 | tf_op jit(solution)/shard_map/all_gather | solution.py:133
  86.9 69.4 %all-gather.5.cloned.1.call-start = ((), (), s32[]{:S(2)}) async-start(), calls=%async_computation.11 | async-start | bytes 4718592 | tf_op jit(solution)/shard_map/all_gather | solution.py:133
  108.5 87.6 %reduce-scatter.6.cloned.1.call-start = ((), (), s32[]{:S(2)}) async-start(), calls=%async_computation.10 | async-start | bytes 4718592 | tf_op jit(solution)/shard_map/reduce_scatter | solution.py:17
  133.4 104.9 %reduce-scatter.8.cloned.1.call-start = ((), (), s32[]{:S(2)}) async-start(), calls=%async_computation.12 | async-start | bytes 4718592 | tf_op jit(solution)/shard_map/reduce_scatter | solution.py:17
  169.8 1.9 copy-start.4
  196.1 42.2 %all-to-all-start.1 = ((bf16[32,16,512]{2,1,0:T(8,128)(2,1)}), bf16[32,16,512]{2,1,0:T(8,128)(2,1)S(1)}, u32[]{:S(2)}, u32[]{:S(2)}) async-start(bf16[32,16,512]{2,1,0:T(8,128)(2,1)} %reduce-scatter.6.cloned.1.call-done), calls=%async_computation.3 | async-start | bytes 1048576 | tf_op jit(solution)/shard_map/all_to_all | solution.py:20
  238.2 10.1 %copy-start.1 = (bf16[32,16,512]{2,1,0:T(8,128)(2,1)}, bf16[32,16,512]{2,1,0:T(8,128)(2,1)S(1)}, u32[]{:S(2)}) copy-start(bf16[32,16,512]{2,1,0:T(8,128)(2,1)S(1)} %all-to-all-done.1) | copy-start | bytes 1572868
  238.3 21.1 %all-to-all-start.3 = ((bf16[32,16,512]{2,1,0:T(8,128)(2,1)}), bf16[32,16,512]{2,1,0:T(8,128)(2,1)}, u32[]{:S(2)}, u32[]{:S(2)}) async-start(bf16[32,16,512]{2,1,0:T(8,128)(2,1)} %reduce-scatter.8.cloned.1.call-done), calls=%async_computation.6 | async-start | bytes 1048576 | tf_op jit(solution)/shard_map/all_to_all | solution.py:20
  264.4 53.5 %copy-start.8 = (f32[512]{0:T(512)S(1)}, f32[512]{0:T(512)}, u32[]{:S(2)}) copy-start(f32[512]{0:T(512)} %param.22) | copy-start | bytes 6148
  276.2 17.2 %all-to-all-start.4 = ((bf16[8,64,512]{2,1,0:T(8,128)(2,1)}), bf16[8,64,512]{2,1,0:T(8,128)(2,1)S(1)}, u32[]{:S(2)}, u32[]{:S(2)}) async-start(bf16[8,64,512]{2,1,0:T(8,128)(2,1)} %convolution_convert_fusion.4), calls=%async_computation.7 | async-start | bytes 1048576 | tf_op jit(solution)/shard_map/all_to_all | solution.py:60
  294.3 24.3 %copy-start.2 = (bf16[64,512]{1,0:T(8,128)(2,1)}, bf16[64,512]{1,0:T(8,128)(2,1)S(1)}, u32[]{:S(2)}) copy-start(bf16[64,512]{1,0:T(8,128)(2,1)S(1)} %get-tuple-element.5) | copy-start | bytes 196612
Sparse Core Ops, SparseCore 0:
  11.4 35.4 reduce-scatter.3
  87.0 32.8 all-gather.2
  121.7 34.5 all-gather.4
  158.8 37.2 reduce-scatter.5
  198.5 39.7 reduce-scatter.7

commit v4 on v2

--- a/solution.py
+++ b/solution.py
@@ -89,9 +89,13 @@
     expert_count = router_weight.shape[1]
     slab_count = groups // expert_count
     partial_proj = jnp.dot(attn_vals, out_weight, preferred_element_type=jnp.float32)
-    project = lax.psum_scatter(
-        partial_proj.astype(jnp.bfloat16), "tensor", scatter_dimension=1, tiled=True
-    ).astype(jnp.float32)
+    tensor_count = lax.axis_size("tensor")
+    width = partial_proj.shape[1] // tensor_count
+    pieces = partial_proj.astype(jnp.bfloat16).reshape(row_count, tensor_count, width)
+    received = lax.all_to_all(
+        pieces.transpose(1, 0, 2), "tensor", split_axis=0, concat_axis=0, tiled=True
+    )
+    project = jnp.sum(received.astype(jnp.float32), axis=0)
     stream_in = (residual.astype(jnp.float32) + project).astype(jnp.bfloat16)
     hidden_f = stream_in.astype(jnp.float32)
     scaled = hidden_f * norm_gain

time: 323 us -> 302 us (0.935)
  waiting for transfers between devices: 170 us -> 143 us
  starting transfers between devices: 15.4 us -> 21.9 us
    reduce_scatter x1 -> x0, waiting for transfers between devices: 32.7 us -> none  [on_device(): lax.psum_scatter(partial_proj.astype(jnp.bfloat16), 'tensor', scatter_dim...]
    all_to_all x0 -> x1, starting transfers between devices: none -> 6.59 us  [on_device(): lax.all_to_all(pieces.transpose(1, 0, 2), 'tensor', split_axis=0, concat_...]
    all_to_all x0 -> x1, waiting for transfers between devices: none -> 6.52 us  [on_device(): lax.all_to_all(pieces.transpose(1, 0, 2), 'tensor', split_axis=0, concat_...]
  transfers between devices with their start and end apart: 5 -> 5, of which waited for: 5 -> 5; matrix products, arithmetic and copies ran while one was open for 2% -> 3% of each run, Pallas kernels for 0% -> 0%
where the time goes in v4:
time: 302 us; the launch traced here: 301 us
  waiting for transfers between devices  143 us (47%)
  blocking collectives  76.3 us (25%)
  matrix products  29.8 us (10%)
  starting transfers between devices  21.9 us (7%)
  between operations  14.4 us (5%)
  local copies, waits for them, and re-layouts  10 us (3%)
  other arithmetic  5.32 us (2%)
    all_gather x1, waiting for transfers between devices, on_device(): arrived = lax.all_gather(arrived_part, 'tensor', axis=2, tiled=True)  50.6 us
    reduce_scatter x1, waiting for transfers between devices, finish_slots(): lax.psum_scatter(partial_out.astype(jnp.bfloat16), 'tensor', scatter_dime...  50.6 us
    all_to_all x1, blocking collectives, on_device(): lax.all_to_all(outgoing, EXPERT, split_axis=0, concat_axis=0, tiled=True)  35.4 us
    all_to_all x1, waiting for transfers between devices, finish_slots(): lax.all_to_all(summed, EXPERT, split_axis=0, concat_axis=0, tiled=True)  23.8 us
    psum x1, blocking collectives, final_norm(): square_total = lax.psum(jnp.sum(stream_f * stream_f, axis=1), 'tensor')  18.2 us
    dot_general x1, matrix products, finish_slots(): jnp.einsum('gmf,fd->gmd', active, down_weight, preferred_element_type=jnp...  17.1 us
    psum x1, blocking collectives, on_device(): lax.psum((jnp.sum(hidden_f * hidden_f, axis=1), jnp.dot(scaled, router_we...  13 us
    all_to_all x1, waiting for transfers between devices, restore(): lax.all_to_all(send, 'ez', split_axis=0, concat_axis=0, tiled=True)  11.7 us
  transfers between devices with their start and end apart: 5, of which 5 were waited for; matrix products, arithmetic and copies ran while one was open for 3% of the time, Pallas kernels for 0%

profile of v4, /device:TPU:1, one launch (start us, length us, event | category | flops | bytes accessed | tf_op | source)
XLA Modules:
  0.0 301.0 jit_solution(15672379183812724691)
XLA Ops:
  7.2 3.2 %convolution_convert_fusion.1 = bf16[64,4096]{1,0:T(8,128)(2,1)S(1)} fusion(bf16[64,512]{1,0:T(8,128)(2,1)} %param.12, bf16[512,4096]{1,0:T(8,128)(2,1)} %param.14), kind=kOutput, calls=%fused_computation.6 | convolution fusion | flops 268697600 | bytes 4784128 | tf_op jit(solution)/shard_map/dot_general | solution.py:91
  10.4 0.8 copy.95
  11.3 6.6 %all-to-all-start = ((bf16[8,64,512]{2,1,0:T(8,128)(2,1)}), bf16[8,64,512]{2,1,0:T(8,128)(2,1)S(1)}, u32[]{:S(2)}, u32[]{:S(2)}) async-start(bf16[8,64,512]{2,1,0:T(8,128)(2,1)} %bitcast.60), calls=%async_computation | async-start | bytes 1048576 | tf_op jit(solution)/shard_map/all_to_all | solution.py:95
  17.9 0.1 copy.78
  18.0 0.2 convert_reduce_fusion.4
  18.1 0.1 reduce_window_sum.11
  18.3 1.2 select_reduce_fusion.1
  19.5 0.4 fusion.13
  19.9 0.1 copy.87
  20.1 0.6 gather_fusion.2
  20.7 6.5 %all-to-all-done = bf16[8,64,512]{2,1,0:T(8,128)(2,1)S(1)} async-done(((bf16[8,64,512]{2,1,0:T(8,128)(2,1)}), bf16[8,64,512]{2,1,0:T(8,128)(2,1)S(1)}, u32[]{:S(2)}, u32[]{:S(2)}) %all-to-all-start) | async-done | bytes 524320 | tf_op jit(solution)/shard_map/all_to_all | solution.py:95
  27.3 0.1 fusion.34
  27.5 0.2 fusion.29
  27.6 13.0 %all-reduce = (f32[64]{0:T(128)S(1)}, f32[64,8]{0,1:T(8,128)S(1)}) all-reduce(f32[64]{0:T(128)S(1)} %get-tuple-element.14, f32[64,8]{0,1:T(8,128)S(1)} %fusion.29), channel_id=1, replica_groups=mesh['ex'=4,'ez'=8,'tensor'=8] {'tensor'}, use_global_device_ids=true, to_apply=%region_6.0 | all-reduce | flops 576 | bytes 4608 | tf_op jit(solution)/shard_map/psum | solution.py:102
  40.6 0.5 convolution_convert_fusion.2
  41.1 35.4 %all_to_all.20 = bf16[32,32,512]{2,1,0:T(8,128)(2,1)} all-to-all(bf16[32,32,512]{2,1,0:T(8,128)(2,1)S(1)} %convolution_convert_fusion.2), channel_id=1, replica_groups=mesh['ex'=4,'ez'=8,'tensor'=8] {'ex','ez'}, dimensions={0} | all-to-all | bytes 2097152 | tf_op jit(solution)/shard_map/all_to_all | solution.py:131
  76.6 50.6 %all-gather.2.cloned.1.call-done = bf16[32,32,4096]{2,1,0:T(8,128)(2,1)} async-done(((bf16[32,32,512]{2,1,0:T(8,128)(2,1)}), bf16[32,32,4096]{2,1,0:T(8,128)(2,1)}) %all-gather.2.cloned.1.call-update) | async-done | bytes 8388624 | tf_op jit(solution)/shard_map/all_gather | solution.py:132
  127.2 7.3 %fusion.3 = f32[32,32,256]{2,1,0:T(8,128)} fusion(bf16[32,32,4096]{2,1,0:T(8,128)(2,1)} %all-gather.2.cloned.1.call-done, bf16[1,4096,256]{2,1,0:T(8,128)(2,1)} %param.18), kind=kOutput, calls=%fused_computation.10 | convolution fusion | flops 2147483648 | bytes 11534336 | tf_op jit(solution)/shard_map/gmd,df->gmf/dot_general | solution.py:133
  134.5 17.1 %convolution_convert_fusion = bf16[32,32,4096]{2,1,0:T(8,128)(2,1)} fusion(bf16[1,256,4096]{2,1,0:T(8,128)(2,1)S(1)} %copy-done, bf16[32,32,4096]{2,1,0:T(8,128)(2,1)} %all-gather.2.cloned.1.call-done, bf16[1,4096,256]{2,1,0:T(8,128)(2,1)} %param.19, f32[32,32,256]{2,1,0:T(8,128)} %fusion.3), kind=kOutput, calls=%fused_computation.5 | convolution fusion | flops 4300734464 | bytes 22020096 | tf_op jit(solution)/shard_map/gmf,fd->gmd/dot_general | solution.py:15
  152.0 0.1 copy.83
  152.1 0.1 reshape.456
  152.2 0.1 select_reduce_fusion.2
  152.4 0.6 gather_fusion.1
  153.1 0.1 copy.84
  153.2 0.1 copy.88
  153.3 0.1 add.324
  153.4 0.1 copy.86
  153.7 1.7 gather_fusion
  155.4 50.6 %reduce-scatter.2.cloned.1.call-done = bf16[32,32,512]{2,1,0:T(8,128)(2,1)} async-done(((bf16[32,32,4096]{2,1,0:T(8,128)(2,1)}), bf16[32,32,512]{2,1,0:T(8,128)(2,1)}) %reduce-scatter.2.cloned.1.call-update) | async-done | bytes 1048592 | tf_op jit(solution)/shard_map/reduce_scatter | solution.py:16
  206.0 9.7 %all-to-all-start.2 = ((bf16[32,32,512]{2,1,0:T(8,128)(2,1)}), bf16[32,32,512]{2,1,0:T(8,128)(2,1)S(1)}, u32[]{:S(2)}, u32[]{:S(2)}) async-start(bf16[32,32,512]{2,1,0:T(8,128)(2,1)} %reduce-scatter.2.cloned.1.call-done), calls=%async_computation.3 | async-start | bytes 2097152 | tf_op jit(solution)/shard_map/all_to_all | solution.py:19
  215.8 0.2 convert_reduce_fusion.3
  216.0 0.2 select_reduce_fusion
  216.3 0.2 fusion.39
  216.8 0.1 copy.82
  216.9 23.8 %all-to-all-done.2 = bf16[32,32,512]{2,1,0:T(8,128)(2,1)S(1)} async-done(((bf16[32,32,512]{2,1,0:T(8,128)(2,1)}), bf16[32,32,512]{2,1,0:T(8,128)(2,1)S(1)}, u32[]{:S(2)}, u32[]{:S(2)}) %all-to-all-start.2) | async-done | bytes 1048608 | tf_op jit(solution)/shard_map/all_to_all | solution.py:19
  240.8 2.6 gather_fusion.3
  243.4 1.2 gather.26
  244.6 0.9 convert_reduce_fusion
  245.5 0.4 multiply_reduce_fusion
  245.9 9.7 %all_gather.7 = bf16[256,512]{1,0:T(8,128)(2,1)S(1)} all-gather(bf16[64,512]{1,0:T(8,128)(2,1)S(1)} %fusion.35), channel_id=1, replica_groups=mesh['ex'=4,'ez'=8,'tensor'=8] {'ex'}, dimensions={0}, use_global_device_ids=true | all-gather | bytes 327680 | tf_op jit(solution)/shard_map/all_gather | solution.py:39
  255.6 1.1 convolution_convert_fusion.3
  256.8 5.5 %all-to-all-start.3 = ((bf16[8,64,512]{2,1,0:T(8,128)(2,1)}), bf16[8,64,512]{2,1,0:T(8,128)(2,1)S(1)}, u32[]{:S(2)}, u32[]{:S(2)}) async-start(bf16[8,64,512]{2,1,0:T(8,128)(2,1)} %convolution_convert_fusion.3), calls=%async_computation.4 | async-start | bytes 1048576 | tf_op jit(solution)/shard_map/all_to_all | solution.py:59
  262.3 0.3 convert_reduce_fusion.2
  262.7 11.7 %all-to-all-done.3 = bf16[8,64,512]{2,1,0:T(8,128)(2,1)S(1)} async-done(((bf16[8,64,512]{2,1,0:T(8,128)(2,1)}), bf16[8,64,512]{2,1,0:T(8,128)(2,1)S(1)}, u32[]{:S(2)}, u32[]{:S(2)}) %all-to-all-start.3) | async-done | bytes 524320 | tf_op jit(solution)/shard_map/all_to_all | solution.py:59
  274.4 0.7 gather_fusion.4
  275.1 0.2 fusion.31
  275.3 18.2 %psum.23 = f32[64]{0:T(128)S(1)} all-reduce(f32[64]{0:T(128)S(1)} %get-tuple-element.4), channel_id=1, replica_groups=mesh['ex'=4,'ez'=8,'tensor'=8] {'tensor'}, use_global_device_ids=true, to_apply=%region_16.17 | all-reduce | flops 64 | bytes 512 | tf_op jit(solution)/shard_map/psum | solution.py:24
  293.5 0.7 fusion.33
  (61 shorter events, 1.2 us)
Async XLA Ops:
  7.2 127.4 %copy-start = (bf16[1,256,4096]{2,1,0:T(8,128)(2,1)S(1)}, bf16[1,256,4096]{2,1,0:T(8,128)(2,1)}, u32[]{:S(2)}) copy-start(bf16[1,256,4096]{2,1,0:T(8,128)(2,1)} %param.20) | copy-start | bytes 6291460
  7.2 10.7 %copy-start.6 = (s32[64,2]{0,1:T(2,128)S(1)}, s32[64,2]{0,1:T(2,128)}, u32[]{:S(2)}) copy-start(s32[64,2]{0,1:T(2,128)} %param.17) | copy-start | bytes 1540
  7.2 12.9 %copy-start.8 = (s32[32]{0:T(128)S(1)}, s32[32]{0:T(128)}, u32[]{:S(2)}) copy-start(s32[32]{0:T(128)} %param.21) | copy-start | bytes 388
  7.2 20.1 %copy-start.2 = (bf16[64,512]{1,0:T(8,128)(2,1)S(1)}, bf16[64,512]{1,0:T(8,128)(2,1)}, u32[]{:S(2)}) copy-start(bf16[64,512]{1,0:T(8,128)(2,1)} %param.13) | copy-start | bytes 196612
  7.2 20.2 %copy-start.5 = (f32[512]{0:T(512)S(1)}, f32[512]{0:T(512)}, u32[]{:S(2)}) copy-start(f32[512]{0:T(512)} %param.15) | copy-start | bytes 6148
  7.2 20.2 %copy-start.4 = (f32[512,8]{0,1:T(8,128)S(1)}, f32[512,8]{0,1:T(8,128)}, u32[]{:S(2)}) copy-start(f32[512,8]{0,1:T(8,128)} %param.16) | copy-start | bytes 49156
  11.3 16.0 %all-to-all-start = ((bf16[8,64,512]{2,1,0:T(8,128)(2,1)}), bf16[8,64,512]{2,1,0:T(8,128)(2,1)S(1)}, u32[]{:S(2)}, u32[]{:S(2)}) async-start(bf16[8,64,512]{2,1,0:T(8,128)(2,1)} %bitcast.60), calls=%async_computation | async-start | bytes 1048576 | tf_op jit(solution)/shard_map/all_to_all | solution.py:95
  17.9 109.4 %all-gather.2.cloned.1.call-start = ((), (), s32[]{:S(2)}) async-start(), calls=%async_computation.5 | async-start | bytes 9437184 | tf_op jit(solution)/shard_map/all_gather | solution.py:132
  76.6 129.5 %reduce-scatter.2.cloned.1.call-start = ((), (), s32[]{:S(2)}) async-start(), calls=%async_computation.6 | async-start | bytes 9437184 | tf_op jit(solution)/shard_map/reduce_scatter | solution.py:16
  151.6 2.0 copy-start.3
  206.0 34.7 %all-to-all-start.2 = ((bf16[32,32,512]{2,1,0:T(8,128)(2,1)}), bf16[32,32,512]{2,1,0:T(8,128)(2,1)S(1)}, u32[]{:S(2)}, u32[]{:S(2)}) async-start(bf16[32,32,512]{2,1,0:T(8,128)(2,1)} %reduce-scatter.2.cloned.1.call-done), calls=%async_computation.3 | async-start | bytes 2097152 | tf_op jit(solution)/shard_map/all_to_all | solution.py:19
  240.8 52.7 %copy-start.7 = (f32[512]{0:T(512)S(1)}, f32[512]{0:T(512)}, u32[]{:S(2)}) copy-start(f32[512]{0:T(512)} %param.22) | copy-start | bytes 6148
  256.8 17.6 %all-to-all-start.3 = ((bf16[8,64,512]{2,1,0:T(8,128)(2,1)}), bf16[8,64,512]{2,1,0:T(8,128)(2,1)S(1)}, u32[]{:S(2)}, u32[]{:S(2)}) async-start(bf16[8,64,512]{2,1,0:T(8,128)(2,1)} %convolution_convert_fusion.3), calls=%async_computation.4 | async-start | bytes 1048576 | tf_op jit(solution)/shard_map/all_to_all | solution.py:59
  275.2 18.9 %copy-start.1 = (bf16[64,512]{1,0:T(8,128)(2,1)}, bf16[64,512]{1,0:T(8,128)(2,1)S(1)}, u32[]{:S(2)}) copy-start(bf16[64,512]{1,0:T(8,128)(2,1)S(1)} %get-tuple-element.5) | copy-start | bytes 196612
Sparse Core Ops, SparseCore 0:
  76.7 50.5 all-gather.1
  151.8 54.2 reduce-scatter.1

commit v5 on v4

--- a/solution.py
+++ b/solution.py
@@ -107,7 +107,6 @@
         "tensor",
     )
     inverse_rms = lax.rsqrt(square_sum / D + EPS)
-    normed_in = (scaled * inverse_rms[:, None]).astype(jnp.bfloat16)
     logits = logit_part * inverse_rms[:, None]
     expert_ids = jnp.arange(expert_count, dtype=jnp.int32)
     route_hot = (routes[:, :, None] == expert_ids[None, None, :]).astype(jnp.int32)
@@ -126,10 +125,13 @@
     target_expert = slab_of // slab_count
     send_map = jnp.take(placing, target_expert, axis=0)
     outgoing = jnp.einsum(
-        "gsr,rd->gsd", send_map, normed_in, preferred_element_type=jnp.float32
+        "gsr,rd->gsd", send_map, stream_in, preferred_element_type=jnp.float32
     ).astype(jnp.bfloat16)
     arrived_part = lax.all_to_all(outgoing, EXPERT, split_axis=0, concat_axis=0, tiled=True)
-    arrived = lax.all_gather(arrived_part, "tensor", axis=2, tiled=True)
+    arrived_rows = lax.all_gather(arrived_part, "tensor", axis=2, tiled=True).astype(jnp.float32)
+    gain_full = lax.all_gather(norm_gain, "tensor", axis=0, tiled=True)
+    slot_rms = lax.rsqrt(jnp.sum(arrived_rows * arrived_rows, axis=2) / D + EPS)
+    arrived = (arrived_rows * gain_full * slot_rms[:, :, None]).astype(jnp.bfloat16)
     gate_val = jnp.einsum("gmd,df->gmf", arrived, w_gate[0], preferred_element_type=jnp.float32)
     up_val = jnp.einsum("gmd,df->gmf", arrived, w_up[0], preferred_element_type=jnp.float32)
     returned = finish_slots(gate_val, up_val, w_down[0])

time: 302 us -> 293 us (0.970)
  waiting for transfers between devices: 143 us -> 113 us
  blocking collectives: 76.3 us -> 93.3 us
  other arithmetic: 5.32 us -> 10.6 us
    all_gather x0 -> x1, blocking collectives: none -> 15.9 us  [on_device(): gain_full = lax.all_gather(norm_gain, 'tensor', axis=0, tiled=True)]
    all_gather x1, waiting for transfers between devices: 50.6 us -> 35.3 us  [on_device(): lax.all_gather(arrived_part, 'tensor', axis=2, tiled=True)]
    all_to_all x1, waiting for transfers between devices: 23.8 us -> 10.2 us  [finish_slots(): lax.all_to_all(summed, EXPERT, split_axis=0, concat_axis=0, tiled=True)]
    reduce_sum x0 -> x1, other arithmetic: none -> 5.23 us  [on_device(): slot_rms = lax.rsqrt(jnp.sum(arrived_rows * arrived_rows, axis=2) / D + EPS)]
where the time goes in v5:
time: 293 us; the launch traced here: 292 us
  waiting for transfers between devices  113 us (39%)
  blocking collectives  93.3 us (32%)
  matrix products  27.7 us (9%)
  starting transfers between devices  21.7 us (7%)
  between operations  14.4 us (5%)
  local copies, waits for them, and re-layouts  11.5 us (4%)
  other arithmetic  10.6 us (4%)
    reduce_scatter x1, waiting for transfers between devices, finish_slots(): lax.psum_scatter(partial_out.astype(jnp.bfloat16), 'tensor', scatter_dime...  49.9 us
    all_to_all x1, blocking collectives, on_device(): lax.all_to_all(outgoing, EXPERT, split_axis=0, concat_axis=0, tiled=True)  35.4 us
    all_gather x1, waiting for transfers between devices, on_device(): lax.all_gather(arrived_part, 'tensor', axis=2, tiled=True)  35.3 us
    psum x1, blocking collectives, final_norm(): square_total = lax.psum(jnp.sum(stream_f * stream_f, axis=1), 'tensor')  18.2 us
    dot_general x1, matrix products, finish_slots(): jnp.einsum('gmf,fd->gmd', active, down_weight, preferred_element_type=jnp...  17.2 us
    all_gather x1, blocking collectives, on_device(): gain_full = lax.all_gather(norm_gain, 'tensor', axis=0, tiled=True)  15.9 us
    psum x1, blocking collectives, on_device(): lax.psum((jnp.sum(hidden_f * hidden_f, axis=1), jnp.dot(scaled, router_we...  14 us
    all_to_all x1, waiting for transfers between devices, restore(): lax.all_to_all(send, 'ez', split_axis=0, concat_axis=0, tiled=True)  11.7 us
  transfers between devices with their start and end apart: 5, of which 5 were waited for; matrix products, arithmetic and copies ran while one was open for 3% of the time, Pallas kernels for 0%

profile of v5, /device:TPU:1, one launch (start us, length us, event | category | flops | bytes accessed | tf_op | source)
XLA Modules:
  0.0 292.1 jit_solution(2725675425420136036)
XLA Ops:
  7.2 3.2 %convolution_convert_fusion.1 = bf16[64,4096]{1,0:T(8,128)(2,1)S(1)} fusion(bf16[64,512]{1,0:T(8,128)(2,1)} %param.12, bf16[512,4096]{1,0:T(8,128)(2,1)} %param.14), kind=kOutput, calls=%fused_computation.13 | convolution fusion | flops 268697600 | bytes 4784128 | tf_op jit(solution)/shard_map/dot_general | solution.py:91
  10.4 0.8 copy.95
  11.3 6.6 %all-to-all-start = ((bf16[8,64,512]{2,1,0:T(8,128)(2,1)}), bf16[8,64,512]{2,1,0:T(8,128)(2,1)S(1)}, u32[]{:S(2)}, u32[]{:S(2)}) async-start(bf16[8,64,512]{2,1,0:T(8,128)(2,1)} %bitcast.60), calls=%async_computation | async-start | bytes 1048576 | tf_op jit(solution)/shard_map/all_to_all | solution.py:95
  17.9 0.8 copy.78
  18.6 0.2 convert_reduce_fusion.4
  18.9 1.2 select_reduce_fusion.1
  20.1 0.4 fusion.24
  20.6 0.1 copy.87
  20.8 0.6 gather_fusion.2
  21.4 5.9 %all-to-all-done = bf16[8,64,512]{2,1,0:T(8,128)(2,1)S(1)} async-done(((bf16[8,64,512]{2,1,0:T(8,128)(2,1)}), bf16[8,64,512]{2,1,0:T(8,128)(2,1)S(1)}, u32[]{:S(2)}, u32[]{:S(2)}) %all-to-all-start) | async-done | bytes 524320 | tf_op jit(solution)/shard_map/all_to_all | solution.py:95
  27.3 0.1 fusion.43
  27.4 0.5 convolution_convert_fusion.2
  27.9 35.4 %all_to_all.20 = bf16[32,32,512]{2,1,0:T(8,128)(2,1)} all-to-all(bf16[32,32,512]{2,1,0:T(8,128)(2,1)S(1)} %convolution_convert_fusion.2), channel_id=1, replica_groups=mesh['ex'=4,'ez'=8,'tensor'=8] {'ex','ez'}, dimensions={0} | all-to-all | bytes 2097152 | tf_op jit(solution)/shard_map/all_to_all | solution.py:130
  63.4 15.9 %all-gather = f32[8,1,512]{2,1,0:T(1,128)S(1)} all-gather(f32[1,1,512]{2,1,0:T(1,128)S(1)} %bitcast.67), channel_id=1, replica_groups=mesh['ex'=4,'ez'=8,'tensor'=8] {'tensor'}, dimensions={0}, use_global_device_ids=true | all-gather | bytes 18432 | tf_op jit(solution)/shard_map/all_gather | solution.py:132
  79.3 35.3 %all-gather.3.cloned.1.call-done = bf16[32,32,4096]{2,1,0:T(8,128)(2,1)} async-done(((bf16[32,32,512]{2,1,0:T(8,128)(2,1)}), bf16[32,32,4096]{2,1,0:T(8,128)(2,1)}) %all-gather.3.cloned.1.call-update) | async-done | bytes 8388624 | tf_op jit(solution)/shard_map/all_gather | solution.py:131
  114.6 5.2 %fusion.2 = f32[32,32]{1,0:T(8,128)S(1)} fusion(bf16[32,32,4096]{2,1,0:T(8,128)(2,1)} %all-gather.3.cloned.1.call-done), kind=kLoop, calls=%fused_computation.9 | loop fusion | flops 12581888 | bytes 8392704 | tf_op jit(solution)/shard_map/reduce_sum | solution.py:133
  119.9 0.5 copy-done.1
  120.4 5.1 %fusion.5 = f32[32,32,256]{2,1,0:T(8,128)} fusion(bf16[32,32,4096]{2,1,0:T(8,128)(2,1)S(1)} %copy-done.1, f32[32,32]{1,0:T(8,128)S(1)} %add_rsqrt_fusion, f32[4096]{0:T(1024)S(1)} %bitcast.65, bf16[1,4096,256]{2,1,0:T(8,128)(2,1)} %param.18), kind=kOutput, calls=%fused_computation.12 | convolution fusion | flops 2164260864 | bytes 11554816 | tf_op jit(solution)/shard_map/gmd,df->gmf/dot_general | solution.py:135
  125.5 17.2 %convolution_convert_fusion = bf16[32,32,4096]{2,1,0:T(8,128)(2,1)} fusion(bf16[1,256,4096]{2,1,0:T(8,128)(2,1)S(1)} %copy-done, bf16[1,4096,256]{2,1,0:T(8,128)(2,1)} %param.19, bf16[32,32,4096]{2,1,0:T(8,128)(2,1)} %all-gather.3.cloned.1.call-done, f32[32,32]{1,0:T(8,128)S(1)} %add_rsqrt_fusion, f32[4096]{0:T(1024)S(1)} %bitcast.66, f32[32,32,256]{2,1,0:T(8,128)} %fusion.5), kind=kOutput, calls=%fused_computation.10 | convolution fusion | flops 4317511680 | bytes 22040576 | tf_op jit(solution)/shard_map/gmf,fd->gmd/dot_general | solution.py:15
  143.0 0.3 copy-done.7
  143.4 0.1 reshape.462
  143.6 0.1 select_reduce_fusion.2
  143.8 0.6 gather_fusion.1
  144.6 0.1 copy.88
  144.7 0.1 add.336
  144.8 0.1 copy.86
  145.0 1.7 gather_fusion
  146.8 0.2 convert_reduce_fusion.3
  147.0 0.2 select_reduce_fusion
  147.2 49.9 %reduce-scatter.2.cloned.1.call-done = bf16[32,32,512]{2,1,0:T(8,128)(2,1)} async-done(((bf16[32,32,4096]{2,1,0:T(8,128)(2,1)}), bf16[32,32,512]{2,1,0:T(8,128)(2,1)}) %reduce-scatter.2.cloned.1.call-update) | async-done | bytes 1048592 | tf_op jit(solution)/shard_map/reduce_scatter | solution.py:16
  197.1 9.5 %all-to-all-start.2 = ((bf16[32,32,512]{2,1,0:T(8,128)(2,1)}), bf16[32,32,512]{2,1,0:T(8,128)(2,1)S(1)}, u32[]{:S(2)}, u32[]{:S(2)}) async-start(bf16[32,32,512]{2,1,0:T(8,128)(2,1)} %reduce-scatter.2.cloned.1.call-done), calls=%async_computation.3 | async-start | bytes 2097152 | tf_op jit(solution)/shard_map/all_to_all | solution.py:19
  206.7 0.2 fusion.42
  206.9 14.0 %all-reduce = (f32[64,8]{0,1:T(8,128)S(1)}, f32[64]{0:T(128)S(1)}) all-reduce(f32[64,8]{0,1:T(8,128)S(1)} %fusion.42, f32[64]{0:T(128)S(1)} %get-tuple-element.12), channel_id=1, replica_groups=mesh['ex'=4,'ez'=8,'tensor'=8] {'tensor'}, use_global_device_ids=true, to_apply=%region_4.0 | all-reduce | flops 576 | bytes 4608 | tf_op jit(solution)/shard_map/psum | solution.py:102
  221.0 0.2 fusion.48
  221.6 10.2 %all-to-all-done.2 = bf16[32,32,512]{2,1,0:T(8,128)(2,1)S(1)} async-done(((bf16[32,32,512]{2,1,0:T(8,128)(2,1)}), bf16[32,32,512]{2,1,0:T(8,128)(2,1)S(1)}, u32[]{:S(2)}, u32[]{:S(2)}) %all-to-all-start.2) | async-done | bytes 1048608 | tf_op jit(solution)/shard_map/all_to_all | solution.py:19
  231.8 2.6 gather_fusion.3
  234.4 1.2 gather.26
  235.6 0.9 convert_reduce_fusion
  236.5 0.4 multiply_reduce_fusion
  236.9 9.7 %all_gather.11 = bf16[256,512]{1,0:T(8,128)(2,1)S(1)} all-gather(bf16[64,512]{1,0:T(8,128)(2,1)S(1)} %fusion.44), channel_id=1, replica_groups=mesh['ex'=4,'ez'=8,'tensor'=8] {'ex'}, dimensions={0}, use_global_device_ids=true | all-gather | bytes 327680 | tf_op jit(solution)/shard_map/all_gather | solution.py:39
  246.7 1.1 convolution_convert_fusion.3
  247.8 5.5 %all-to-all-start.3 = ((bf16[8,64,512]{2,1,0:T(8,128)(2,1)}), bf16[8,64,512]{2,1,0:T(8,128)(2,1)S(1)}, u32[]{:S(2)}, u32[]{:S(2)}) async-start(bf16[8,64,512]{2,1,0:T(8,128)(2,1)} %convolution_convert_fusion.3), calls=%async_computation.4 | async-start | bytes 1048576 | tf_op jit(solution)/shard_map/all_to_all | solution.py:59
  253.4 0.3 convert_reduce_fusion.2
  253.7 11.7 %all-to-all-done.3 = bf16[8,64,512]{2,1,0:T(8,128)(2,1)S(1)} async-done(((bf16[8,64,512]{2,1,0:T(8,128)(2,1)}), bf16[8,64,512]{2,1,0:T(8,128)(2,1)S(1)}, u32[]{:S(2)}, u32[]{:S(2)}) %all-to-all-start.3) | async-done | bytes 524320 | tf_op jit(solution)/shard_map/all_to_all | solution.py:59
  265.4 0.7 gather_fusion.4
  266.1 0.2 fusion.39
  266.3 18.2 %psum.23 = f32[64]{0:T(128)S(1)} all-reduce(f32[64]{0:T(128)S(1)} %get-tuple-element.4), channel_id=1, replica_groups=mesh['ex'=4,'ez'=8,'tensor'=8] {'tensor'}, use_global_device_ids=true, to_apply=%region_17.18 | all-reduce | flops 64 | bytes 512 | tf_op jit(solution)/shard_map/psum | solution.py:24
  284.5 0.7 fusion.41
  (66 shorter events, 1.6 us)
Async XLA Ops:
  7.2 118.3 %copy-start = (bf16[1,256,4096]{2,1,0:T(8,128)(2,1)S(1)}, bf16[1,256,4096]{2,1,0:T(8,128)(2,1)}, u32[]{:S(2)}) copy-start(bf16[1,256,4096]{2,1,0:T(8,128)(2,1)} %param.20) | copy-start | bytes 6291460
  7.2 13.5 %copy-start.9 = (s32[32]{0:T(128)S(1)}, s32[32]{0:T(128)}, u32[]{:S(2)}) copy-start(s32[32]{0:T(128)} %param.21) | copy-start | bytes 388
  7.2 20.1 %copy-start.3 = (bf16[64,512]{1,0:T(8,128)(2,1)S(1)}, bf16[64,512]{1,0:T(8,128)(2,1)}, u32[]{:S(2)}) copy-start(bf16[64,512]{1,0:T(8,128)(2,1)} %param.13) | copy-start | bytes 196612
  7.2 56.2 %copy-start.6 = (f32[512]{0:T(512)S(1)}, f32[512]{0:T(512)}, u32[]{:S(2)}) copy-start(f32[512]{0:T(512)} %param.15) | copy-start | bytes 6148
  11.3 16.0 %all-to-all-start = ((bf16[8,64,512]{2,1,0:T(8,128)(2,1)}), bf16[8,64,512]{2,1,0:T(8,128)(2,1)S(1)}, u32[]{:S(2)}, u32[]{:S(2)}) async-start(bf16[8,64,512]{2,1,0:T(8,128)(2,1)} %bitcast.60), calls=%async_computation | async-start | bytes 1048576 | tf_op jit(solution)/shard_map/all_to_all | solution.py:95
  17.9 96.8 %all-gather.3.cloned.1.call-start = ((), (), s32[]{:S(2)}) async-start(), calls=%async_computation.5 | async-start | bytes 9437184 | tf_op jit(solution)/shard_map/all_gather | solution.py:131
  63.3 133.8 %reduce-scatter.2.cloned.1.call-start = ((), (), s32[]{:S(2)}) async-start(), calls=%async_computation.6 | async-start | bytes 9437184 | tf_op jit(solution)/shard_map/reduce_scatter | solution.py:16
  114.6 5.8 %copy-start.1 = (bf16[32,32,4096]{2,1,0:T(8,128)(2,1)S(1)}, bf16[32,32,4096]{2,1,0:T(8,128)(2,1)}, u32[]{:S(2)}) copy-start(bf16[32,32,4096]{2,1,0:T(8,128)(2,1)} %all-gather.3.cloned.1.call-done) | copy-start | bytes 25165828
  142.7 0.7 copy-start.7
  142.7 2.3 copy-start.4
  142.7 64.0 %copy-start.5 = (f32[512,8]{0,1:T(8,128)S(1)}, f32[512,8]{0,1:T(8,128)}, u32[]{:S(2)}) copy-start(f32[512,8]{0,1:T(8,128)} %param.16) | copy-start | bytes 49156
  142.7 141.8 %copy-start.8 = (f32[512]{0:T(512)S(1)}, f32[512]{0:T(512)}, u32[]{:S(2)}) copy-start(f32[512]{0:T(512)} %param.22) | copy-start | bytes 6148
  197.1 34.7 %all-to-all-start.2 = ((bf16[32,32,512]{2,1,0:T(8,128)(2,1)}), bf16[32,32,512]{2,1,0:T(8,128)(2,1)S(1)}, u32[]{:S(2)}, u32[]{:S(2)}) async-start(bf16[32,32,512]{2,1,0:T(8,128)(2,1)} %reduce-scatter.2.cloned.1.call-done), calls=%async_computation.3 | async-start | bytes 2097152 | tf_op jit(solution)/shard_map/all_to_all | solution.py:19
  247.8 17.6 %all-to-all-start.3 = ((bf16[8,64,512]{2,1,0:T(8,128)(2,1)}), bf16[8,64,512]{2,1,0:T(8,128)(2,1)S(1)}, u32[]{:S(2)}, u32[]{:S(2)}) async-start(bf16[8,64,512]{2,1,0:T(8,128)(2,1)} %convolution_convert_fusion.3), calls=%async_computation.4 | async-start | bytes 1048576 | tf_op jit(solution)/shard_map/all_to_all | solution.py:59
  266.3 19.0 %copy-start.2 = (bf16[64,512]{1,0:T(8,128)(2,1)}, bf16[64,512]{1,0:T(8,128)(2,1)S(1)}, u32[]{:S(2)}) copy-start(bf16[64,512]{1,0:T(8,128)(2,1)S(1)} %get-tuple-element.5) | copy-start | bytes 196612
Sparse Core Ops, SparseCore 0:
  63.4 51.1 all-gather.2
  142.8 54.2 reduce-scatter.1

commit v6 on v4

--- a/solution.py
+++ b/solution.py
@@ -107,7 +107,6 @@
         "tensor",
     )
     inverse_rms = lax.rsqrt(square_sum / D + EPS)
-    normed_in = (scaled * inverse_rms[:, None]).astype(jnp.bfloat16)
     logits = logit_part * inverse_rms[:, None]
     expert_ids = jnp.arange(expert_count, dtype=jnp.int32)
     route_hot = (routes[:, :, None] == expert_ids[None, None, :]).astype(jnp.int32)
@@ -126,12 +125,19 @@
     target_expert = slab_of // slab_count
     send_map = jnp.take(placing, target_expert, axis=0)
     outgoing = jnp.einsum(
-        "gsr,rd->gsd", send_map, normed_in, preferred_element_type=jnp.float32
+        "gsr,rd->gsd", send_map, stream_in, preferred_element_type=jnp.float32
     ).astype(jnp.bfloat16)
     arrived_part = lax.all_to_all(outgoing, EXPERT, split_axis=0, concat_axis=0, tiled=True)
     arrived = lax.all_gather(arrived_part, "tensor", axis=2, tiled=True)
-    gate_val = jnp.einsum("gmd,df->gmf", arrived, w_gate[0], preferred_element_type=jnp.float32)
-    up_val = jnp.einsum("gmd,df->gmf", arrived, w_up[0], preferred_element_type=jnp.float32)
+    arrived_f = arrived.astype(jnp.float32)
+    slot_rms = lax.rsqrt(jnp.sum(arrived_f * arrived_f, axis=2) / D + EPS)[:, :, None]
+    gain_full = lax.all_gather(norm_gain, "tensor", axis=0, tiled=True)[:, None]
+    gate_weight = (w_gate[0].astype(jnp.float32) * gain_full).astype(jnp.bfloat16)
+    up_weight = (w_up[0].astype(jnp.float32) * gain_full).astype(jnp.bfloat16)
+    gate_val = slot_rms * jnp.einsum(
+        "gmd,df->gmf", arrived, gate_weight, preferred_element_type=jnp.float32
+    )
+    up_val = slot_rms * jnp.einsum("gmd,df->gmf", arrived, up_weight, preferred_element_type=jnp.float32)
     returned = finish_slots(gate_val, up_val, w_down[0])
     group_ids = jnp.arange(groups, dtype=jnp.int32)
     holder_hot = (slab_of[None, :] == group_ids[:, None]).astype(jnp.int32)

time: 302 us -> 292 us (0.967)
  waiting for transfers between devices: 143 us -> 114 us
  blocking collectives: 76.3 us -> 93.1 us
  other arithmetic: 5.32 us -> 10.6 us
  matrix products: 29.8 us -> 26.7 us
    all_gather x0 -> x1, blocking collectives: none -> 15.9 us  [on_device(): gain_full = lax.all_gather(norm_gain, 'tensor', axis=0, tiled=True)[:, None]]
    all_gather x1, waiting for transfers between devices: 50.6 us -> 35.3 us  [on_device(): arrived = lax.all_gather(arrived_part, 'tensor', axis=2, tiled=True)]
    all_to_all x1, waiting for transfers between devices: 23.8 us -> 10.4 us  [finish_slots(): lax.all_to_all(summed, EXPERT, split_axis=0, concat_axis=0, tiled=True)]
    reduce_sum x0 -> x1, other arithmetic: none -> 5.23 us  [on_device(): jnp.sum(arrived_f * arrived_f, axis=2) / D + EPS]
where the time goes in v6:
time: 292 us; the launch traced here: 291 us
  waiting for transfers between devices  114 us (39%)
  blocking collectives  93.1 us (32%)
  matrix products  26.7 us (9%)
  starting transfers between devices  21.9 us (8%)
  between operations  14.4 us (5%)
  local copies, waits for them, and re-layouts  10.7 us (4%)
  other arithmetic  10.6 us (4%)
    reduce_scatter x1, waiting for transfers between devices, finish_slots(): lax.psum_scatter(partial_out.astype(jnp.bfloat16), 'tensor', scatter_dime...  50 us
    all_to_all x1, blocking collectives, on_device(): lax.all_to_all(outgoing, EXPERT, split_axis=0, concat_axis=0, tiled=True)  35.4 us
    all_gather x1, waiting for transfers between devices, on_device(): arrived = lax.all_gather(arrived_part, 'tensor', axis=2, tiled=True)  35.3 us
    psum x1, blocking collectives, final_norm(): square_total = lax.psum(jnp.sum(stream_f * stream_f, axis=1), 'tensor')  18.2 us
    dot_general x1, matrix products, finish_slots(): jnp.einsum('gmf,fd->gmd', active, down_weight, preferred_element_type=jnp...  16.2 us
    all_gather x1, blocking collectives, on_device(): gain_full = lax.all_gather(norm_gain, 'tensor', axis=0, tiled=True)[:, None]  15.9 us
    psum x1, blocking collectives, on_device(): lax.psum((jnp.sum(hidden_f * hidden_f, axis=1), jnp.dot(scaled, router_we...  13.8 us
    all_to_all x1, waiting for transfers between devices, restore(): lax.all_to_all(send, 'ez', split_axis=0, concat_axis=0, tiled=True)  11.7 us
  transfers between devices with their start and end apart: 5, of which 5 were waited for; matrix products, arithmetic and copies ran while one was open for 3% of the time, Pallas kernels for 0%

profile of v6, /device:TPU:1, one launch (start us, length us, event | category | flops | bytes accessed | tf_op | source)
XLA Modules:
  0.0 291.3 jit_solution(17338211660797892997)
XLA Ops:
  7.2 3.2 %convolution_convert_fusion.1 = bf16[64,4096]{1,0:T(8,128)(2,1)S(1)} fusion(bf16[64,512]{1,0:T(8,128)(2,1)} %param.12, bf16[512,4096]{1,0:T(8,128)(2,1)} %param.14), kind=kOutput, calls=%fused_computation.7 | convolution fusion | flops 268697600 | bytes 4784128 | tf_op jit(solution)/shard_map/dot_general | solution.py:91
  10.4 0.8 copy.95
  11.3 6.7 %all-to-all-start = ((bf16[8,64,512]{2,1,0:T(8,128)(2,1)}), bf16[8,64,512]{2,1,0:T(8,128)(2,1)S(1)}, u32[]{:S(2)}, u32[]{:S(2)}) async-start(bf16[8,64,512]{2,1,0:T(8,128)(2,1)} %bitcast.86), calls=%async_computation | async-start | bytes 1048576 | tf_op jit(solution)/shard_map/all_to_all | solution.py:95
  18.1 0.2 convert_reduce_fusion.4
  18.4 1.2 select_reduce_fusion.1
  19.6 0.4 fusion.27
  20.1 0.1 copy.87
  20.2 0.6 gather_fusion.2
  20.8 6.5 %all-to-all-done = bf16[8,64,512]{2,1,0:T(8,128)(2,1)S(1)} async-done(((bf16[8,64,512]{2,1,0:T(8,128)(2,1)}), bf16[8,64,512]{2,1,0:T(8,128)(2,1)S(1)}, u32[]{:S(2)}, u32[]{:S(2)}) %all-to-all-start) | async-done | bytes 524320 | tf_op jit(solution)/shard_map/all_to_all | solution.py:95
  27.5 0.1 fusion.47
  27.6 0.5 convolution_convert_fusion.2
  28.0 35.4 %all_to_all.20 = bf16[32,32,512]{2,1,0:T(8,128)(2,1)} all-to-all(bf16[32,32,512]{2,1,0:T(8,128)(2,1)S(1)} %convolution_convert_fusion.2), channel_id=1, replica_groups=mesh['ex'=4,'ez'=8,'tensor'=8] {'ex','ez'}, dimensions={0} | all-to-all | bytes 2097152 | tf_op jit(solution)/shard_map/all_to_all | solution.py:130
  63.5 15.9 %all-gather = f32[8,1,512]{2,1,0:T(1,128)S(1)} all-gather(f32[1,1,512]{2,1,0:T(1,128)S(1)} %bitcast.93), channel_id=1, replica_groups=mesh['ex'=4,'ez'=8,'tensor'=8] {'tensor'}, dimensions={0}, use_global_device_ids=true | all-gather | bytes 18432 | tf_op jit(solution)/shard_map/all_gather | solution.py:134
  79.4 35.3 %all-gather.3.cloned.1.call-done = bf16[32,32,4096]{2,1,0:T(8,128)(2,1)} async-done(((bf16[32,32,512]{2,1,0:T(8,128)(2,1)}), bf16[32,32,4096]{2,1,0:T(8,128)(2,1)}) %all-gather.3.cloned.1.call-update) | async-done | bytes 8388624 | tf_op jit(solution)/shard_map/all_gather | solution.py:131
  114.8 5.2 %multiply_reduce_fusion = f32[32,32]{1,0:T(8,128)S(1)} fusion(bf16[32,32,4096]{2,1,0:T(8,128)(2,1)} %all-gather.3.cloned.1.call-done), kind=kLoop, calls=%fused_computation.5 | loop fusion | flops 12581888 | bytes 8392704 | tf_op jit(solution)/shard_map/reduce_sum | solution.py:133
  120.0 0.5 copy-done.1
  120.5 5.1 %fusion.19 = f32[32,32,256]{2,1,0:T(8,128)} fusion(bf16[32,32,4096]{2,1,0:T(8,128)(2,1)S(1)} %copy-done.1, bf16[1,4096,256]{2,1,0:T(8,128)(2,1)} %param.18, f32[4096]{0:T(1024)S(1)} %bitcast.91, f32[32,32]{1,0:T(8,128)S(1)} %add_rsqrt_fusion), kind=kOutput, calls=%fused_computation.24 | convolution fusion | flops 2150891520 | bytes 11554816 | tf_op jit(solution)/shard_map/gmd,df->gmf/dot_general | solution.py:137
  125.6 16.2 %convolution_convert_fusion = bf16[32,32,4096]{2,1,0:T(8,128)(2,1)} fusion(bf16[1,256,4096]{2,1,0:T(8,128)(2,1)S(1)} %copy-done, bf16[32,32,4096]{2,1,0:T(8,128)(2,1)} %all-gather.3.cloned.1.call-done, bf16[1,4096,256]{2,1,0:T(8,128)(2,1)} %param.19, f32[4096]{0:T(1024)S(1)} %bitcast.92, f32[32,32,256]{2,1,0:T(8,128)} %fusion.19, f32[32,32]{1,0:T(8,128)S(1)} %add_rsqrt_fusion), kind=kOutput, calls=%fused_computation.6 | convolution fusion | flops 4304142336 | bytes 22040576 | tf_op jit(solution)/shard_map/gmf,fd->gmd/dot_general | solution.py:15
  142.2 0.1 copy.83
  142.3 0.1 reshape.468
  142.4 0.1 select_reduce_fusion.2
  142.7 0.6 gather_fusion.1
  143.4 0.1 copy.88
  143.5 0.1 add.336
  143.7 0.1 copy.86
  143.9 1.9 gather_fusion
  145.9 0.2 convert_reduce_fusion.3
  146.1 0.2 select_reduce_fusion
  146.3 50.0 %reduce-scatter.2.cloned.1.call-done = bf16[32,32,512]{2,1,0:T(8,128)(2,1)} async-done(((bf16[32,32,4096]{2,1,0:T(8,128)(2,1)}), bf16[32,32,512]{2,1,0:T(8,128)(2,1)}) %reduce-scatter.2.cloned.1.call-update) | async-done | bytes 1048592 | tf_op jit(solution)/shard_map/reduce_scatter | solution.py:16
  196.3 9.5 %all-to-all-start.2 = ((bf16[32,32,512]{2,1,0:T(8,128)(2,1)}), bf16[32,32,512]{2,1,0:T(8,128)(2,1)S(1)}, u32[]{:S(2)}, u32[]{:S(2)}) async-start(bf16[32,32,512]{2,1,0:T(8,128)(2,1)} %reduce-scatter.2.cloned.1.call-done), calls=%async_computation.3 | async-start | bytes 2097152 | tf_op jit(solution)/shard_map/all_to_all | solution.py:19
  205.9 0.2 fusion.46
  206.0 13.8 %all-reduce = (f32[64,8]{0,1:T(8,128)S(1)}, f32[64]{0:T(128)S(1)}) all-reduce(f32[64,8]{0,1:T(8,128)S(1)} %fusion.46, f32[64]{0:T(128)S(1)} %get-tuple-element.12), channel_id=1, replica_groups=mesh['ex'=4,'ez'=8,'tensor'=8] {'tensor'}, use_global_device_ids=true, to_apply=%region_4.0 | all-reduce | flops 576 | bytes 4608 | tf_op jit(solution)/shard_map/psum | solution.py:102
  220.0 0.2 fusion.52
  220.5 0.1 copy.82
  220.6 10.4 %all-to-all-done.2 = bf16[32,32,512]{2,1,0:T(8,128)(2,1)S(1)} async-done(((bf16[32,32,512]{2,1,0:T(8,128)(2,1)}), bf16[32,32,512]{2,1,0:T(8,128)(2,1)S(1)}, u32[]{:S(2)}, u32[]{:S(2)}) %all-to-all-start.2) | async-done | bytes 1048608 | tf_op jit(solution)/shard_map/all_to_all | solution.py:19
  231.0 2.6 gather_fusion.3
  233.6 1.2 gather.26
  234.8 0.9 convert_reduce_fusion
  235.7 0.4 multiply_reduce_fusion.1
  236.1 9.7 %all_gather.11 = bf16[256,512]{1,0:T(8,128)(2,1)S(1)} all-gather(bf16[64,512]{1,0:T(8,128)(2,1)S(1)} %fusion.48), channel_id=1, replica_groups=mesh['ex'=4,'ez'=8,'tensor'=8] {'ex'}, dimensions={0}, use_global_device_ids=true | all-gather | bytes 327680 | tf_op jit(solution)/shard_map/all_gather | solution.py:39
  245.9 1.1 convolution_convert_fusion.3
  247.0 5.6 %all-to-all-start.3 = ((bf16[8,64,512]{2,1,0:T(8,128)(2,1)}), bf16[8,64,512]{2,1,0:T(8,128)(2,1)S(1)}, u32[]{:S(2)}, u32[]{:S(2)}) async-start(bf16[8,64,512]{2,1,0:T(8,128)(2,1)} %convolution_convert_fusion.3), calls=%async_computation.4 | async-start | bytes 1048576 | tf_op jit(solution)/shard_map/all_to_all | solution.py:59
  252.5 0.3 convert_reduce_fusion.2
  252.9 11.7 %all-to-all-done.3 = bf16[8,64,512]{2,1,0:T(8,128)(2,1)S(1)} async-done(((bf16[8,64,512]{2,1,0:T(8,128)(2,1)}), bf16[8,64,512]{2,1,0:T(8,128)(2,1)S(1)}, u32[]{:S(2)}, u32[]{:S(2)}) %all-to-all-start.3) | async-done | bytes 524320 | tf_op jit(solution)/shard_map/all_to_all | solution.py:59
  264.6 0.7 gather_fusion.4
  265.3 0.2 fusion.43
  265.5 18.2 %psum.23 = f32[64]{0:T(128)S(1)} all-reduce(f32[64]{0:T(128)S(1)} %get-tuple-element.4), channel_id=1, replica_groups=mesh['ex'=4,'ez'=8,'tensor'=8] {'tensor'}, use_global_device_ids=true, to_apply=%region_17.18 | all-reduce | flops 64 | bytes 512 | tf_op jit(solution)/shard_map/psum | solution.py:24
  283.7 0.7 fusion.45
  (66 shorter events, 1.5 us)
Async XLA Ops:
  7.2 118.4 %copy-start = (bf16[1,256,4096]{2,1,0:T(8,128)(2,1)S(1)}, bf16[1,256,4096]{2,1,0:T(8,128)(2,1)}, u32[]{:S(2)}) copy-start(bf16[1,256,4096]{2,1,0:T(8,128)(2,1)} %param.20) | copy-start | bytes 6291460
  7.2 10.8 %copy-start.7 = (s32[64,2]{0,1:T(2,128)S(1)}, s32[64,2]{0,1:T(2,128)}, u32[]{:S(2)}) copy-start(s32[64,2]{0,1:T(2,128)} %param.17) | copy-start | bytes 1540
  7.2 13.0 %copy-start.9 = (s32[32]{0:T(128)S(1)}, s32[32]{0:T(128)}, u32[]{:S(2)}) copy-start(s32[32]{0:T(128)} %param.21) | copy-start | bytes 388
  7.2 20.2 %copy-start.3 = (bf16[64,512]{1,0:T(8,128)(2,1)S(1)}, bf16[64,512]{1,0:T(8,128)(2,1)}, u32[]{:S(2)}) copy-start(bf16[64,512]{1,0:T(8,128)(2,1)} %param.13) | copy-start | bytes 196612
  11.3 52.2 %copy-start.6 = (f32[512]{0:T(512)S(1)}, f32[512]{0:T(512)}, u32[]{:S(2)}) copy-start(f32[512]{0:T(512)} %param.15) | copy-start | bytes 6148
  11.3 16.1 %all-to-all-start = ((bf16[8,64,512]{2,1,0:T(8,128)(2,1)}), bf16[8,64,512]{2,1,0:T(8,128)(2,1)S(1)}, u32[]{:S(2)}, u32[]{:S(2)}) async-start(bf16[8,64,512]{2,1,0:T(8,128)(2,1)} %bitcast.86), calls=%async_computation | async-start | bytes 1048576 | tf_op jit(solution)/shard_map/all_to_all | solution.py:95
  18.0 96.8 %all-gather.3.cloned.1.call-start = ((), (), s32[]{:S(2)}) async-start(), calls=%async_computation.5 | async-start | bytes 9437184 | tf_op jit(solution)/shard_map/all_gather | solution.py:131
  63.4 132.8 %reduce-scatter.2.cloned.1.call-start = ((), (), s32[]{:S(2)}) async-start(), calls=%async_computation.6 | async-start | bytes 9437184 | tf_op jit(solution)/shard_map/reduce_scatter | solution.py:16
  114.8 5.8 %copy-start.1 = (bf16[32,32,4096]{2,1,0:T(8,128)(2,1)S(1)}, bf16[32,32,4096]{2,1,0:T(8,128)(2,1)}, u32[]{:S(2)}) copy-start(bf16[32,32,4096]{2,1,0:T(8,128)(2,1)} %all-gather.3.cloned.1.call-done) | copy-start | bytes 25165828
  141.8 2.0 copy-start.4
  141.9 64.0 %copy-start.5 = (f32[512,8]{0,1:T(8,128)S(1)}, f32[512,8]{0,1:T(8,128)}, u32[]{:S(2)}) copy-start(f32[512,8]{0,1:T(8,128)} %param.16) | copy-start | bytes 49156
  196.3 34.7 %all-to-all-start.2 = ((bf16[32,32,512]{2,1,0:T(8,128)(2,1)}), bf16[32,32,512]{2,1,0:T(8,128)(2,1)S(1)}, u32[]{:S(2)}, u32[]{:S(2)}) async-start(bf16[32,32,512]{2,1,0:T(8,128)(2,1)} %reduce-scatter.2.cloned.1.call-done), calls=%async_computation.3 | async-start | bytes 2097152 | tf_op jit(solution)/shard_map/all_to_all | solution.py:19
  231.0 52.7 %copy-start.8 = (f32[512]{0:T(512)S(1)}, f32[512]{0:T(512)}, u32[]{:S(2)}) copy-start(f32[512]{0:T(512)} %param.22) | copy-start | bytes 6148
  247.0 17.6 %all-to-all-start.3 = ((bf16[8,64,512]{2,1,0:T(8,128)(2,1)}), bf16[8,64,512]{2,1,0:T(8,128)(2,1)S(1)}, u32[]{:S(2)}, u32[]{:S(2)}) async-start(bf16[8,64,512]{2,1,0:T(8,128)(2,1)} %convolution_convert_fusion.3), calls=%async_computation.4 | async-start | bytes 1048576 | tf_op jit(solution)/shard_map/all_to_all | solution.py:59
  265.5 19.0 %copy-start.2 = (bf16[64,512]{1,0:T(8,128)(2,1)}, bf16[64,512]{1,0:T(8,128)(2,1)S(1)}, u32[]{:S(2)}) copy-start(bf16[64,512]{1,0:T(8,128)(2,1)S(1)} %get-tuple-element.5) | copy-start | bytes 196612
Sparse Core Ops, SparseCore 0:
  63.6 51.1 all-gather.2
  142.0 54.2 reduce-scatter.1

commit v7 on v6

--- a/solution.py
+++ b/solution.py
@@ -11,7 +11,7 @@
 
 
 def finish_slots(gate_val, up_val, down_weight):
-    active = (jax.nn.silu(gate_val) * up_val).astype(jnp.bfloat16)
+    active = lax.optimization_barrier((jax.nn.silu(gate_val) * up_val).astype(jnp.bfloat16))
     partial_out = jnp.einsum("gmf,fd->gmd", active, down_weight, preferred_element_type=jnp.float32)
     summed = lax.psum_scatter(
         partial_out.astype(jnp.bfloat16), "tensor", scatter_dimension=2, tiled=True

time: 292 us -> 283 us (0.969)
  matrix products: 26.7 us -> 17.8 us
    dot_general x1, matrix products: 16.2 us -> 5.58 us  [finish_slots(): jnp.einsum('gmf,fd->gmd', active, down_weight, preferred_element_type=jnp...]
where the time goes in v7:
time: 283 us; the launch traced here: 282 us
  waiting for transfers between devices  114 us (40%)
  blocking collectives  93.3 us (33%)
  starting transfers between devices  21.8 us (8%)
  matrix products  17.8 us (6%)
  between operations  14.4 us (5%)
  local copies, waits for them, and re-layouts  10.5 us (4%)
  other arithmetic  10.5 us (4%)
    reduce_scatter x1, waiting for transfers between devices, finish_slots(): lax.psum_scatter(partial_out.astype(jnp.bfloat16), 'tensor', scatter_dime...  50.2 us
    all_to_all x1, blocking collectives, on_device(): lax.all_to_all(outgoing, EXPERT, split_axis=0, concat_axis=0, tiled=True)  35.4 us
    all_gather x1, waiting for transfers between devices, on_device(): arrived = lax.all_gather(arrived_part, 'tensor', axis=2, tiled=True)  35.3 us
    psum x1, blocking collectives, final_norm(): square_total = lax.psum(jnp.sum(stream_f * stream_f, axis=1), 'tensor')  18.2 us
    all_gather x1, blocking collectives, on_device(): gain_full = lax.all_gather(norm_gain, 'tensor', axis=0, tiled=True)[:, None]  15.9 us
    psum x1, blocking collectives, on_device(): lax.psum((jnp.sum(hidden_f * hidden_f, axis=1), jnp.dot(scaled, router_we...  14 us
    all_to_all x1, waiting for transfers between devices, restore(): lax.all_to_all(send, 'ez', split_axis=0, concat_axis=0, tiled=True)  11.7 us
    all_to_all x1, waiting for transfers between devices, finish_slots(): lax.all_to_all(summed, EXPERT, split_axis=0, concat_axis=0, tiled=True)  10.2 us
  transfers between devices with their start and end apart: 5, of which 5 were waited for; matrix products, arithmetic and copies ran while one was open for 3% of the time, Pallas kernels for 0%

profile of v7, /device:TPU:1, one launch (start us, length us, event | category | flops | bytes accessed | tf_op | source)
XLA Modules:
  0.0 282.4 jit_solution(17507936370876516725)
XLA Ops:
  7.2 3.2 %convolution_convert_fusion.1 = bf16[64,4096]{1,0:T(8,128)(2,1)S(1)} fusion(bf16[64,512]{1,0:T(8,128)(2,1)} %param.12, bf16[512,4096]{1,0:T(8,128)(2,1)} %param.14), kind=kOutput, calls=%fused_computation.7 | convolution fusion | flops 268697600 | bytes 4784128 | tf_op jit(solution)/shard_map/dot_general | solution.py:91
  10.4 0.8 copy.95
  11.3 6.7 %all-to-all-start = ((bf16[8,64,512]{2,1,0:T(8,128)(2,1)}), bf16[8,64,512]{2,1,0:T(8,128)(2,1)S(1)}, u32[]{:S(2)}, u32[]{:S(2)}) async-start(bf16[8,64,512]{2,1,0:T(8,128)(2,1)} %bitcast.83), calls=%async_computation | async-start | bytes 1048576 | tf_op jit(solution)/shard_map/all_to_all | solution.py:95
  18.1 0.2 convert_reduce_fusion.4
  18.4 1.2 select_reduce_fusion.1
  19.6 0.4 fusion.25
  20.1 0.1 copy.87
  20.2 0.6 gather_fusion.2
  20.8 6.5 %all-to-all-done = bf16[8,64,512]{2,1,0:T(8,128)(2,1)S(1)} async-done(((bf16[8,64,512]{2,1,0:T(8,128)(2,1)}), bf16[8,64,512]{2,1,0:T(8,128)(2,1)S(1)}, u32[]{:S(2)}, u32[]{:S(2)}) %all-to-all-start) | async-done | bytes 524320 | tf_op jit(solution)/shard_map/all_to_all | solution.py:95
  27.4 0.1 fusion.38
  27.6 0.5 convolution_convert_fusion.2
  28.0 35.4 %all_to_all.20 = bf16[32,32,512]{2,1,0:T(8,128)(2,1)} all-to-all(bf16[32,32,512]{2,1,0:T(8,128)(2,1)S(1)} %convolution_convert_fusion.2), channel_id=1, replica_groups=mesh['ex'=4,'ez'=8,'tensor'=8] {'ex','ez'}, dimensions={0} | all-to-all | bytes 2097152 | tf_op jit(solution)/shard_map/all_to_all | solution.py:130
  63.5 15.9 %all-gather = f32[8,1,512]{2,1,0:T(1,128)S(1)} all-gather(f32[1,1,512]{2,1,0:T(1,128)S(1)} %bitcast.90), channel_id=1, replica_groups=mesh['ex'=4,'ez'=8,'tensor'=8] {'tensor'}, dimensions={0}, use_global_device_ids=true | all-gather | bytes 18432 | tf_op jit(solution)/shard_map/all_gather | solution.py:134
  79.4 35.3 %all-gather.3.cloned.1.call-done = bf16[32,32,4096]{2,1,0:T(8,128)(2,1)} async-done(((bf16[32,32,512]{2,1,0:T(8,128)(2,1)}), bf16[32,32,4096]{2,1,0:T(8,128)(2,1)}) %all-gather.3.cloned.1.call-update) | async-done | bytes 8388624 | tf_op jit(solution)/shard_map/all_gather | solution.py:131
  114.8 5.2 %multiply_reduce_fusion = f32[32,32]{1,0:T(8,128)S(1)} fusion(bf16[32,32,4096]{2,1,0:T(8,128)(2,1)} %all-gather.3.cloned.1.call-done), kind=kLoop, calls=%fused_computation.5 | loop fusion | flops 12581888 | bytes 8392704 | tf_op jit(solution)/shard_map/reduce_sum | solution.py:133
  120.0 0.5 copy-done.1
  120.5 4.2 %fusion.19 = f32[32,32,256]{2,1,0:T(8,128)S(1)} fusion(bf16[32,32,4096]{2,1,0:T(8,128)(2,1)S(1)} %copy-done.1, bf16[1,4096,256]{2,1,0:T(8,128)(2,1)} %param.18, f32[4096]{0:T(1024)S(1)} %bitcast.88, f32[32,32]{1,0:T(8,128)S(1)} %add_rsqrt_fusion), kind=kOutput, calls=%fused_computation.24 | convolution fusion | flops 2150891520 | bytes 11554816 | tf_op jit(solution)/shard_map/gmd,df->gmf/dot_general | solution.py:137
  124.8 2.6 fusion.22
  127.4 5.6 %convolution_convert_fusion = bf16[32,32,4096]{2,1,0:T(8,128)(2,1)} fusion(bf16[32,32,256]{2,1,0:T(8,128)(2,1)S(1)} %fusion.22, bf16[1,256,4096]{2,1,0:T(8,128)(2,1)S(1)} %copy-done), kind=kOutput, calls=%fused_computation.6 | convolution fusion | flops 2151677952 | bytes 11010048 | tf_op jit(solution)/shard_map/gmf,fd->gmd/dot_general | solution.py:15
  133.3 0.1 copy.83
  133.4 0.1 reshape.468
  133.6 0.1 select_reduce_fusion.2
  133.8 0.6 gather_fusion.1
  134.6 0.1 copy.88
  134.7 0.1 add.336
  134.8 0.1 copy.86
  135.0 1.7 gather_fusion
  136.8 0.2 convert_reduce_fusion.3
  137.0 0.2 select_reduce_fusion
  137.2 50.2 %reduce-scatter.2.cloned.1.call-done = bf16[32,32,512]{2,1,0:T(8,128)(2,1)} async-done(((bf16[32,32,4096]{2,1,0:T(8,128)(2,1)}), bf16[32,32,512]{2,1,0:T(8,128)(2,1)}) %reduce-scatter.2.cloned.1.call-update) | async-done | bytes 1048592 | tf_op jit(solution)/shard_map/reduce_scatter | solution.py:16
  187.4 9.5 %all-to-all-start.2 = ((bf16[32,32,512]{2,1,0:T(8,128)(2,1)}), bf16[32,32,512]{2,1,0:T(8,128)(2,1)S(1)}, u32[]{:S(2)}, u32[]{:S(2)}) async-start(bf16[32,32,512]{2,1,0:T(8,128)(2,1)} %reduce-scatter.2.cloned.1.call-done), calls=%async_computation.3 | async-start | bytes 2097152 | tf_op jit(solution)/shard_map/all_to_all | solution.py:19
  197.0 0.2 fusion.37
  197.2 14.0 %all-reduce = (f32[64,8]{0,1:T(8,128)S(1)}, f32[64]{0:T(128)S(1)}) all-reduce(f32[64,8]{0,1:T(8,128)S(1)} %fusion.37, f32[64]{0:T(128)S(1)} %get-tuple-element.12), channel_id=1, replica_groups=mesh['ex'=4,'ez'=8,'tensor'=8] {'tensor'}, use_global_device_ids=true, to_apply=%region_4.0 | all-reduce | flops 576 | bytes 4608 | tf_op jit(solution)/shard_map/psum | solution.py:102
  211.3 0.2 fusion.43
  211.9 10.2 %all-to-all-done.2 = bf16[32,32,512]{2,1,0:T(8,128)(2,1)S(1)} async-done(((bf16[32,32,512]{2,1,0:T(8,128)(2,1)}), bf16[32,32,512]{2,1,0:T(8,128)(2,1)S(1)}, u32[]{:S(2)}, u32[]{:S(2)}) %all-to-all-start.2) | async-done | bytes 1048608 | tf_op jit(solution)/shard_map/all_to_all | solution.py:19
  222.1 2.6 gather_fusion.3
  224.8 1.2 gather.26
  225.9 0.9 convert_reduce_fusion
  226.8 0.4 multiply_reduce_fusion.1
  227.3 9.7 %all_gather.11 = bf16[256,512]{1,0:T(8,128)(2,1)S(1)} all-gather(bf16[64,512]{1,0:T(8,128)(2,1)S(1)} %fusion.39), channel_id=1, replica_groups=mesh['ex'=4,'ez'=8,'tensor'=8] {'ex'}, dimensions={0}, use_global_device_ids=true | all-gather | bytes 327680 | tf_op jit(solution)/shard_map/all_gather | solution.py:39
  237.0 1.1 convolution_convert_fusion.3
  238.1 5.5 %all-to-all-start.3 = ((bf16[8,64,512]{2,1,0:T(8,128)(2,1)}), bf16[8,64,512]{2,1,0:T(8,128)(2,1)S(1)}, u32[]{:S(2)}, u32[]{:S(2)}) async-start(bf16[8,64,512]{2,1,0:T(8,128)(2,1)} %convolution_convert_fusion.3), calls=%async_computation.4 | async-start | bytes 1048576 | tf_op jit(solution)/shard_map/all_to_all | solution.py:59
  243.7 0.3 convert_reduce_fusion.2
  244.0 11.7 %all-to-all-done.3 = bf16[8,64,512]{2,1,0:T(8,128)(2,1)S(1)} async-done(((bf16[8,64,512]{2,1,0:T(8,128)(2,1)}), bf16[8,64,512]{2,1,0:T(8,128)(2,1)S(1)}, u32[]{:S(2)}, u32[]{:S(2)}) %all-to-all-start.3) | async-done | bytes 524320 | tf_op jit(solution)/shard_map/all_to_all | solution.py:59
  255.7 0.7 gather_fusion.4
  256.4 0.2 fusion.34
  256.6 18.2 %psum.23 = f32[64]{0:T(128)S(1)} all-reduce(f32[64]{0:T(128)S(1)} %get-tuple-element.4), channel_id=1, replica_groups=mesh['ex'=4,'ez'=8,'tensor'=8] {'tensor'}, use_global_device_ids=true, to_apply=%region_17.18 | all-reduce | flops 64 | bytes 512 | tf_op jit(solution)/shard_map/psum | solution.py:24
  274.8 0.7 fusion.36
  (69 shorter events, 1.6 us)
Async XLA Ops:
  7.2 120.2 %copy-start = (bf16[1,256,4096]{2,1,0:T(8,128)(2,1)S(1)}, bf16[1,256,4096]{2,1,0:T(8,128)(2,1)}, u32[]{:S(2)}) copy-start(bf16[1,256,4096]{2,1,0:T(8,128)(2,1)} %param.20) | copy-start | bytes 6291460
  7.2 10.8 %copy-start.7 = (s32[64,2]{0,1:T(2,128)S(1)}, s32[64,2]{0,1:T(2,128)}, u32[]{:S(2)}) copy-start(s32[64,2]{0,1:T(2,128)} %param.17) | copy-start | bytes 1540
  7.2 13.0 %copy-start.10 = (s32[32]{0:T(128)S(1)}, s32[32]{0:T(128)}, u32[]{:S(2)}) copy-start(s32[32]{0:T(128)} %param.21) | copy-start | bytes 388
  7.2 20.2 %copy-start.3 = (bf16[64,512]{1,0:T(8,128)(2,1)S(1)}, bf16[64,512]{1,0:T(8,128)(2,1)}, u32[]{:S(2)}) copy-start(bf16[64,512]{1,0:T(8,128)(2,1)} %param.13) | copy-start | bytes 196612
  11.3 52.2 %copy-start.6 = (f32[512]{0:T(512)S(1)}, f32[512]{0:T(512)}, u32[]{:S(2)}) copy-start(f32[512]{0:T(512)} %param.15) | copy-start | bytes 6148
  11.3 16.1 %all-to-all-start = ((bf16[8,64,512]{2,1,0:T(8,128)(2,1)}), bf16[8,64,512]{2,1,0:T(8,128)(2,1)S(1)}, u32[]{:S(2)}, u32[]{:S(2)}) async-start(bf16[8,64,512]{2,1,0:T(8,128)(2,1)} %bitcast.83), calls=%async_computation | async-start | bytes 1048576 | tf_op jit(solution)/shard_map/all_to_all | solution.py:95
  18.0 96.8 %all-gather.3.cloned.1.call-start = ((), (), s32[]{:S(2)}) async-start(), calls=%async_computation.5 | async-start | bytes 9437184 | tf_op jit(solution)/shard_map/all_gather | solution.py:131
  63.4 124.0 %reduce-scatter.2.cloned.1.call-start = ((), (), s32[]{:S(2)}) async-start(), calls=%async_computation.6 | async-start | bytes 9437184 | tf_op jit(solution)/shard_map/reduce_scatter | solution.py:16
  114.8 5.8 %copy-start.1 = (bf16[32,32,4096]{2,1,0:T(8,128)(2,1)S(1)}, bf16[32,32,4096]{2,1,0:T(8,128)(2,1)}, u32[]{:S(2)}) copy-start(bf16[32,32,4096]{2,1,0:T(8,128)(2,1)} %all-gather.3.cloned.1.call-done) | copy-start | bytes 25165828
  120.5 4.2 %copy-start.9 = (bf16[1,4096,256]{2,1,0:T(8,128)(2,1)S(1)}, bf16[1,4096,256]{2,1,0:T(8,128)(2,1)}, u32[]{:S(2)}) copy-start(bf16[1,4096,256]{2,1,0:T(8,128)(2,1)} %param.19) | copy-start | bytes 6291460
  133.0 2.0 copy-start.4
  133.0 64.0 %copy-start.5 = (f32[512,8]{0,1:T(8,128)S(1)}, f32[512,8]{0,1:T(8,128)}, u32[]{:S(2)}) copy-start(f32[512,8]{0,1:T(8,128)} %param.16) | copy-start | bytes 49156
  187.4 34.7 %all-to-all-start.2 = ((bf16[32,32,512]{2,1,0:T(8,128)(2,1)}), bf16[32,32,512]{2,1,0:T(8,128)(2,1)S(1)}, u32[]{:S(2)}, u32[]{:S(2)}) async-start(bf16[32,32,512]{2,1,0:T(8,128)(2,1)} %reduce-scatter.2.cloned.1.call-done), calls=%async_computation.3 | async-start | bytes 2097152 | tf_op jit(solution)/shard_map/all_to_all | solution.py:19
  222.1 52.7 %copy-start.8 = (f32[512]{0:T(512)S(1)}, f32[512]{0:T(512)}, u32[]{:S(2)}) copy-start(f32[512]{0:T(512)} %param.22) | copy-start | bytes 6148
  238.1 17.6 %all-to-all-start.3 = ((bf16[8,64,512]{2,1,0:T(8,128)(2,1)}), bf16[8,64,512]{2,1,0:T(8,128)(2,1)S(1)}, u32[]{:S(2)}, u32[]{:S(2)}) async-start(bf16[8,64,512]{2,1,0:T(8,128)(2,1)} %convolution_convert_fusion.3), calls=%async_computation.4 | async-start | bytes 1048576 | tf_op jit(solution)/shard_map/all_to_all | solution.py:59
  256.6 18.9 %copy-start.2 = (bf16[64,512]{1,0:T(8,128)(2,1)}, bf16[64,512]{1,0:T(8,128)(2,1)S(1)}, u32[]{:S(2)}) copy-start(bf16[64,512]{1,0:T(8,128)(2,1)S(1)} %get-tuple-element.5) | copy-start | bytes 196612
Sparse Core Ops, SparseCore 0:
  63.6 51.1 all-gather.2
  133.1 54.2 reduce-scatter.1

commit v8 on v7

--- a/solution.py
+++ b/solution.py
@@ -129,8 +129,9 @@
     ).astype(jnp.bfloat16)
     arrived_part = lax.all_to_all(outgoing, EXPERT, split_axis=0, concat_axis=0, tiled=True)
     arrived = lax.all_gather(arrived_part, "tensor", axis=2, tiled=True)
-    arrived_f = arrived.astype(jnp.float32)
-    slot_rms = lax.rsqrt(jnp.sum(arrived_f * arrived_f, axis=2) / D + EPS)[:, :, None]
+    part_f = arrived_part.astype(jnp.float32)
+    slot_square = lax.psum(jnp.sum(part_f * part_f, axis=2), "tensor")
+    slot_rms = lax.rsqrt(slot_square / D + EPS)[:, :, None]
     gain_full = lax.all_gather(norm_gain, "tensor", axis=0, tiled=True)[:, None]
     gate_weight = (w_gate[0].astype(jnp.float32) * gain_full).astype(jnp.bfloat16)
     up_weight = (w_up[0].astype(jnp.float32) * gain_full).astype(jnp.bfloat16)

time: 283 us -> 280 us (0.989)
  waiting for transfers between devices: 114 us -> 103 us
  blocking collectives: 93.3 us -> 102 us
  other arithmetic: 10.5 us -> 6.86 us
    all_gather x1, waiting for transfers between devices: 35.3 us -> 10.7 us  [on_device(): arrived = lax.all_gather(arrived_part, 'tensor', axis=2, tiled=True)]
    all_to_all x1, waiting for transfers between devices: 10.2 us -> 24.2 us  [finish_slots(): lax.all_to_all(summed, EXPERT, split_axis=0, concat_axis=0, tiled=True)]
    psum x1, blocking collectives: 14 us -> 23.4 us  [on_device(): slot_square = lax.psum(jnp.sum(part_f * part_f, axis=2), 'tensor')]
    reduce_sum x1, other arithmetic: 5.23 us -> 1.54 us  [on_device(): slot_square = lax.psum(jnp.sum(part_f * part_f, axis=2), 'tensor')]
where the time goes in v8:
time: 280 us
  waiting for transfers between devices  103 us (37%)
  blocking collectives  102 us (36%)
  starting transfers between devices  21.9 us (8%)
  matrix products  20.1 us (7%)
  between operations  14.4 us (5%)
  local copies, waits for them, and re-layouts  10.4 us (4%)
  other arithmetic  6.86 us (2%)
    reduce_scatter x1, waiting for transfers between devices, finish_slots(): lax.psum_scatter(partial_out.astype(jnp.bfloat16), 'tensor', scatter_dime...  50.3 us
    all_to_all x1, blocking collectives, on_device(): lax.all_to_all(outgoing, EXPERT, split_axis=0, concat_axis=0, tiled=True)  35.4 us
    all_to_all x1, waiting for transfers between devices, finish_slots(): lax.all_to_all(summed, EXPERT, split_axis=0, concat_axis=0, tiled=True)  24.2 us
    psum x1, blocking collectives, on_device(): slot_square = lax.psum(jnp.sum(part_f * part_f, axis=2), 'tensor')  23.4 us
    psum x1, blocking collectives, final_norm(): square_total = lax.psum(jnp.sum(stream_f * stream_f, axis=1), 'tensor')  18.2 us
    all_gather x1, blocking collectives, on_device(): gain_full = lax.all_gather(norm_gain, 'tensor', axis=0, tiled=True)[:, None]  15.8 us
    all_to_all x1, waiting for transfers between devices, restore(): lax.all_to_all(send, 'ez', split_axis=0, concat_axis=0, tiled=True)  11.7 us
    all_gather x1, waiting for transfers between devices, on_device(): arrived = lax.all_gather(arrived_part, 'tensor', axis=2, tiled=True)  10.7 us
  transfers between devices with their start and end apart: 5, of which 5 were waited for; matrix products, arithmetic and copies ran while one was open for 3% of the time, Pallas kernels for 0%

profile of v8, /device:TPU:1, one launch (start us, length us, event | category | flops | bytes accessed | tf_op | source)
XLA Modules:
  0.0 279.6 jit_solution(3446582628782328790)
XLA Ops:
  7.2 3.2 %convolution_convert_fusion.1 = bf16[64,4096]{1,0:T(8,128)(2,1)S(1)} fusion(bf16[64,512]{1,0:T(8,128)(2,1)} %param.12, bf16[512,4096]{1,0:T(8,128)(2,1)} %param.14), kind=kOutput, calls=%fused_computation.6 | convolution fusion | flops 268697600 | bytes 4784128 | tf_op jit(solution)/shard_map/dot_general | solution.py:91
  10.4 0.8 copy.95
  11.3 6.7 %all-to-all-start = ((bf16[8,64,512]{2,1,0:T(8,128)(2,1)}), bf16[8,64,512]{2,1,0:T(8,128)(2,1)S(1)}, u32[]{:S(2)}, u32[]{:S(2)}) async-start(bf16[8,64,512]{2,1,0:T(8,128)(2,1)} %bitcast.83), calls=%async_computation | async-start | bytes 1048576 | tf_op jit(solution)/shard_map/all_to_all | solution.py:95
  18.1 0.2 convert_reduce_fusion.4
  18.4 1.2 select_reduce_fusion.1
  19.6 0.4 fusion.25
  20.1 0.1 copy.87
  20.2 0.6 gather_fusion.2
  20.8 6.5 %all-to-all-done = bf16[8,64,512]{2,1,0:T(8,128)(2,1)S(1)} async-done(((bf16[8,64,512]{2,1,0:T(8,128)(2,1)}), bf16[8,64,512]{2,1,0:T(8,128)(2,1)S(1)}, u32[]{:S(2)}, u32[]{:S(2)}) %all-to-all-start) | async-done | bytes 524320 | tf_op jit(solution)/shard_map/all_to_all | solution.py:95
  27.5 0.1 fusion.38
  27.6 0.5 convolution_convert_fusion.2
  28.1 35.4 %all_to_all.20 = bf16[32,32,512]{2,1,0:T(8,128)(2,1)} all-to-all(bf16[32,32,512]{2,1,0:T(8,128)(2,1)S(1)} %convolution_convert_fusion.2), channel_id=1, replica_groups=mesh['ex'=4,'ez'=8,'tensor'=8] {'ex','ez'}, dimensions={0} | all-to-all | bytes 2097152 | tf_op jit(solution)/shard_map/all_to_all | solution.py:130
  63.5 15.8 %all-gather = f32[8,1,512]{2,1,0:T(1,128)S(1)} all-gather(f32[1,1,512]{2,1,0:T(1,128)S(1)} %bitcast.90), channel_id=1, replica_groups=mesh['ex'=4,'ez'=8,'tensor'=8] {'tensor'}, dimensions={0}, use_global_device_ids=true | all-gather | bytes 18432 | tf_op jit(solution)/shard_map/all_gather | solution.py:135
  79.3 0.2 fusion.37
  79.5 1.5 multiply_reduce_fusion
  81.0 23.4 %all-reduce = (f32[32,32]{1,0:T(8,128)S(1)}, f32[64,8]{0,1:T(8,128)S(1)}, f32[64]{0:T(128)S(1)}) all-reduce(f32[32,32]{1,0:T(8,128)S(1)} %multiply_reduce_fusion, f32[64,8]{0,1:T(8,128)S(1)} %fusion.37, f32[64]{0:T(128)S(1)} %get-tuple-element.15), channel_id=1, replica_groups=mesh['ex'=4,'ez'=8,'tensor'=8] {'tensor'}, use_global_device_ids=true, to_apply=%region_13.14 | all-reduce | flops 1600 | bytes 12800 | tf_op jit(solution)/shard_map/psum | solution.py:133
  104.4 10.7 %all-gather.3.cloned.1.call-done = bf16[32,32,4096]{2,1,0:T(8,128)(2,1)} async-done(((bf16[32,32,512]{2,1,0:T(8,128)(2,1)}), bf16[32,32,4096]{2,1,0:T(8,128)(2,1)}) %all-gather.3.cloned.1.call-update) | async-done | bytes 8388624 | tf_op jit(solution)/shard_map/all_gather | solution.py:131
  115.1 6.6 %fusion.19 = f32[32,32,256]{2,1,0:T(8,128)S(1)} fusion(bf16[32,32,4096]{2,1,0:T(8,128)(2,1)} %all-gather.3.cloned.1.call-done, bf16[1,4096,256]{2,1,0:T(8,128)(2,1)} %param.18, f32[4096]{0:T(1024)S(1)} %bitcast.88, f32[32,32]{1,0:T(8,128)S(1)} %add_rsqrt_fusion), kind=kOutput, calls=%fused_computation.24 | convolution fusion | flops 2150891520 | bytes 11554816 | tf_op jit(solution)/shard_map/gmd,df->gmf/dot_general | solution.py:138
  121.7 0.4 copy-done.9
  122.1 2.5 fusion.22
  124.6 5.6 %convolution_convert_fusion = bf16[32,32,4096]{2,1,0:T(8,128)(2,1)} fusion(bf16[32,32,256]{2,1,0:T(8,128)(2,1)S(1)} %fusion.22, bf16[1,256,4096]{2,1,0:T(8,128)(2,1)S(1)} %copy-done), kind=kOutput, calls=%fused_computation.5 | convolution fusion | flops 2151677952 | bytes 11010048 | tf_op jit(solution)/shard_map/gmf,fd->gmd/dot_general | solution.py:15
  130.6 0.1 copy.83
  130.7 0.1 reshape.464
  130.8 0.1 select_reduce_fusion.2
  131.0 0.6 gather_fusion.1
  131.8 0.1 copy.88
  131.9 0.1 add.334
  132.1 0.1 copy.86
  132.3 1.7 gather_fusion
  134.0 0.2 convert_reduce_fusion.3
  134.2 50.3 %reduce-scatter.2.cloned.1.call-done = bf16[32,32,512]{2,1,0:T(8,128)(2,1)} async-done(((bf16[32,32,4096]{2,1,0:T(8,128)(2,1)}), bf16[32,32,512]{2,1,0:T(8,128)(2,1)}) %reduce-scatter.2.cloned.1.call-update) | async-done | bytes 1048592 | tf_op jit(solution)/shard_map/reduce_scatter | solution.py:16
  184.6 9.5 %all-to-all-start.2 = ((bf16[32,32,512]{2,1,0:T(8,128)(2,1)}), bf16[32,32,512]{2,1,0:T(8,128)(2,1)S(1)}, u32[]{:S(2)}, u32[]{:S(2)}) async-start(bf16[32,32,512]{2,1,0:T(8,128)(2,1)} %reduce-scatter.2.cloned.1.call-done), calls=%async_computation.3 | async-start | bytes 2097152 | tf_op jit(solution)/shard_map/all_to_all | solution.py:19
  194.1 0.2 select_reduce_fusion
  194.5 0.2 fusion.43
  195.1 24.2 %all-to-all-done.2 = bf16[32,32,512]{2,1,0:T(8,128)(2,1)S(1)} async-done(((bf16[32,32,512]{2,1,0:T(8,128)(2,1)}), bf16[32,32,512]{2,1,0:T(8,128)(2,1)S(1)}, u32[]{:S(2)}, u32[]{:S(2)}) %all-to-all-start.2) | async-done | bytes 1048608 | tf_op jit(solution)/shard_map/all_to_all | solution.py:19
  219.3 2.6 gather_fusion.3
  221.9 1.2 gather.26
  223.1 0.9 convert_reduce_fusion
  224.0 0.4 multiply_reduce_fusion.1
  224.4 9.7 %all_gather.11 = bf16[256,512]{1,0:T(8,128)(2,1)S(1)} all-gather(bf16[64,512]{1,0:T(8,128)(2,1)S(1)} %fusion.39), channel_id=1, replica_groups=mesh['ex'=4,'ez'=8,'tensor'=8] {'ex'}, dimensions={0}, use_global_device_ids=true | all-gather | bytes 327680 | tf_op jit(solution)/shard_map/all_gather | solution.py:39
  234.2 1.1 convolution_convert_fusion.3
  235.3 5.5 %all-to-all-start.3 = ((bf16[8,64,512]{2,1,0:T(8,128)(2,1)}), bf16[8,64,512]{2,1,0:T(8,128)(2,1)S(1)}, u32[]{:S(2)}, u32[]{:S(2)}) async-start(bf16[8,64,512]{2,1,0:T(8,128)(2,1)} %convolution_convert_fusion.3), calls=%async_computation.4 | async-start | bytes 1048576 | tf_op jit(solution)/shard_map/all_to_all | solution.py:59
  240.8 0.3 convert_reduce_fusion.2
  241.2 11.7 %all-to-all-done.3 = bf16[8,64,512]{2,1,0:T(8,128)(2,1)S(1)} async-done(((bf16[8,64,512]{2,1,0:T(8,128)(2,1)}), bf16[8,64,512]{2,1,0:T(8,128)(2,1)S(1)}, u32[]{:S(2)}, u32[]{:S(2)}) %all-to-all-start.3) | async-done | bytes 524320 | tf_op jit(solution)/shard_map/all_to_all | solution.py:59
  252.9 0.7 gather_fusion.4
  253.6 0.2 fusion.34
  253.8 18.2 %psum.31 = f32[64]{0:T(128)S(1)} all-reduce(f32[64]{0:T(128)S(1)} %get-tuple-element.5), channel_id=1, replica_groups=mesh['ex'=4,'ez'=8,'tensor'=8] {'tensor'}, use_global_device_ids=true, to_apply=%region_18.19 | all-reduce | flops 64 | bytes 512 | tf_op jit(solution)/shard_map/psum | solution.py:24
  272.0 0.7 fusion.36
  (69 shorter events, 1.6 us)
Async XLA Ops:
  7.2 117.5 %copy-start = (bf16[1,256,4096]{2,1,0:T(8,128)(2,1)S(1)}, bf16[1,256,4096]{2,1,0:T(8,128)(2,1)}, u32[]{:S(2)}) copy-start(bf16[1,256,4096]{2,1,0:T(8,128)(2,1)} %param.20) | copy-start | bytes 6291460
  7.2 10.8 %copy-start.6 = (s32[64,2]{0,1:T(2,128)S(1)}, s32[64,2]{0,1:T(2,128)}, u32[]{:S(2)}) copy-start(s32[64,2]{0,1:T(2,128)} %param.17) | copy-start | bytes 1540
  7.2 13.0 %copy-start.10 = (s32[32]{0:T(128)S(1)}, s32[32]{0:T(128)}, u32[]{:S(2)}) copy-start(s32[32]{0:T(128)} %param.21) | copy-start | bytes 388
  7.2 20.2 %copy-start.2 = (bf16[64,512]{1,0:T(8,128)(2,1)S(1)}, bf16[64,512]{1,0:T(8,128)(2,1)}, u32[]{:S(2)}) copy-start(bf16[64,512]{1,0:T(8,128)(2,1)} %param.13) | copy-start | bytes 196612
  11.3 52.2 %copy-start.5 = (f32[512]{0:T(512)S(1)}, f32[512]{0:T(512)}, u32[]{:S(2)}) copy-start(f32[512]{0:T(512)} %param.15) | copy-start | bytes 6148
  11.3 68.0 %copy-start.4 = (f32[512,8]{0,1:T(8,128)S(1)}, f32[512,8]{0,1:T(8,128)}, u32[]{:S(2)}) copy-start(f32[512,8]{0,1:T(8,128)} %param.16) | copy-start | bytes 49156
  11.3 16.1 %all-to-all-start = ((bf16[8,64,512]{2,1,0:T(8,128)(2,1)}), bf16[8,64,512]{2,1,0:T(8,128)(2,1)S(1)}, u32[]{:S(2)}, u32[]{:S(2)}) async-start(bf16[8,64,512]{2,1,0:T(8,128)(2,1)} %bitcast.83), calls=%async_computation | async-start | bytes 1048576 | tf_op jit(solution)/shard_map/all_to_all | solution.py:95
  18.0 97.1 %all-gather.3.cloned.1.call-start = ((), (), s32[]{:S(2)}) async-start(), calls=%async_computation.5 | async-start | bytes 9437184 | tf_op jit(solution)/shard_map/all_gather | solution.py:131
  63.5 121.1 %reduce-scatter.2.cloned.1.call-start = ((), (), s32[]{:S(2)}) async-start(), calls=%async_computation.6 | async-start | bytes 9437184 | tf_op jit(solution)/shard_map/reduce_scatter | solution.py:16
  115.1 6.6 %copy-start.8 = (bf16[32,32,4096]{2,1,0:T(8,128)(2,1)S(1)}, bf16[32,32,4096]{2,1,0:T(8,128)(2,1)}, u32[]{:S(2)}) copy-start(bf16[32,32,4096]{2,1,0:T(8,128)(2,1)} %all-gather.3.cloned.1.call-done) | copy-start | bytes 25165828
  115.1 7.0 %copy-start.9 = (bf16[1,4096,256]{2,1,0:T(8,128)(2,1)S(1)}, bf16[1,4096,256]{2,1,0:T(8,128)(2,1)}, u32[]{:S(2)}) copy-start(bf16[1,4096,256]{2,1,0:T(8,128)(2,1)} %param.19) | copy-start | bytes 6291460
  130.2 2.0 copy-start.3
  184.6 34.7 %all-to-all-start.2 = ((bf16[32,32,512]{2,1,0:T(8,128)(2,1)}), bf16[32,32,512]{2,1,0:T(8,128)(2,1)S(1)}, u32[]{:S(2)}, u32[]{:S(2)}) async-start(bf16[32,32,512]{2,1,0:T(8,128)(2,1)} %reduce-scatter.2.cloned.1.call-done), calls=%async_computation.3 | async-start | bytes 2097152 | tf_op jit(solution)/shard_map/all_to_all | solution.py:19
  219.3 52.7 %copy-start.7 = (f32[512]{0:T(512)S(1)}, f32[512]{0:T(512)}, u32[]{:S(2)}) copy-start(f32[512]{0:T(512)} %param.22) | copy-start | bytes 6148
  235.3 17.6 %all-to-all-start.3 = ((bf16[8,64,512]{2,1,0:T(8,128)(2,1)}), bf16[8,64,512]{2,1,0:T(8,128)(2,1)S(1)}, u32[]{:S(2)}, u32[]{:S(2)}) async-start(bf16[8,64,512]{2,1,0:T(8,128)(2,1)} %convolution_convert_fusion.3), calls=%async_computation.4 | async-start | bytes 1048576 | tf_op jit(solution)/shard_map/all_to_all | solution.py:59
  253.8 19.0 %copy-start.1 = (bf16[64,512]{1,0:T(8,128)(2,1)}, bf16[64,512]{1,0:T(8,128)(2,1)S(1)}, u32[]{:S(2)}) copy-start(bf16[64,512]{1,0:T(8,128)(2,1)S(1)} %get-tuple-element.6) | copy-start | bytes 196612
Sparse Core Ops, SparseCore 0:
  63.6 51.5 all-gather.2
  130.4 54.1 reduce-scatter.1

commit v9 on v8

--- a/solution.py
+++ b/solution.py
@@ -36,10 +36,10 @@
     x_idx = lax.axis_index("ex")
     z_idx = lax.axis_index("ez")
     e_idx = x_idx * inner + z_idx
-    gathered = lax.all_gather(stream, "ex", axis=0, tiled=True)
+    gathered = lax.all_gather(stream, "ez", axis=0, tiled=True)
     dest = row_order // rows
     held = (
-        (jnp.arange(outer, dtype=jnp.int32)[:, None] * inner + z_idx) * rows
+        (x_idx * inner + jnp.arange(inner, dtype=jnp.int32)[:, None]) * rows
         + jnp.arange(rows, dtype=jnp.int32)[None, :]
     ).reshape(-1)
     held_dest = jnp.take(dest, held, axis=0)
@@ -47,26 +47,26 @@
     order = jnp.arange(count, dtype=jnp.int32)
     earlier = (held_dest[:, None] == held_dest[None, :]) & (order[None, :] < order[:, None])
     held_slot = jnp.sum(earlier.astype(jnp.int32), axis=1)
-    mine = (held_dest // inner) == x_idx
+    mine = (held_dest % inner) == z_idx
     pick = (
         mine[None, None, :]
-        & ((held_dest % inner)[None, None, :] == jnp.arange(inner, dtype=jnp.int32)[:, None, None])
+        & ((held_dest // inner)[None, None, :] == jnp.arange(outer, dtype=jnp.int32)[:, None, None])
         & (held_slot[None, None, :] == jnp.arange(rows, dtype=jnp.int32)[None, :, None])
     ).astype(jnp.bfloat16)
-    send = jnp.einsum("zkg,gf->zkf", pick, gathered, preferred_element_type=jnp.float32).astype(
+    send = jnp.einsum("xkg,gf->xkf", pick, gathered, preferred_element_type=jnp.float32).astype(
         jnp.bfloat16
     )
-    received = lax.all_to_all(send, "ez", split_axis=0, concat_axis=0, tiled=True)
+    received = lax.all_to_all(send, "ex", split_axis=0, concat_axis=0, tiled=True)
     arrival = jnp.arange(row_order.shape[0], dtype=jnp.int32)
-    column = (arrival // rows) % inner
-    source_column = (source // rows) % inner
+    column = arrival // (rows * inner)
+    source_column = source // (rows * inner)
     before = (
         (dest == e_idx)[None, :]
         & (column[None, :] == source_column[:, None])
         & (arrival[None, :] < source[:, None])
     )
     slot = jnp.sum(before.astype(jnp.int32), axis=1)
-    flat = received.reshape(inner * rows, received.shape[2])
+    flat = received.reshape(outer * rows, received.shape[2])
     return jnp.take(flat, source_column * rows + slot, axis=0)
 
 

time: 280 us -> 286 us (1.021)
  blocking collectives: 102 us -> 117 us
  waiting for transfers between devices: 103 us -> 95.4 us
    all_gather x1, blocking collectives: 9.74 us -> 20.2 us  [restore(): gathered = lax.all_gather(stream, 'ez', axis=0, tiled=True)]
    all_to_all x1, waiting for transfers between devices: 11.7 us -> 5.47 us  [restore(): lax.all_to_all(send, 'ex', split_axis=0, concat_axis=0, tiled=True)]
    psum x1, blocking collectives: 18.2 us -> 22.7 us  [final_norm(): square_total = lax.psum(jnp.sum(stream_f * stream_f, axis=1), 'tensor')]
  transfers between devices with their start and end apart: 5 -> 5, of which waited for: 5 -> 5; matrix products, arithmetic and copies ran while one was open for 3% -> 4% of each run, Pallas kernels for 0% -> 0%
where the time goes in v9:
time: 286 us
  blocking collectives  117 us (41%)
  waiting for transfers between devices  95.4 us (33%)
  matrix products  20 us (7%)
  starting transfers between devices  19.7 us (7%)
  between operations  14.4 us (5%)
  local copies, waits for them, and re-layouts  11.8 us (4%)
  other arithmetic  6.92 us (2%)
    reduce_scatter x1, waiting for transfers between devices, finish_slots(): lax.psum_scatter(partial_out.astype(jnp.bfloat16), 'tensor', scatter_dime...  48.5 us
    all_to_all x1, blocking collectives, on_device(): lax.all_to_all(outgoing, EXPERT, split_axis=0, concat_axis=0, tiled=True)  35.4 us
    all_to_all x1, waiting for transfers between devices, finish_slots(): lax.all_to_all(summed, EXPERT, split_axis=0, concat_axis=0, tiled=True)  24.1 us
    psum x1, blocking collectives, on_device(): slot_square = lax.psum(jnp.sum(part_f * part_f, axis=2), 'tensor')  23.4 us
    psum x1, blocking collectives, final_norm(): square_total = lax.psum(jnp.sum(stream_f * stream_f, axis=1), 'tensor')  22.7 us
    all_gather x1, blocking collectives, restore(): gathered = lax.all_gather(stream, 'ez', axis=0, tiled=True)  20.2 us
    all_gather x1, blocking collectives, on_device(): gain_full = lax.all_gather(norm_gain, 'tensor', axis=0, tiled=True)[:, None]  15.7 us
    all_gather x1, waiting for transfers between devices, on_device(): arrived = lax.all_gather(arrived_part, 'tensor', axis=2, tiled=True)  10.7 us
  transfers between devices with their start and end apart: 5, of which 5 were waited for; matrix products, arithmetic and copies ran while one was open for 4% of the time, Pallas kernels for 0%

profile of v9, /device:TPU:1, one launch (start us, length us, event | category | flops | bytes accessed | tf_op | source)
XLA Modules:
  0.0 285.6 jit_solution(4488465909218434587)
XLA Ops:
  7.2 3.2 %convolution_convert_fusion.1 = bf16[64,4096]{1,0:T(8,128)(2,1)S(1)} fusion(bf16[64,512]{1,0:T(8,128)(2,1)} %param.12, bf16[512,4096]{1,0:T(8,128)(2,1)} %param.14), kind=kOutput, calls=%fused_computation.6 | convolution fusion | flops 268697600 | bytes 4784128 | tf_op jit(solution)/shard_map/dot_general | solution.py:91
  10.4 0.8 copy.95
  11.3 6.7 %all-to-all-start = ((bf16[8,64,512]{2,1,0:T(8,128)(2,1)}), bf16[8,64,512]{2,1,0:T(8,128)(2,1)S(1)}, u32[]{:S(2)}, u32[]{:S(2)}) async-start(bf16[8,64,512]{2,1,0:T(8,128)(2,1)} %bitcast.81), calls=%async_computation | async-start | bytes 1048576 | tf_op jit(solution)/shard_map/all_to_all | solution.py:95
  18.1 0.2 convert_reduce_fusion.4
  18.4 1.2 select_reduce_fusion.1
  19.6 0.4 fusion.25
  20.1 0.1 copy.87
  20.2 0.6 gather_fusion.2
  20.8 6.5 %all-to-all-done = bf16[8,64,512]{2,1,0:T(8,128)(2,1)S(1)} async-done(((bf16[8,64,512]{2,1,0:T(8,128)(2,1)}), bf16[8,64,512]{2,1,0:T(8,128)(2,1)S(1)}, u32[]{:S(2)}, u32[]{:S(2)}) %all-to-all-start) | async-done | bytes 524320 | tf_op jit(solution)/shard_map/all_to_all | solution.py:95
  27.5 0.1 fusion.38
  27.6 0.5 convolution_convert_fusion.2
  28.1 35.4 %all_to_all.20 = bf16[32,32,512]{2,1,0:T(8,128)(2,1)} all-to-all(bf16[32,32,512]{2,1,0:T(8,128)(2,1)S(1)} %convolution_convert_fusion.2), channel_id=1, replica_groups=mesh['ex'=4,'ez'=8,'tensor'=8] {'ex','ez'}, dimensions={0} | all-to-all | bytes 2097152 | tf_op jit(solution)/shard_map/all_to_all | solution.py:130
  63.5 15.7 %all-gather = f32[8,1,512]{2,1,0:T(1,128)S(1)} all-gather(f32[1,1,512]{2,1,0:T(1,128)S(1)} %bitcast.88), channel_id=1, replica_groups=mesh['ex'=4,'ez'=8,'tensor'=8] {'tensor'}, dimensions={0}, use_global_device_ids=true | all-gather | bytes 18432 | tf_op jit(solution)/shard_map/all_gather | solution.py:135
  79.3 0.2 fusion.37
  79.5 1.5 multiply_reduce_fusion
  81.0 23.4 %all-reduce = (f32[32,32]{1,0:T(8,128)S(1)}, f32[64,8]{0,1:T(8,128)S(1)}, f32[64]{0:T(128)S(1)}) all-reduce(f32[32,32]{1,0:T(8,128)S(1)} %multiply_reduce_fusion, f32[64,8]{0,1:T(8,128)S(1)} %fusion.37, f32[64]{0:T(128)S(1)} %get-tuple-element.15), channel_id=1, replica_groups=mesh['ex'=4,'ez'=8,'tensor'=8] {'tensor'}, use_global_device_ids=true, to_apply=%region_13.14 | all-reduce | flops 1600 | bytes 12800 | tf_op jit(solution)/shard_map/psum | solution.py:133
  104.4 10.7 %all-gather.3.cloned.1.call-done = bf16[32,32,4096]{2,1,0:T(8,128)(2,1)} async-done(((bf16[32,32,512]{2,1,0:T(8,128)(2,1)}), bf16[32,32,4096]{2,1,0:T(8,128)(2,1)}) %all-gather.3.cloned.1.call-update) | async-done | bytes 8388624 | tf_op jit(solution)/shard_map/all_gather | solution.py:131
  115.1 6.6 %fusion.19 = f32[32,32,256]{2,1,0:T(8,128)S(1)} fusion(bf16[32,32,4096]{2,1,0:T(8,128)(2,1)} %all-gather.3.cloned.1.call-done, bf16[1,4096,256]{2,1,0:T(8,128)(2,1)} %param.18, f32[4096]{0:T(1024)S(1)} %bitcast.86, f32[32,32]{1,0:T(8,128)S(1)} %add_rsqrt_fusion), kind=kOutput, calls=%fused_computation.24 | convolution fusion | flops 2150891520 | bytes 11554816 | tf_op jit(solution)/shard_map/gmd,df->gmf/dot_general | solution.py:138
  121.7 0.4 copy-done.9
  122.1 2.5 fusion.22
  124.6 5.6 %convolution_convert_fusion = bf16[32,32,4096]{2,1,0:T(8,128)(2,1)} fusion(bf16[32,32,256]{2,1,0:T(8,128)(2,1)S(1)} %fusion.22, bf16[1,256,4096]{2,1,0:T(8,128)(2,1)S(1)} %copy-done), kind=kOutput, calls=%fused_computation.5 | convolution fusion | flops 2151677952 | bytes 11010048 | tf_op jit(solution)/shard_map/gmf,fd->gmd/dot_general | solution.py:15
  130.5 0.1 copy.83
  130.6 0.1 reshape.418
  130.8 0.1 select_reduce_fusion.2
  131.0 0.6 gather_fusion.1
  131.7 0.1 copy.88
  131.9 0.1 add.302
  132.0 0.1 copy.86
  132.2 3.1 %gather_fusion = s32[512]{0:T(512)S(1)} fusion(s32[2048]{0:T(1024)S(1)} %get-tuple-element.8, s32[1024]{0:T(1024)S(1)} %pad_clamp_fusion.4), kind=kCustom, calls=%fused_computation | custom fusion | bytes 6144 | tf_op jit(solution)/shard_map/jit(_take)/gather | solution.py:45
  135.4 0.2 select_reduce_fusion
  135.6 0.3 convert_reduce_fusion.3
  136.0 48.5 %reduce-scatter.2.cloned.1.call-done = bf16[32,32,512]{2,1,0:T(8,128)(2,1)} async-done(((bf16[32,32,4096]{2,1,0:T(8,128)(2,1)}), bf16[32,32,512]{2,1,0:T(8,128)(2,1)}) %reduce-scatter.2.cloned.1.call-update) | async-done | bytes 1048592 | tf_op jit(solution)/shard_map/reduce_scatter | solution.py:16
  184.5 9.5 %all-to-all-start.2 = ((bf16[32,32,512]{2,1,0:T(8,128)(2,1)}), bf16[32,32,512]{2,1,0:T(8,128)(2,1)S(1)}, u32[]{:S(2)}, u32[]{:S(2)}) async-start(bf16[32,32,512]{2,1,0:T(8,128)(2,1)} %reduce-scatter.2.cloned.1.call-done), calls=%async_computation.3 | async-start | bytes 2097152 | tf_op jit(solution)/shard_map/all_to_all | solution.py:19
  194.1 0.3 convert_reduce_fusion.2
  194.5 0.2 fusion.43
  195.1 24.1 %all-to-all-done.2 = bf16[32,32,512]{2,1,0:T(8,128)(2,1)S(1)} async-done(((bf16[32,32,512]{2,1,0:T(8,128)(2,1)}), bf16[32,32,512]{2,1,0:T(8,128)(2,1)S(1)}, u32[]{:S(2)}, u32[]{:S(2)}) %all-to-all-start.2) | async-done | bytes 1048608 | tf_op jit(solution)/shard_map/all_to_all | solution.py:19
  219.2 2.6 gather_fusion.3
  221.9 1.2 gather.26
  223.0 0.9 convert_reduce_fusion
  224.0 0.4 multiply_reduce_fusion.1
  224.4 20.2 %all_gather.11 = bf16[512,512]{1,0:T(8,128)(2,1)S(1)} all-gather(bf16[64,512]{1,0:T(8,128)(2,1)S(1)} %fusion.39), channel_id=1, replica_groups=mesh['ex'=4,'ez'=8,'tensor'=8] {'ez'}, dimensions={0}, use_global_device_ids=true | all-gather | bytes 589824 | tf_op jit(solution)/shard_map/all_gather | solution.py:39
  244.5 1.0 convolution_convert_fusion.3
  245.5 3.4 %all-to-all-start.3 = ((bf16[4,64,512]{2,1,0:T(8,128)(2,1)}), bf16[4,64,512]{2,1,0:T(8,128)(2,1)S(1)}, u32[]{:S(2)}, u32[]{:S(2)}) async-start(bf16[4,64,512]{2,1,0:T(8,128)(2,1)} %convolution_convert_fusion.3), calls=%async_computation.4 | async-start | bytes 524288 | tf_op jit(solution)/shard_map/all_to_all | solution.py:59
  249.0 5.5 %all-to-all-done.3 = bf16[4,64,512]{2,1,0:T(8,128)(2,1)S(1)} async-done(((bf16[4,64,512]{2,1,0:T(8,128)(2,1)}), bf16[4,64,512]{2,1,0:T(8,128)(2,1)S(1)}, u32[]{:S(2)}, u32[]{:S(2)}) %all-to-all-start.3) | async-done | bytes 262176 | tf_op jit(solution)/shard_map/all_to_all | solution.py:59
  254.4 0.7 gather_fusion.4
  255.1 0.2 fusion.34
  255.3 22.7 %psum.31 = f32[64]{0:T(128)S(1)} all-reduce(f32[64]{0:T(128)S(1)} %get-tuple-element.5), channel_id=1, replica_groups=mesh['ex'=4,'ez'=8,'tensor'=8] {'tensor'}, use_global_device_ids=true, to_apply=%region_18.19 | all-reduce | flops 64 | bytes 512 | tf_op jit(solution)/shard_map/psum | solution.py:24
  278.0 0.7 fusion.36
  (69 shorter events, 1.6 us)
Async XLA Ops:
  7.2 117.4 %copy-start = (bf16[1,256,4096]{2,1,0:T(8,128)(2,1)S(1)}, bf16[1,256,4096]{2,1,0:T(8,128)(2,1)}, u32[]{:S(2)}) copy-start(bf16[1,256,4096]{2,1,0:T(8,128)(2,1)} %param.20) | copy-start | bytes 6291460
  7.2 10.8 %copy-start.6 = (s32[64,2]{0,1:T(2,128)S(1)}, s32[64,2]{0,1:T(2,128)}, u32[]{:S(2)}) copy-start(s32[64,2]{0,1:T(2,128)} %param.17) | copy-start | bytes 1540
  7.2 13.0 %copy-start.10 = (s32[32]{0:T(128)S(1)}, s32[32]{0:T(128)}, u32[]{:S(2)}) copy-start(s32[32]{0:T(128)} %param.21) | copy-start | bytes 388
  7.2 20.2 %copy-start.2 = (bf16[64,512]{1,0:T(8,128)(2,1)S(1)}, bf16[64,512]{1,0:T(8,128)(2,1)}, u32[]{:S(2)}) copy-start(bf16[64,512]{1,0:T(8,128)(2,1)} %param.13) | copy-start | bytes 196612
  11.3 52.3 %copy-start.5 = (f32[512]{0:T(512)S(1)}, f32[512]{0:T(512)}, u32[]{:S(2)}) copy-start(f32[512]{0:T(512)} %param.15) | copy-start | bytes 6148
  11.3 68.0 %copy-start.4 = (f32[512,8]{0,1:T(8,128)S(1)}, f32[512,8]{0,1:T(8,128)}, u32[]{:S(2)}) copy-start(f32[512,8]{0,1:T(8,128)} %param.16) | copy-start | bytes 49156
  11.3 16.1 %all-to-all-start = ((bf16[8,64,512]{2,1,0:T(8,128)(2,1)}), bf16[8,64,512]{2,1,0:T(8,128)(2,1)S(1)}, u32[]{:S(2)}, u32[]{:S(2)}) async-start(bf16[8,64,512]{2,1,0:T(8,128)(2,1)} %bitcast.81), calls=%async_computation | async-start | bytes 1048576 | tf_op jit(solution)/shard_map/all_to_all | solution.py:95
  18.0 97.1 %all-gather.3.cloned.1.call-start = ((), (), s32[]{:S(2)}) async-start(), calls=%async_computation.5 | async-start | bytes 9437184 | tf_op jit(solution)/shard_map/all_gather | solution.py:131
  63.5 121.0 %reduce-scatter.2.cloned.1.call-start = ((), (), s32[]{:S(2)}) async-start(), calls=%async_computation.6 | async-start | bytes 9437184 | tf_op jit(solution)/shard_map/reduce_scatter | solution.py:16
  115.1 6.6 %copy-start.8 = (bf16[32,32,4096]{2,1,0:T(8,128)(2,1)S(1)}, bf16[32,32,4096]{2,1,0:T(8,128)(2,1)}, u32[]{:S(2)}) copy-start(bf16[32,32,4096]{2,1,0:T(8,128)(2,1)} %all-gather.3.cloned.1.call-done) | copy-start | bytes 25165828
  115.1 7.0 %copy-start.9 = (bf16[1,4096,256]{2,1,0:T(8,128)(2,1)S(1)}, bf16[1,4096,256]{2,1,0:T(8,128)(2,1)}, u32[]{:S(2)}) copy-start(bf16[1,4096,256]{2,1,0:T(8,128)(2,1)} %param.19) | copy-start | bytes 6291460
  130.2 2.0 copy-start.3
  184.5 34.7 %all-to-all-start.2 = ((bf16[32,32,512]{2,1,0:T(8,128)(2,1)}), bf16[32,32,512]{2,1,0:T(8,128)(2,1)S(1)}, u32[]{:S(2)}, u32[]{:S(2)}) async-start(bf16[32,32,512]{2,1,0:T(8,128)(2,1)} %reduce-scatter.2.cloned.1.call-done), calls=%async_computation.3 | async-start | bytes 2097152 | tf_op jit(solution)/shard_map/all_to_all | solution.py:19
  219.2 58.8 %copy-start.7 = (f32[512]{0:T(512)S(1)}, f32[512]{0:T(512)}, u32[]{:S(2)}) copy-start(f32[512]{0:T(512)} %param.22) | copy-start | bytes 6148
  245.5 8.9 %all-to-all-start.3 = ((bf16[4,64,512]{2,1,0:T(8,128)(2,1)}), bf16[4,64,512]{2,1,0:T(8,128)(2,1)S(1)}, u32[]{:S(2)}, u32[]{:S(2)}) async-start(bf16[4,64,512]{2,1,0:T(8,128)(2,1)} %convolution_convert_fusion.3), calls=%async_computation.4 | async-start | bytes 524288 | tf_op jit(solution)/shard_map/all_to_all | solution.py:59
  255.3 23.4 %copy-start.1 = (bf16[64,512]{1,0:T(8,128)(2,1)}, bf16[64,512]{1,0:T(8,128)(2,1)S(1)}, u32[]{:S(2)}) copy-start(bf16[64,512]{1,0:T(8,128)(2,1)S(1)} %get-tuple-element.6) | copy-start | bytes 196612
Sparse Core Ops, SparseCore 0:
  63.6 51.4 all-gather.2
  130.3 54.1 reduce-scatter.1

commit v10 on v8

--- a/solution.py
+++ b/solution.py
@@ -128,13 +128,12 @@
         "gsr,rd->gsd", send_map, stream_in, preferred_element_type=jnp.float32
     ).astype(jnp.bfloat16)
     arrived_part = lax.all_to_all(outgoing, EXPERT, split_axis=0, concat_axis=0, tiled=True)
-    arrived = lax.all_gather(arrived_part, "tensor", axis=2, tiled=True)
     part_f = arrived_part.astype(jnp.float32)
+    arrived = lax.all_gather((part_f * norm_gain).astype(jnp.bfloat16), "tensor", axis=2, tiled=True)
     slot_square = lax.psum(jnp.sum(part_f * part_f, axis=2), "tensor")
     slot_rms = lax.rsqrt(slot_square / D + EPS)[:, :, None]
-    gain_full = lax.all_gather(norm_gain, "tensor", axis=0, tiled=True)[:, None]
-    gate_weight = (w_gate[0].astype(jnp.float32) * gain_full).astype(jnp.bfloat16)
-    up_weight = (w_up[0].astype(jnp.float32) * gain_full).astype(jnp.bfloat16)
+    gate_weight = w_gate[0]
+    up_weight = w_up[0]
     gate_val = slot_rms * jnp.einsum(
         "gmd,df->gmf", arrived, gate_weight, preferred_element_type=jnp.float32
     )

time: 280 us -> 281 us (level)
  waiting for transfers between devices: 103 us -> 118 us
  blocking collectives: 102 us -> 88.8 us
    all_gather x1 -> x0, blocking collectives: 15.8 us -> none  [on_device(): gain_full = lax.all_gather(norm_gain, 'tensor', axis=0, tiled=True)[:, None]]
    all_gather x1, waiting for transfers between devices: 10.7 us -> 25.7 us  [on_device(): lax.all_gather((part_f * norm_gain).astype(jnp.bfloat16), 'tensor', axis=...]
where the time goes in v10:
time: 281 us; the launch traced here: 280 us
  waiting for transfers between devices  118 us (42%)
  blocking collectives  88.8 us (32%)
  starting transfers between devices  21.8 us (8%)
  matrix products  19.9 us (7%)
  between operations  14.4 us (5%)
  local copies, waits for them, and re-layouts  10.5 us (4%)
  other arithmetic  6.69 us (2%)
    reduce_scatter x1, waiting for transfers between devices, finish_slots(): lax.psum_scatter(partial_out.astype(jnp.bfloat16), 'tensor', scatter_dime...  50.3 us
    all_to_all x1, blocking collectives, on_device(): lax.all_to_all(outgoing, EXPERT, split_axis=0, concat_axis=0, tiled=True)  35.3 us
    all_gather x1, waiting for transfers between devices, on_device(): lax.all_gather((part_f * norm_gain).astype(jnp.bfloat16), 'tensor', axis=...  25.7 us
    psum x1, blocking collectives, on_device(): slot_square = lax.psum(jnp.sum(part_f * part_f, axis=2), 'tensor')  25.6 us
    all_to_all x1, waiting for transfers between devices, finish_slots(): lax.all_to_all(summed, EXPERT, split_axis=0, concat_axis=0, tiled=True)  24.2 us
    psum x1, blocking collectives, final_norm(): square_total = lax.psum(jnp.sum(stream_f * stream_f, axis=1), 'tensor')  18.2 us
    all_to_all x1, waiting for transfers between devices, restore(): lax.all_to_all(send, 'ez', split_axis=0, concat_axis=0, tiled=True)  11.7 us
    all_gather x1, blocking collectives, restore(): gathered = lax.all_gather(stream, 'ex', axis=0, tiled=True)  9.74 us
  transfers between devices with their start and end apart: 5, of which 5 were waited for; matrix products, arithmetic and copies ran while one was open for 3% of the time, Pallas kernels for 0%

profile of v10, /device:TPU:1, one launch (start us, length us, event | category | flops | bytes accessed | tf_op | source)
XLA Modules:
  0.0 280.5 jit_solution(4654078834163454598)
XLA Ops:
  7.2 3.2 %convolution_convert_fusion.1 = bf16[64,4096]{1,0:T(8,128)(2,1)S(1)} fusion(bf16[64,512]{1,0:T(8,128)(2,1)} %param.12, bf16[512,4096]{1,0:T(8,128)(2,1)} %param.14), kind=kOutput, calls=%fused_computation.6 | convolution fusion | flops 268697600 | bytes 4784128 | tf_op jit(solution)/shard_map/dot_general | solution.py:91
  10.4 0.8 copy.95
  11.3 6.7 %all-to-all-start = ((bf16[8,64,512]{2,1,0:T(8,128)(2,1)}), bf16[8,64,512]{2,1,0:T(8,128)(2,1)S(1)}, u32[]{:S(2)}, u32[]{:S(2)}) async-start(bf16[8,64,512]{2,1,0:T(8,128)(2,1)} %bitcast.63), calls=%async_computation | async-start | bytes 1048576 | tf_op jit(solution)/shard_map/all_to_all | solution.py:95
  18.0 0.1 copy.78
  18.1 0.2 convert_reduce_fusion.4
  18.4 1.2 select_reduce_fusion.1
  19.6 0.4 fusion.19
  20.1 0.1 copy.87
  20.2 0.6 gather_fusion.2
  20.9 6.5 %all-to-all-done = bf16[8,64,512]{2,1,0:T(8,128)(2,1)S(1)} async-done(((bf16[8,64,512]{2,1,0:T(8,128)(2,1)}), bf16[8,64,512]{2,1,0:T(8,128)(2,1)S(1)}, u32[]{:S(2)}, u32[]{:S(2)}) %all-to-all-start) | async-done | bytes 524320 | tf_op jit(solution)/shard_map/all_to_all | solution.py:95
  27.4 0.1 fusion.32
  27.6 0.5 convolution_convert_fusion.2
  28.0 35.3 %all_to_all.20 = bf16[32,32,512]{2,1,0:T(8,128)(2,1)S(1)} all-to-all(bf16[32,32,512]{2,1,0:T(8,128)(2,1)S(1)} %convolution_convert_fusion.2), channel_id=1, replica_groups=mesh['ex'=4,'ez'=8,'tensor'=8] {'ex','ez'}, dimensions={0} | all-to-all | bytes 2097152 | tf_op jit(solution)/shard_map/all_to_all | solution.py:130
  63.3 1.4 fusion
  64.8 0.2 fusion.31
  65.0 25.6 %all-reduce = (f32[32,32]{1,0:T(8,128)S(1)}, f32[64,8]{0,1:T(8,128)S(1)}, f32[64]{0:T(128)S(1)}) all-reduce(f32[32,32]{1,0:T(8,128)S(1)} %get-tuple-element.19, f32[64,8]{0,1:T(8,128)S(1)} %fusion.31, f32[64]{0:T(128)S(1)} %get-tuple-element.15), channel_id=1, replica_groups=mesh['ex'=4,'ez'=8,'tensor'=8] {'tensor'}, use_global_device_ids=true, to_apply=%region_13.14 | all-reduce | flops 1600 | bytes 12800 | tf_op jit(solution)/shard_map/psum | solution.py:133
  90.6 25.7 %all-gather.2.cloned.1.call-done = bf16[32,32,4096]{2,1,0:T(8,128)(2,1)} async-done(((bf16[32,32,512]{2,1,0:T(8,128)(2,1)}), bf16[32,32,4096]{2,1,0:T(8,128)(2,1)}) %all-gather.2.cloned.1.call-update) | async-done | bytes 8388624 | tf_op jit(solution)/shard_map/all_gather | solution.py:132
  116.2 6.5 %fusion.7 = f32[32,32,256]{2,1,0:T(8,128)S(1)} fusion(bf16[32,32,4096]{2,1,0:T(8,128)(2,1)} %all-gather.2.cloned.1.call-done, bf16[1,4096,256]{2,1,0:T(8,128)(2,1)} %param.18, f32[32,32]{1,0:T(8,128)S(1)} %add_rsqrt_fusion), kind=kOutput, calls=%fused_computation.17 | convolution fusion | flops 2147745792 | bytes 11538432 | tf_op jit(solution)/shard_map/gmd,df->gmf/dot_general | solution.py:137
  122.7 0.5 copy-done.9
  123.2 2.4 fusion.16
  125.6 5.6 %convolution_convert_fusion = bf16[32,32,4096]{2,1,0:T(8,128)(2,1)} fusion(bf16[32,32,256]{2,1,0:T(8,128)(2,1)S(1)} %fusion.16, bf16[1,256,4096]{2,1,0:T(8,128)(2,1)S(1)} %copy-done), kind=kOutput, calls=%fused_computation.5 | convolution fusion | flops 2151677952 | bytes 11010048 | tf_op jit(solution)/shard_map/gmf,fd->gmd/dot_general | solution.py:15
  131.6 0.1 copy.83
  131.7 0.1 reshape.458
  131.8 0.1 select_reduce_fusion.2
  132.0 0.6 gather_fusion.1
  132.8 0.1 copy.88
  132.9 0.1 add.334
  133.0 0.1 copy.86
  133.3 1.7 gather_fusion
  135.0 0.2 convert_reduce_fusion.3
  135.2 50.3 %reduce-scatter.2.cloned.1.call-done = bf16[32,32,512]{2,1,0:T(8,128)(2,1)} async-done(((bf16[32,32,4096]{2,1,0:T(8,128)(2,1)}), bf16[32,32,512]{2,1,0:T(8,128)(2,1)}) %reduce-scatter.2.cloned.1.call-update) | async-done | bytes 1048592 | tf_op jit(solution)/shard_map/reduce_scatter | solution.py:16
  185.5 9.5 %all-to-all-start.2 = ((bf16[32,32,512]{2,1,0:T(8,128)(2,1)}), bf16[32,32,512]{2,1,0:T(8,128)(2,1)S(1)}, u32[]{:S(2)}, u32[]{:S(2)}) async-start(bf16[32,32,512]{2,1,0:T(8,128)(2,1)} %reduce-scatter.2.cloned.1.call-done), calls=%async_computation.3 | async-start | bytes 2097152 | tf_op jit(solution)/shard_map/all_to_all | solution.py:19
  195.0 0.2 select_reduce_fusion
  195.4 0.2 fusion.37
  196.0 24.2 %all-to-all-done.2 = bf16[32,32,512]{2,1,0:T(8,128)(2,1)S(1)} async-done(((bf16[32,32,512]{2,1,0:T(8,128)(2,1)}), bf16[32,32,512]{2,1,0:T(8,128)(2,1)S(1)}, u32[]{:S(2)}, u32[]{:S(2)}) %all-to-all-start.2) | async-done | bytes 1048608 | tf_op jit(solution)/shard_map/all_to_all | solution.py:19
  220.2 2.6 gather_fusion.3
  222.8 1.2 gather.26
  224.0 0.9 convert_reduce_fusion
  224.9 0.4 multiply_reduce_fusion
  225.3 9.7 %all_gather.7 = bf16[256,512]{1,0:T(8,128)(2,1)S(1)} all-gather(bf16[64,512]{1,0:T(8,128)(2,1)S(1)} %fusion.33), channel_id=1, replica_groups=mesh['ex'=4,'ez'=8,'tensor'=8] {'ex'}, dimensions={0}, use_global_device_ids=true | all-gather | bytes 327680 | tf_op jit(solution)/shard_map/all_gather | solution.py:39
  235.1 1.1 convolution_convert_fusion.3
  236.2 5.5 %all-to-all-start.3 = ((bf16[8,64,512]{2,1,0:T(8,128)(2,1)}), bf16[8,64,512]{2,1,0:T(8,128)(2,1)S(1)}, u32[]{:S(2)}, u32[]{:S(2)}) async-start(bf16[8,64,512]{2,1,0:T(8,128)(2,1)} %convolution_convert_fusion.3), calls=%async_computation.4 | async-start | bytes 1048576 | tf_op jit(solution)/shard_map/all_to_all | solution.py:59
  241.8 0.3 convert_reduce_fusion.2
  242.1 11.7 %all-to-all-done.3 = bf16[8,64,512]{2,1,0:T(8,128)(2,1)S(1)} async-done(((bf16[8,64,512]{2,1,0:T(8,128)(2,1)}), bf16[8,64,512]{2,1,0:T(8,128)(2,1)S(1)}, u32[]{:S(2)}, u32[]{:S(2)}) %all-to-all-start.3) | async-done | bytes 524320 | tf_op jit(solution)/shard_map/all_to_all | solution.py:59
  253.8 0.7 gather_fusion.4
  254.5 0.2 fusion.28
  254.7 18.2 %psum.31 = f32[64]{0:T(128)S(1)} all-reduce(f32[64]{0:T(128)S(1)} %get-tuple-element.5), channel_id=1, replica_groups=mesh['ex'=4,'ez'=8,'tensor'=8] {'tensor'}, use_global_device_ids=true, to_apply=%region_18.19 | all-reduce | flops 64 | bytes 512 | tf_op jit(solution)/shard_map/psum | solution.py:24
  272.9 0.7 fusion.30
  (68 shorter events, 1.5 us)
Async XLA Ops:
  7.2 118.5 %copy-start = (bf16[1,256,4096]{2,1,0:T(8,128)(2,1)S(1)}, bf16[1,256,4096]{2,1,0:T(8,128)(2,1)}, u32[]{:S(2)}) copy-start(bf16[1,256,4096]{2,1,0:T(8,128)(2,1)} %param.20) | copy-start | bytes 6291460
  10.4 7.6 %copy-start.6 = (s32[64,2]{0,1:T(2,128)S(1)}, s32[64,2]{0,1:T(2,128)}, u32[]{:S(2)}) copy-start(s32[64,2]{0,1:T(2,128)} %param.17) | copy-start | bytes 1540
  10.4 9.8 %copy-start.10 = (s32[32]{0:T(128)S(1)}, s32[32]{0:T(128)}, u32[]{:S(2)}) copy-start(s32[32]{0:T(128)} %param.21) | copy-start | bytes 388
  11.3 16.2 %copy-start.2 = (bf16[64,512]{1,0:T(8,128)(2,1)S(1)}, bf16[64,512]{1,0:T(8,128)(2,1)}, u32[]{:S(2)}) copy-start(bf16[64,512]{1,0:T(8,128)(2,1)} %param.13) | copy-start | bytes 196612
  11.3 16.1 %all-to-all-start = ((bf16[8,64,512]{2,1,0:T(8,128)(2,1)}), bf16[8,64,512]{2,1,0:T(8,128)(2,1)S(1)}, u32[]{:S(2)}, u32[]{:S(2)}) async-start(bf16[8,64,512]{2,1,0:T(8,128)(2,1)} %bitcast.63), calls=%async_computation | async-start | bytes 1048576 | tf_op jit(solution)/shard_map/all_to_all | solution.py:95
  18.0 98.3 %all-gather.2.cloned.1.call-start = ((), (), s32[]{:S(2)}) async-start(), calls=%async_computation.5 | async-start | bytes 9437184 | tf_op jit(solution)/shard_map/all_gather | solution.py:132
  20.8 42.5 %copy-start.5 = (f32[512]{0:T(512)S(1)}, f32[512]{0:T(512)}, u32[]{:S(2)}) copy-start(f32[512]{0:T(512)} %param.15) | copy-start | bytes 6148
  63.3 1.4 copy-start.4
  64.7 120.8 %reduce-scatter.2.cloned.1.call-start = ((), (), s32[]{:S(2)}) async-start(), calls=%async_computation.6 | async-start | bytes 9437184 | tf_op jit(solution)/shard_map/reduce_scatter | solution.py:16
  116.2 6.5 %copy-start.8 = (bf16[32,32,4096]{2,1,0:T(8,128)(2,1)S(1)}, bf16[32,32,4096]{2,1,0:T(8,128)(2,1)}, u32[]{:S(2)}) copy-start(bf16[32,32,4096]{2,1,0:T(8,128)(2,1)} %all-gather.2.cloned.1.call-done) | copy-start | bytes 25165828
  116.2 7.0 %copy-start.9 = (bf16[1,4096,256]{2,1,0:T(8,128)(2,1)S(1)}, bf16[1,4096,256]{2,1,0:T(8,128)(2,1)}, u32[]{:S(2)}) copy-start(bf16[1,4096,256]{2,1,0:T(8,128)(2,1)} %param.19) | copy-start | bytes 6291460
  131.2 2.0 copy-start.3
  185.5 34.7 %all-to-all-start.2 = ((bf16[32,32,512]{2,1,0:T(8,128)(2,1)}), bf16[32,32,512]{2,1,0:T(8,128)(2,1)S(1)}, u32[]{:S(2)}, u32[]{:S(2)}) async-start(bf16[32,32,512]{2,1,0:T(8,128)(2,1)} %reduce-scatter.2.cloned.1.call-done), calls=%async_computation.3 | async-start | bytes 2097152 | tf_op jit(solution)/shard_map/all_to_all | solution.py:19
  224.0 48.9 %copy-start.7 = (f32[512]{0:T(512)S(1)}, f32[512]{0:T(512)}, u32[]{:S(2)}) copy-start(f32[512]{0:T(512)} %param.22) | copy-start | bytes 6148
  236.2 17.6 %all-to-all-start.3 = ((bf16[8,64,512]{2,1,0:T(8,128)(2,1)}), bf16[8,64,512]{2,1,0:T(8,128)(2,1)S(1)}, u32[]{:S(2)}, u32[]{:S(2)}) async-start(bf16[8,64,512]{2,1,0:T(8,128)(2,1)} %convolution_convert_fusion.3), calls=%async_computation.4 | async-start | bytes 1048576 | tf_op jit(solution)/shard_map/all_to_all | solution.py:59
  254.7 19.0 %copy-start.1 = (bf16[64,512]{1,0:T(8,128)(2,1)}, bf16[64,512]{1,0:T(8,128)(2,1)S(1)}, u32[]{:S(2)}) copy-start(bf16[64,512]{1,0:T(8,128)(2,1)S(1)} %get-tuple-element.6) | copy-start | bytes 196612
Sparse Core Ops, SparseCore 0:
  64.8 51.3 all-gather.1
  131.4 54.0 reduce-scatter.1

commit v11 on v8

--- a/solution.py
+++ b/solution.py
@@ -36,7 +36,10 @@
     x_idx = lax.axis_index("ex")
     z_idx = lax.axis_index("ez")
     e_idx = x_idx * inner + z_idx
-    gathered = lax.all_gather(stream, "ex", axis=0, tiled=True)
+    copies = jnp.broadcast_to(stream[None], (outer,) + stream.shape)
+    gathered = lax.all_to_all(copies, "ex", split_axis=0, concat_axis=0, tiled=True).reshape(
+        outer * rows, stream.shape[1]
+    )
     dest = row_order // rows
     held = (
         (jnp.arange(outer, dtype=jnp.int32)[:, None] * inner + z_idx) * rows

time: 280 us -> 280 us (level)
  blocking collectives: 102 us -> 90.5 us
  waiting for transfers between devices: 103 us -> 111 us
  starting transfers between devices: 21.9 us -> 25.7 us
    all_gather x1 -> x0, blocking collectives: 9.74 us -> none  [restore(): gathered = lax.all_gather(stream, 'ex', axis=0, tiled=True)]
    all_to_all x0 -> x1, waiting for transfers between devices: none -> 5.48 us  [restore(): lax.all_to_all(copies, 'ex', split_axis=0, concat_axis=0, tiled=True)]
    all_to_all x0 -> x1, starting transfers between devices: none -> 3.4 us  [restore(): lax.all_to_all(copies, 'ex', split_axis=0, concat_axis=0, tiled=True)]
  transfers between devices with their start and end apart: 5 -> 6, of which waited for: 5 -> 6; matrix products, arithmetic and copies ran while one was open for 3% -> 3% of each run, Pallas kernels for 0% -> 0%
where the time goes in v11:
time: 280 us
  waiting for transfers between devices  111 us (40%)
  blocking collectives  90.5 us (32%)
  starting transfers between devices  25.7 us (9%)
  matrix products  20.1 us (7%)
  between operations  14.4 us (5%)
  local copies, waits for them, and re-layouts  11.1 us (4%)
  other arithmetic  6.87 us (2%)
    reduce_scatter x1, waiting for transfers between devices, finish_slots(): lax.psum_scatter(partial_out.astype(jnp.bfloat16), 'tensor', scatter_dime...  50.5 us
    all_to_all x1, blocking collectives, on_device(): lax.all_to_all(outgoing, EXPERT, split_axis=0, concat_axis=0, tiled=True)  35.4 us
    all_to_all x1, waiting for transfers between devices, finish_slots(): lax.all_to_all(summed, EXPERT, split_axis=0, concat_axis=0, tiled=True)  24 us
    psum x1, blocking collectives, on_device(): slot_square = lax.psum(jnp.sum(part_f * part_f, axis=2), 'tensor')  23.4 us
    psum x1, blocking collectives, final_norm(): square_total = lax.psum(jnp.sum(stream_f * stream_f, axis=1), 'tensor')  16 us
    all_gather x1, blocking collectives, on_device(): gain_full = lax.all_gather(norm_gain, 'tensor', axis=0, tiled=True)[:, None]  15.8 us
    all_to_all x1, waiting for transfers between devices, restore(): lax.all_to_all(send, 'ez', split_axis=0, concat_axis=0, tiled=True)  13.9 us
    all_gather x1, waiting for transfers between devices, on_device(): arrived = lax.all_gather(arrived_part, 'tensor', axis=2, tiled=True)  10.7 us
  transfers between devices with their start and end apart: 6, of which 6 were waited for; matrix products, arithmetic and copies ran while one was open for 3% of the time, Pallas kernels for 0%

profile of v11, /device:TPU:1, one launch (start us, length us, event | category | flops | bytes accessed | tf_op | source)
XLA Modules:
  0.0 279.8 jit_solution(15356213727412492276)
XLA Ops:
  7.2 3.2 %convolution_convert_fusion.1 = bf16[64,4096]{1,0:T(8,128)(2,1)S(1)} fusion(bf16[64,512]{1,0:T(8,128)(2,1)} %param.12, bf16[512,4096]{1,0:T(8,128)(2,1)} %param.14), kind=kOutput, calls=%fused_computation.6 | convolution fusion | flops 268697600 | bytes 4784128 | tf_op jit(solution)/shard_map/dot_general | solution.py:94
  10.4 0.8 copy.95
  11.3 6.7 %all-to-all-start = ((bf16[8,64,512]{2,1,0:T(8,128)(2,1)}), bf16[8,64,512]{2,1,0:T(8,128)(2,1)S(1)}, u32[]{:S(2)}, u32[]{:S(2)}) async-start(bf16[8,64,512]{2,1,0:T(8,128)(2,1)} %bitcast.84), calls=%async_computation | async-start | bytes 1048576 | tf_op jit(solution)/shard_map/all_to_all | solution.py:98
  18.1 0.2 convert_reduce_fusion.4
  18.4 1.2 select_reduce_fusion.1
  19.6 0.4 fusion.25
  20.1 0.1 copy.87
  20.2 0.6 gather_fusion.2
  20.8 6.5 %all-to-all-done = bf16[8,64,512]{2,1,0:T(8,128)(2,1)S(1)} async-done(((bf16[8,64,512]{2,1,0:T(8,128)(2,1)}), bf16[8,64,512]{2,1,0:T(8,128)(2,1)S(1)}, u32[]{:S(2)}, u32[]{:S(2)}) %all-to-all-start) | async-done | bytes 524320 | tf_op jit(solution)/shard_map/all_to_all | solution.py:98
  27.5 0.1 fusion.37
  27.6 0.5 convolution_convert_fusion.2
  28.1 35.4 %all_to_all.25 = bf16[32,32,512]{2,1,0:T(8,128)(2,1)} all-to-all(bf16[32,32,512]{2,1,0:T(8,128)(2,1)S(1)} %convolution_convert_fusion.2), channel_id=1, replica_groups=mesh['ex'=4,'ez'=8,'tensor'=8] {'ex','ez'}, dimensions={0} | all-to-all | bytes 2097152 | tf_op jit(solution)/shard_map/all_to_all | solution.py:133
  63.5 15.8 %all-gather = f32[8,1,512]{2,1,0:T(1,128)S(1)} all-gather(f32[1,1,512]{2,1,0:T(1,128)S(1)} %bitcast.92), channel_id=1, replica_groups=mesh['ex'=4,'ez'=8,'tensor'=8] {'tensor'}, dimensions={0}, use_global_device_ids=true | all-gather | bytes 18432 | tf_op jit(solution)/shard_map/all_gather | solution.py:138
  79.3 0.2 fusion.36
  79.5 1.5 multiply_reduce_fusion
  81.0 23.4 %all-reduce = (f32[32,32]{1,0:T(8,128)S(1)}, f32[64,8]{0,1:T(8,128)S(1)}, f32[64]{0:T(128)S(1)}) all-reduce(f32[32,32]{1,0:T(8,128)S(1)} %multiply_reduce_fusion, f32[64,8]{0,1:T(8,128)S(1)} %fusion.36, f32[64]{0:T(128)S(1)} %get-tuple-element.15), channel_id=1, replica_groups=mesh['ex'=4,'ez'=8,'tensor'=8] {'tensor'}, use_global_device_ids=true, to_apply=%region_13.14 | all-reduce | flops 1600 | bytes 12800 | tf_op jit(solution)/shard_map/psum | solution.py:136
  104.4 10.7 %all-gather.3.cloned.1.call-done = bf16[32,32,4096]{2,1,0:T(8,128)(2,1)} async-done(((bf16[32,32,512]{2,1,0:T(8,128)(2,1)}), bf16[32,32,4096]{2,1,0:T(8,128)(2,1)}) %all-gather.3.cloned.1.call-update) | async-done | bytes 8388624 | tf_op jit(solution)/shard_map/all_gather | solution.py:134
  115.1 6.6 %fusion.19 = f32[32,32,256]{2,1,0:T(8,128)S(1)} fusion(bf16[32,32,4096]{2,1,0:T(8,128)(2,1)} %all-gather.3.cloned.1.call-done, bf16[1,4096,256]{2,1,0:T(8,128)(2,1)} %param.18, f32[4096]{0:T(1024)S(1)} %bitcast.90, f32[32,32]{1,0:T(8,128)S(1)} %add_rsqrt_fusion), kind=kOutput, calls=%fused_computation.24 | convolution fusion | flops 2150891520 | bytes 11554816 | tf_op jit(solution)/shard_map/gmd,df->gmf/dot_general | solution.py:141
  121.7 0.4 copy-done.9
  122.1 2.5 fusion.22
  124.6 5.6 %convolution_convert_fusion = bf16[32,32,4096]{2,1,0:T(8,128)(2,1)} fusion(bf16[32,32,256]{2,1,0:T(8,128)(2,1)S(1)} %fusion.22, bf16[1,256,4096]{2,1,0:T(8,128)(2,1)S(1)} %copy-done), kind=kOutput, calls=%fused_computation.5 | convolution fusion | flops 2151677952 | bytes 11010048 | tf_op jit(solution)/shard_map/gmf,fd->gmd/dot_general | solution.py:15
  130.7 0.1 reshape.469
  131.0 0.6 gather_fusion.1
  131.8 0.1 copy.88
  131.9 0.1 add.334
  132.1 0.1 copy.86
  132.3 1.7 gather_fusion
  134.0 50.5 %reduce-scatter.2.cloned.1.call-done = bf16[32,32,512]{2,1,0:T(8,128)(2,1)} async-done(((bf16[32,32,4096]{2,1,0:T(8,128)(2,1)}), bf16[32,32,512]{2,1,0:T(8,128)(2,1)}) %reduce-scatter.2.cloned.1.call-update) | async-done | bytes 1048592 | tf_op jit(solution)/shard_map/reduce_scatter | solution.py:16
  184.6 9.5 %all-to-all-start.2 = ((bf16[32,32,512]{2,1,0:T(8,128)(2,1)}), bf16[32,32,512]{2,1,0:T(8,128)(2,1)S(1)}, u32[]{:S(2)}, u32[]{:S(2)}) async-start(bf16[32,32,512]{2,1,0:T(8,128)(2,1)} %reduce-scatter.2.cloned.1.call-done), calls=%async_computation.3 | async-start | bytes 2097152 | tf_op jit(solution)/shard_map/all_to_all | solution.py:19
  194.1 0.2 convert_reduce_fusion.3
  194.3 0.2 select_reduce_fusion
  194.7 0.2 fusion.42
  195.3 24.0 %all-to-all-done.2 = bf16[32,32,512]{2,1,0:T(8,128)(2,1)S(1)} async-done(((bf16[32,32,512]{2,1,0:T(8,128)(2,1)}), bf16[32,32,512]{2,1,0:T(8,128)(2,1)S(1)}, u32[]{:S(2)}, u32[]{:S(2)}) %all-to-all-start.2) | async-done | bytes 1048608 | tf_op jit(solution)/shard_map/all_to_all | solution.py:19
  219.3 2.6 gather_fusion.3
  221.9 1.2 gather.26
  223.1 0.9 convert_reduce_fusion
  224.0 0.4 multiply_reduce_fusion.1
  224.4 0.7 broadcast_in_dim.59
  225.2 3.4 %all-to-all-start.3 = ((bf16[4,64,512]{2,1,0:T(8,128)(2,1)}), bf16[4,64,512]{2,1,0:T(8,128)(2,1)S(1)}, u32[]{:S(2)}, u32[]{:S(2)}) async-start(bf16[4,64,512]{2,1,0:T(8,128)(2,1)} %broadcast_in_dim.59), calls=%async_computation.4 | async-start | bytes 524288 | tf_op jit(solution)/shard_map/all_to_all | solution.py:40
  228.6 5.5 %all-to-all-done.3 = bf16[4,64,512]{2,1,0:T(8,128)(2,1)S(1)} async-done(((bf16[4,64,512]{2,1,0:T(8,128)(2,1)}), bf16[4,64,512]{2,1,0:T(8,128)(2,1)S(1)}, u32[]{:S(2)}, u32[]{:S(2)}) %all-to-all-start.3) | async-done | bytes 262176 | tf_op jit(solution)/shard_map/all_to_all | solution.py:40
  234.1 1.1 convolution_convert_fusion.3
  235.2 6.0 %all-to-all-start.4 = ((bf16[8,64,512]{2,1,0:T(8,128)(2,1)}), bf16[8,64,512]{2,1,0:T(8,128)(2,1)S(1)}, u32[]{:S(2)}, u32[]{:S(2)}) async-start(bf16[8,64,512]{2,1,0:T(8,128)(2,1)} %convolution_convert_fusion.3), calls=%async_computation.5 | async-start | bytes 1048576 | tf_op jit(solution)/shard_map/all_to_all | solution.py:62
  241.2 0.3 convert_reduce_fusion.2
  241.5 13.9 %all-to-all-done.4 = bf16[8,64,512]{2,1,0:T(8,128)(2,1)S(1)} async-done(((bf16[8,64,512]{2,1,0:T(8,128)(2,1)}), bf16[8,64,512]{2,1,0:T(8,128)(2,1)S(1)}, u32[]{:S(2)}, u32[]{:S(2)}) %all-to-all-start.4) | async-done | bytes 524320 | tf_op jit(solution)/shard_map/all_to_all | solution.py:62
  255.4 0.7 gather_fusion.4
  256.1 0.2 fusion.33
  256.3 16.0 %psum.31 = f32[64]{0:T(128)S(1)} all-reduce(f32[64]{0:T(128)S(1)} %get-tuple-element.5), channel_id=1, replica_groups=mesh['ex'=4,'ez'=8,'tensor'=8] {'tensor'}, use_global_device_ids=true, to_apply=%region_18.19 | all-reduce | flops 64 | bytes 512 | tf_op jit(solution)/shard_map/psum | solution.py:24
  272.3 0.7 fusion.35
  (71 shorter events, 1.8 us)
Async XLA Ops:
  7.2 117.5 %copy-start = (bf16[1,256,4096]{2,1,0:T(8,128)(2,1)S(1)}, bf16[1,256,4096]{2,1,0:T(8,128)(2,1)}, u32[]{:S(2)}) copy-start(bf16[1,256,4096]{2,1,0:T(8,128)(2,1)} %param.20) | copy-start | bytes 6291460
  7.2 10.8 %copy-start.6 = (s32[64,2]{0,1:T(2,128)S(1)}, s32[64,2]{0,1:T(2,128)}, u32[]{:S(2)}) copy-start(s32[64,2]{0,1:T(2,128)} %param.17) | copy-start | bytes 1540
  7.2 13.0 %copy-start.10 = (s32[32]{0:T(128)S(1)}, s32[32]{0:T(128)}, u32[]{:S(2)}) copy-start(s32[32]{0:T(128)} %param.21) | copy-start | bytes 388
  7.2 20.2 %copy-start.2 = (bf16[64,512]{1,0:T(8,128)(2,1)S(1)}, bf16[64,512]{1,0:T(8,128)(2,1)}, u32[]{:S(2)}) copy-start(bf16[64,512]{1,0:T(8,128)(2,1)} %param.13) | copy-start | bytes 196612
  11.3 52.2 %copy-start.5 = (f32[512]{0:T(512)S(1)}, f32[512]{0:T(512)}, u32[]{:S(2)}) copy-start(f32[512]{0:T(512)} %param.15) | copy-start | bytes 6148
  11.3 68.0 %copy-start.4 = (f32[512,8]{0,1:T(8,128)S(1)}, f32[512,8]{0,1:T(8,128)}, u32[]{:S(2)}) copy-start(f32[512,8]{0,1:T(8,128)} %param.16) | copy-start | bytes 49156
  11.3 16.1 %all-to-all-start = ((bf16[8,64,512]{2,1,0:T(8,128)(2,1)}), bf16[8,64,512]{2,1,0:T(8,128)(2,1)S(1)}, u32[]{:S(2)}, u32[]{:S(2)}) async-start(bf16[8,64,512]{2,1,0:T(8,128)(2,1)} %bitcast.84), calls=%async_computation | async-start | bytes 1048576 | tf_op jit(solution)/shard_map/all_to_all | solution.py:98
  18.0 97.1 %all-gather.3.cloned.1.call-start = ((), (), s32[]{:S(2)}) async-start(), calls=%async_computation.6 | async-start | bytes 9437184 | tf_op jit(solution)/shard_map/all_gather | solution.py:134
  63.5 121.1 %reduce-scatter.2.cloned.1.call-start = ((), (), s32[]{:S(2)}) async-start(), calls=%async_computation.7 | async-start | bytes 9437184 | tf_op jit(solution)/shard_map/reduce_scatter | solution.py:16
  115.1 6.6 %copy-start.8 = (bf16[32,32,4096]{2,1,0:T(8,128)(2,1)S(1)}, bf16[32,32,4096]{2,1,0:T(8,128)(2,1)}, u32[]{:S(2)}) copy-start(bf16[32,32,4096]{2,1,0:T(8,128)(2,1)} %all-gather.3.cloned.1.call-done) | copy-start | bytes 25165828
  115.1 7.0 %copy-start.9 = (bf16[1,4096,256]{2,1,0:T(8,128)(2,1)S(1)}, bf16[1,4096,256]{2,1,0:T(8,128)(2,1)}, u32[]{:S(2)}) copy-start(bf16[1,4096,256]{2,1,0:T(8,128)(2,1)} %param.19) | copy-start | bytes 6291460
  130.2 2.0 copy-start.3
  184.6 34.7 %all-to-all-start.2 = ((bf16[32,32,512]{2,1,0:T(8,128)(2,1)}), bf16[32,32,512]{2,1,0:T(8,128)(2,1)S(1)}, u32[]{:S(2)}, u32[]{:S(2)}) async-start(bf16[32,32,512]{2,1,0:T(8,128)(2,1)} %reduce-scatter.2.cloned.1.call-done), calls=%async_computation.3 | async-start | bytes 2097152 | tf_op jit(solution)/shard_map/all_to_all | solution.py:19
  221.9 50.4 %copy-start.7 = (f32[512]{0:T(512)S(1)}, f32[512]{0:T(512)}, u32[]{:S(2)}) copy-start(f32[512]{0:T(512)} %param.22) | copy-start | bytes 6148
  225.2 8.9 %all-to-all-start.3 = ((bf16[4,64,512]{2,1,0:T(8,128)(2,1)}), bf16[4,64,512]{2,1,0:T(8,128)(2,1)S(1)}, u32[]{:S(2)}, u32[]{:S(2)}) async-start(bf16[4,64,512]{2,1,0:T(8,128)(2,1)} %broadcast_in_dim.59), calls=%async_computation.4 | async-start | bytes 524288 | tf_op jit(solution)/shard_map/all_to_all | solution.py:40
  235.2 20.2 %all-to-all-start.4 = ((bf16[8,64,512]{2,1,0:T(8,128)(2,1)}), bf16[8,64,512]{2,1,0:T(8,128)(2,1)S(1)}, u32[]{:S(2)}, u32[]{:S(2)}) async-start(bf16[8,64,512]{2,1,0:T(8,128)(2,1)} %convolution_convert_fusion.3), calls=%async_computation.5 | async-start | bytes 1048576 | tf_op jit(solution)/shard_map/all_to_all | solution.py:62
  256.3 16.7 %copy-start.1 = (bf16[64,512]{1,0:T(8,128)(2,1)}, bf16[64,512]{1,0:T(8,128)(2,1)S(1)}, u32[]{:S(2)}) copy-start(bf16[64,512]{1,0:T(8,128)(2,1)S(1)} %get-tuple-element.6) | copy-start | bytes 196612
Sparse Core Ops, SparseCore 0:
  63.6 51.5 all-gather.2
  130.4 54.1 reduce-scatter.1

commit v12 on v11

--- a/solution.py
+++ b/solution.py
@@ -21,7 +21,14 @@
 
 def final_norm(stream, final_gain):
     stream_f = stream.astype(jnp.float32)
-    square_total = lax.psum(jnp.sum(stream_f * stream_f, axis=1), "tensor")
+    square_total = jnp.sum(stream_f * stream_f, axis=1)
+    count = lax.axis_size("tensor")
+    step = 1
+    while step < count:
+        square_total = square_total + lax.ppermute(
+            square_total, "tensor", [(i, i ^ step) for i in range(count)]
+        )
+        step *= 2
     factor = lax.rsqrt(square_total / D + EPS)
     return (stream_f * factor[:, None] * final_gain).astype(jnp.bfloat16)
 

time: 280 us -> 278 us (level)
  blocking collectives: 90.5 us -> 74.5 us
  starting transfers between devices: 25.7 us -> 34.4 us
  waiting for transfers between devices: 111 us -> 115 us
    psum x1 -> x0, blocking collectives: 16 us -> none  [final_norm(): square_total = lax.psum(jnp.sum(stream_f * stream_f, axis=1), 'tensor')]
    ppermute x0 -> x3, starting transfers between devices: none -> 8.67 us  [final_norm(): lax.ppermute(square_total, 'tensor', [(i, i ^ step) for i in range(count)])]
    ppermute x0 -> x3, waiting for transfers between devices: none -> 3.61 us  [final_norm(): lax.ppermute(square_total, 'tensor', [(i, i ^ step) for i in range(count)])]
  transfers between devices with their start and end apart: 6 -> 9, of which waited for: 6 -> 9; matrix products, arithmetic and copies ran while one was open for 3% -> 4% of each run, Pallas kernels for 0% -> 0%
where the time goes in v12:
time: 278 us; the launch traced here: 276 us
  waiting for transfers between devices  115 us (41%)
  blocking collectives  74.5 us (27%)
  starting transfers between devices  34.4 us (12%)
  matrix products  20.1 us (7%)
  between operations  14.4 us (5%)
  local copies, waits for them, and re-layouts  11.1 us (4%)
  other arithmetic  6.87 us (2%)
    reduce_scatter x1, waiting for transfers between devices, finish_slots(): lax.psum_scatter(partial_out.astype(jnp.bfloat16), 'tensor', scatter_dime...  50.5 us
    all_to_all x1, blocking collectives, on_device(): lax.all_to_all(outgoing, EXPERT, split_axis=0, concat_axis=0, tiled=True)  35.4 us
    all_to_all x1, waiting for transfers between devices, finish_slots(): lax.all_to_all(summed, EXPERT, split_axis=0, concat_axis=0, tiled=True)  24 us
    psum x1, blocking collectives, on_device(): slot_square = lax.psum(jnp.sum(part_f * part_f, axis=2), 'tensor')  23.4 us
    all_gather x1, blocking collectives, on_device(): gain_full = lax.all_gather(norm_gain, 'tensor', axis=0, tiled=True)[:, None]  15.8 us
    all_to_all x1, waiting for transfers between devices, restore(): lax.all_to_all(send, 'ez', split_axis=0, concat_axis=0, tiled=True)  13.9 us
    all_gather x1, waiting for transfers between devices, on_device(): arrived = lax.all_gather(arrived_part, 'tensor', axis=2, tiled=True)  10.7 us
    all_to_all x1, starting transfers between devices, finish_slots(): lax.all_to_all(summed, EXPERT, split_axis=0, concat_axis=0, tiled=True)  9.54 us
  transfers between devices with their start and end apart: 9, of which 9 were waited for; matrix products, arithmetic and copies ran while one was open for 4% of the time, Pallas kernels for 0%

profile of v12, /device:TPU:1, one launch (start us, length us, event | category | flops | bytes accessed | tf_op | source)
XLA Modules:
  0.0 276.2 jit_solution(14804064407952191715)
XLA Ops:
  7.2 3.2 %convolution_convert_fusion.1 = bf16[64,4096]{1,0:T(8,128)(2,1)S(1)} fusion(bf16[64,512]{1,0:T(8,128)(2,1)} %param.12, bf16[512,4096]{1,0:T(8,128)(2,1)} %param.14), kind=kOutput, calls=%fused_computation.6 | convolution fusion | flops 268697600 | bytes 4784128 | tf_op jit(solution)/shard_map/dot_general | solution.py:101
  10.4 0.8 copy.95
  11.3 6.7 %all-to-all-start = ((bf16[8,64,512]{2,1,0:T(8,128)(2,1)}), bf16[8,64,512]{2,1,0:T(8,128)(2,1)S(1)}, u32[]{:S(2)}, u32[]{:S(2)}) async-start(bf16[8,64,512]{2,1,0:T(8,128)(2,1)} %bitcast.84), calls=%async_computation | async-start | bytes 1048576 | tf_op jit(solution)/shard_map/all_to_all | solution.py:105
  18.1 0.2 convert_reduce_fusion.4
  18.4 1.2 select_reduce_fusion.1
  19.6 0.4 fusion.25
  20.2 0.6 gather_fusion.2
  20.8 6.5 %all-to-all-done = bf16[8,64,512]{2,1,0:T(8,128)(2,1)S(1)} async-done(((bf16[8,64,512]{2,1,0:T(8,128)(2,1)}), bf16[8,64,512]{2,1,0:T(8,128)(2,1)S(1)}, u32[]{:S(2)}, u32[]{:S(2)}) %all-to-all-start) | async-done | bytes 524320 | tf_op jit(solution)/shard_map/all_to_all | solution.py:105
  27.6 0.5 convolution_convert_fusion.2
  28.1 35.4 %all_to_all.25 = bf16[32,32,512]{2,1,0:T(8,128)(2,1)} all-to-all(bf16[32,32,512]{2,1,0:T(8,128)(2,1)S(1)} %convolution_convert_fusion.2), channel_id=1, replica_groups=mesh['ex'=4,'ez'=8,'tensor'=8] {'ex','ez'}, dimensions={0} | all-to-all | bytes 2097152 | tf_op jit(solution)/shard_map/all_to_all | solution.py:140
  63.5 15.8 %all-gather = f32[8,1,512]{2,1,0:T(1,128)S(1)} all-gather(f32[1,1,512]{2,1,0:T(1,128)S(1)} %bitcast.92), channel_id=1, replica_groups=mesh['ex'=4,'ez'=8,'tensor'=8] {'tensor'}, dimensions={0}, use_global_device_ids=true | all-gather | bytes 18432 | tf_op jit(solution)/shard_map/all_gather | solution.py:145
  79.3 0.2 fusion.36
  79.5 1.5 multiply_reduce_fusion
  81.0 23.4 %all-reduce = (f32[32,32]{1,0:T(8,128)S(1)}, f32[64,8]{0,1:T(8,128)S(1)}, f32[64]{0:T(128)S(1)}) all-reduce(f32[32,32]{1,0:T(8,128)S(1)} %multiply_reduce_fusion, f32[64,8]{0,1:T(8,128)S(1)} %fusion.36, f32[64]{0:T(128)S(1)} %get-tuple-element.15), channel_id=1, replica_groups=mesh['ex'=4,'ez'=8,'tensor'=8] {'tensor'}, use_global_device_ids=true, to_apply=%region_13.14 | all-reduce | flops 1600 | bytes 12800 | tf_op jit(solution)/shard_map/psum | solution.py:143
  104.4 10.7 %all-gather.3.cloned.1.call-done = bf16[32,32,4096]{2,1,0:T(8,128)(2,1)} async-done(((bf16[32,32,512]{2,1,0:T(8,128)(2,1)}), bf16[32,32,4096]{2,1,0:T(8,128)(2,1)}) %all-gather.3.cloned.1.call-update) | async-done | bytes 8388624 | tf_op jit(solution)/shard_map/all_gather | solution.py:141
  115.1 6.6 %fusion.19 = f32[32,32,256]{2,1,0:T(8,128)S(1)} fusion(bf16[32,32,4096]{2,1,0:T(8,128)(2,1)} %all-gather.3.cloned.1.call-done, bf16[1,4096,256]{2,1,0:T(8,128)(2,1)} %param.18, f32[4096]{0:T(1024)S(1)} %bitcast.90, f32[32,32]{1,0:T(8,128)S(1)} %add_rsqrt_fusion), kind=kOutput, calls=%fused_computation.24 | convolution fusion | flops 2150891520 | bytes 11554816 | tf_op jit(solution)/shard_map/gmd,df->gmf/dot_general | solution.py:148
  121.7 0.4 copy-done.9
  122.1 2.5 fusion.22
  124.6 5.6 %convolution_convert_fusion = bf16[32,32,4096]{2,1,0:T(8,128)(2,1)} fusion(bf16[32,32,256]{2,1,0:T(8,128)(2,1)S(1)} %fusion.22, bf16[1,256,4096]{2,1,0:T(8,128)(2,1)S(1)} %copy-done), kind=kOutput, calls=%fused_computation.5 | convolution fusion | flops 2151677952 | bytes 11010048 | tf_op jit(solution)/shard_map/gmf,fd->gmd/dot_general | solution.py:15
  130.7 0.1 reshape.469
  131.0 0.6 gather_fusion.1
  132.3 1.7 gather_fusion
  134.0 50.5 %reduce-scatter.2.cloned.1.call-done = bf16[32,32,512]{2,1,0:T(8,128)(2,1)} async-done(((bf16[32,32,4096]{2,1,0:T(8,128)(2,1)}), bf16[32,32,512]{2,1,0:T(8,128)(2,1)}) %reduce-scatter.2.cloned.1.call-update) | async-done | bytes 1048592 | tf_op jit(solution)/shard_map/reduce_scatter | solution.py:16
  184.6 9.5 %all-to-all-start.2 = ((bf16[32,32,512]{2,1,0:T(8,128)(2,1)}), bf16[32,32,512]{2,1,0:T(8,128)(2,1)S(1)}, u32[]{:S(2)}, u32[]{:S(2)}) async-start(bf16[32,32,512]{2,1,0:T(8,128)(2,1)} %reduce-scatter.2.cloned.1.call-done), calls=%async_computation.3 | async-start | bytes 2097152 | tf_op jit(solution)/shard_map/all_to_all | solution.py:19
  194.1 0.2 convert_reduce_fusion.3
  194.3 0.2 select_reduce_fusion
  194.7 0.2 fusion.42
  195.3 24.0 %all-to-all-done.2 = bf16[32,32,512]{2,1,0:T(8,128)(2,1)S(1)} async-done(((bf16[32,32,512]{2,1,0:T(8,128)(2,1)}), bf16[32,32,512]{2,1,0:T(8,128)(2,1)S(1)}, u32[]{:S(2)}, u32[]{:S(2)}) %all-to-all-start.2) | async-done | bytes 1048608 | tf_op jit(solution)/shard_map/all_to_all | solution.py:19
  219.3 2.6 gather_fusion.3
  221.9 1.2 gather.26
  223.1 0.9 convert_reduce_fusion
  224.0 0.4 multiply_reduce_fusion.1
  224.4 0.7 broadcast_in_dim.59
  225.2 3.4 %all-to-all-start.3 = ((bf16[4,64,512]{2,1,0:T(8,128)(2,1)}), bf16[4,64,512]{2,1,0:T(8,128)(2,1)S(1)}, u32[]{:S(2)}, u32[]{:S(2)}) async-start(bf16[4,64,512]{2,1,0:T(8,128)(2,1)} %broadcast_in_dim.59), calls=%async_computation.4 | async-start | bytes 524288 | tf_op jit(solution)/shard_map/all_to_all | solution.py:47
  228.6 5.5 %all-to-all-done.3 = bf16[4,64,512]{2,1,0:T(8,128)(2,1)S(1)} async-done(((bf16[4,64,512]{2,1,0:T(8,128)(2,1)}), bf16[4,64,512]{2,1,0:T(8,128)(2,1)S(1)}, u32[]{:S(2)}, u32[]{:S(2)}) %all-to-all-start.3) | async-done | bytes 262176 | tf_op jit(solution)/shard_map/all_to_all | solution.py:47
  234.1 1.1 convolution_convert_fusion.3
  235.2 6.0 %all-to-all-start.4 = ((bf16[8,64,512]{2,1,0:T(8,128)(2,1)}), bf16[8,64,512]{2,1,0:T(8,128)(2,1)S(1)}, u32[]{:S(2)}, u32[]{:S(2)}) async-start(bf16[8,64,512]{2,1,0:T(8,128)(2,1)} %convolution_convert_fusion.3), calls=%async_computation.5 | async-start | bytes 1048576 | tf_op jit(solution)/shard_map/all_to_all | solution.py:69
  241.2 0.3 convert_reduce_fusion.2
  241.5 13.9 %all-to-all-done.4 = bf16[8,64,512]{2,1,0:T(8,128)(2,1)S(1)} async-done(((bf16[8,64,512]{2,1,0:T(8,128)(2,1)}), bf16[8,64,512]{2,1,0:T(8,128)(2,1)S(1)}, u32[]{:S(2)}, u32[]{:S(2)}) %all-to-all-start.4) | async-done | bytes 524320 | tf_op jit(solution)/shard_map/all_to_all | solution.py:69
  255.4 0.7 gather_fusion.4
  256.1 0.2 fusion.33
  256.3 4.3 %collective-permute-start = (f32[64]{0:T(128)S(1)}, f32[64]{0:T(128)S(1)}, u32[]{:S(2)}, u32[]{:S(2)}) collective-permute-start(f32[64]{0:T(128)S(1)} %get-tuple-element.5), channel_id=1, source_target_pairs={{0,1},{1,0},{2,3},{3,2},{4,5},{5,4},{6,7},{7,6},{8,9},{9,8},{10,11... | collective-permute-start | bytes 776 | tf_op jit(solution)/shard_map/ppermute | solution.py:28
  260.6 0.8 collective-permute-done
  261.4 2.3 collective-permute-start.1
  263.7 1.0 collective-permute-done.1
  264.7 2.1 collective-permute-start.2
  266.8 1.8 collective-permute-done.2
  268.6 0.7 fusion.35
  (78 shorter events, 2.4 us)
Async XLA Ops:
  7.2 117.5 %copy-start = (bf16[1,256,4096]{2,1,0:T(8,128)(2,1)S(1)}, bf16[1,256,4096]{2,1,0:T(8,128)(2,1)}, u32[]{:S(2)}) copy-start(bf16[1,256,4096]{2,1,0:T(8,128)(2,1)} %param.20) | copy-start | bytes 6291460
  7.2 10.8 %copy-start.6 = (s32[64,2]{0,1:T(2,128)S(1)}, s32[64,2]{0,1:T(2,128)}, u32[]{:S(2)}) copy-start(s32[64,2]{0,1:T(2,128)} %param.17) | copy-start | bytes 1540
  7.2 13.0 %copy-start.10 = (s32[32]{0:T(128)S(1)}, s32[32]{0:T(128)}, u32[]{:S(2)}) copy-start(s32[32]{0:T(128)} %param.21) | copy-start | bytes 388
  7.2 20.2 %copy-start.2 = (bf16[64,512]{1,0:T(8,128)(2,1)S(1)}, bf16[64,512]{1,0:T(8,128)(2,1)}, u32[]{:S(2)}) copy-start(bf16[64,512]{1,0:T(8,128)(2,1)} %param.13) | copy-start | bytes 196612
  11.3 52.2 %copy-start.5 = (f32[512]{0:T(512)S(1)}, f32[512]{0:T(512)}, u32[]{:S(2)}) copy-start(f32[512]{0:T(512)} %param.15) | copy-start | bytes 6148
  11.3 68.0 %copy-start.4 = (f32[512,8]{0,1:T(8,128)S(1)}, f32[512,8]{0,1:T(8,128)}, u32[]{:S(2)}) copy-start(f32[512,8]{0,1:T(8,128)} %param.16) | copy-start | bytes 49156
  11.3 16.1 %all-to-all-start = ((bf16[8,64,512]{2,1,0:T(8,128)(2,1)}), bf16[8,64,512]{2,1,0:T(8,128)(2,1)S(1)}, u32[]{:S(2)}, u32[]{:S(2)}) async-start(bf16[8,64,512]{2,1,0:T(8,128)(2,1)} %bitcast.84), calls=%async_computation | async-start | bytes 1048576 | tf_op jit(solution)/shard_map/all_to_all | solution.py:105
  18.0 97.1 %all-gather.3.cloned.1.call-start = ((), (), s32[]{:S(2)}) async-start(), calls=%async_computation.6 | async-start | bytes 9437184 | tf_op jit(solution)/shard_map/all_gather | solution.py:141
  63.5 121.1 %reduce-scatter.2.cloned.1.call-start = ((), (), s32[]{:S(2)}) async-start(), calls=%async_computation.7 | async-start | bytes 9437184 | tf_op jit(solution)/shard_map/reduce_scatter | solution.py:16
  115.1 6.6 %copy-start.8 = (bf16[32,32,4096]{2,1,0:T(8,128)(2,1)S(1)}, bf16[32,32,4096]{2,1,0:T(8,128)(2,1)}, u32[]{:S(2)}) copy-start(bf16[32,32,4096]{2,1,0:T(8,128)(2,1)} %all-gather.3.cloned.1.call-done) | copy-start | bytes 25165828
  115.1 7.0 %copy-start.9 = (bf16[1,4096,256]{2,1,0:T(8,128)(2,1)S(1)}, bf16[1,4096,256]{2,1,0:T(8,128)(2,1)}, u32[]{:S(2)}) copy-start(bf16[1,4096,256]{2,1,0:T(8,128)(2,1)} %param.19) | copy-start | bytes 6291460
  130.2 2.0 copy-start.3
  184.6 34.7 %all-to-all-start.2 = ((bf16[32,32,512]{2,1,0:T(8,128)(2,1)}), bf16[32,32,512]{2,1,0:T(8,128)(2,1)S(1)}, u32[]{:S(2)}, u32[]{:S(2)}) async-start(bf16[32,32,512]{2,1,0:T(8,128)(2,1)} %reduce-scatter.2.cloned.1.call-done), calls=%async_computation.3 | async-start | bytes 2097152 | tf_op jit(solution)/shard_map/all_to_all | solution.py:19
  221.9 46.7 %copy-start.7 = (f32[512]{0:T(512)S(1)}, f32[512]{0:T(512)}, u32[]{:S(2)}) copy-start(f32[512]{0:T(512)} %param.22) | copy-start | bytes 6148
  225.2 8.9 %all-to-all-start.3 = ((bf16[4,64,512]{2,1,0:T(8,128)(2,1)}), bf16[4,64,512]{2,1,0:T(8,128)(2,1)S(1)}, u32[]{:S(2)}, u32[]{:S(2)}) async-start(bf16[4,64,512]{2,1,0:T(8,128)(2,1)} %broadcast_in_dim.59), calls=%async_computation.4 | async-start | bytes 524288 | tf_op jit(solution)/shard_map/all_to_all | solution.py:47
  235.2 20.2 %all-to-all-start.4 = ((bf16[8,64,512]{2,1,0:T(8,128)(2,1)}), bf16[8,64,512]{2,1,0:T(8,128)(2,1)S(1)}, u32[]{:S(2)}, u32[]{:S(2)}) async-start(bf16[8,64,512]{2,1,0:T(8,128)(2,1)} %convolution_convert_fusion.3), calls=%async_computation.5 | async-start | bytes 1048576 | tf_op jit(solution)/shard_map/all_to_all | solution.py:69
  256.3 13.0 %copy-start.1 = (bf16[64,512]{1,0:T(8,128)(2,1)}, bf16[64,512]{1,0:T(8,128)(2,1)S(1)}, u32[]{:S(2)}) copy-start(bf16[64,512]{1,0:T(8,128)(2,1)S(1)} %get-tuple-element.6) | copy-start | bytes 196612
  256.3 5.1 %collective-permute-start = (f32[64]{0:T(128)S(1)}, f32[64]{0:T(128)S(1)}, u32[]{:S(2)}, u32[]{:S(2)}) collective-permute-start(f32[64]{0:T(128)S(1)} %get-tuple-element.5), channel_id=1, source_target_pairs={{0,1},{1,0},{2,3},{3,2},{4,5},{5,4},{6,7},{7,6},{8,9},{9,8},{10,11... | collective-permute-start | bytes 776 | tf_op jit(solution)/shard_map/ppermute | solution.py:28
  261.4 3.3 %collective-permute-start.1 = (f32[64]{0:T(128)S(1)}, f32[64]{0:T(128)S(1)}, u32[]{:S(2)}, u32[]{:S(2)}) collective-permute-start(f32[64]{0:T(128)S(1)} %add.349), channel_id=1, source_target_pairs={{0,2},{1,3},{2,0},{3,1},{4,6},{5,7},{6,4},{7,5},{8,10},{9,11},{10,... | collective-permute-start | bytes 776 | tf_op jit(solution)/shard_map/ppermute | solution.py:28
  264.7 3.9 %collective-permute-start.2 = (f32[64]{0:T(128)S(1)}, f32[64]{0:T(128)S(1)}, u32[]{:S(2)}, u32[]{:S(2)}) collective-permute-start(f32[64]{0:T(128)S(1)} %add.350), channel_id=1, source_target_pairs={{0,4},{1,5},{2,6},{3,7},{4,0},{5,1},{6,2},{7,3},{8,12},{9,13},{10,... | collective-permute-start | bytes 776 | tf_op jit(solution)/shard_map/ppermute | solution.py:28
Sparse Core Ops, SparseCore 0:
  63.6 51.5 all-gather.2
  130.4 54.1 reduce-scatter.1
